TPU v7x, 1024 devices: a whole 4x4x32 slice. The times are simulated.
1024 devices in a mesh: ctx: 64 (over z, core), exp: 16 (over x, y).
Axes of the slice: x: 4, y: 4, z: 32, core: 2. Of those that a mesh axis runs over, the one named last changes fastest.
Arguments:
- route_ids: int32 [8192, 8], P('ctx'), may hold values from 0 to 255, all different within a row; in each aligned block of 128 rows (0 to 127, 128 to 255, ...) at most 6 rows name the same one
- route_probs: float32 [8192, 8], P('ctx'), may hold values from 0.02 to 0.4
- moe_grad: bfloat16 [8192, 2304], P('ctx'), may hold values from -6 to 6
- saved_gate: bfloat16 [1024, 64, 6, 256], P(('ctx', 'exp')), may hold values from -6 to 6
- saved_up: bfloat16 [1024, 64, 6, 256], P(('ctx', 'exp')), may hold values from -6 to 6
- w_up: bfloat16 [1024, 2304, 256], P(('ctx', 'exp')), may hold values from -0.125 to 0.125
- w_down: bfloat16 [1024, 256, 2304], P(('ctx', 'exp')), may hold values from -0.1875 to 0.1875
- conv_grad: bfloat16 [8192, 4096], P('ctx', 'exp'), may hold values from -6 to 6
- conv_pre: bfloat16 [8192, 4096], P('ctx', 'exp'), may hold values from -6 to 6
- conv_kernel: float32 [4, 4096], P(None, 'exp'), may hold values from -3 to 3
- w_key: bfloat16 [2304, 4096], P('exp'), may hold values from -0.125 to 0.125
Outputs:
- input_grad: float32 [8192, 2304], P('ctx', 'exp')
- gate_grad: bfloat16 [1024, 64, 6, 256], P(('ctx', 'exp'))
Inputs may be any that keep to these rules, and one draw needn't show every extreme that they name: `route_ids`: each row names 8 different experts. Among the rows of one index of ctx (128 rows in a row) no expert is named more than 6 times, and in every draw some expert is named exactly 6 times by the rows of some index of ctx.
All inputs are finite; a program needn't handle non-finite values.
Results may differ from a plain program's by a relative error of at most 0.0095.
Values may be sent and summed in bfloat16 or wider, within the bound.
No kernel may reach another device: no remote copies, remote signals or barrier semaphores. Data moves between devices by JAX's collectives and lax.ppermute only.
A program may use at most 32 MiB of HBM per device.

v0:
```python
import jax
import jax.numpy as jnp
from jax import lax
from jax.sharding import PartitionSpec as P

SPLIT = 4


def passed_along(value, axis, steps):
    count = lax.axis_size(axis)
    leading, last = (max(0, -steps), min(count, count - steps))
    return lax.ppermute(value, axis, [(source, source + steps) for source in range(leading, last)])


def silu_slope(values):
    logistic = jax.nn.sigmoid(values)
    return logistic * (1.0 + values * (1.0 - logistic))


def contract_last(first_operand, second_operand):
    return lax.dot_general(
        first_operand, second_operand, (((1,), (1,)), ((), ())), preferred_element_type=jnp.float32
    )


def local(
    route_ids,
    route_probs,
    moe_grad,
    saved_gate,
    saved_up,
    w_up,
    w_down,
    conv_grad,
    conv_pre,
    conv_kernel,
    w_key,
):
    ctx_count = lax.axis_size("ctx")
    exp_count = lax.axis_size("exp")
    groups = exp_count // SPLIT
    my_group = lax.axis_index("exp") // SPLIT
    tok_rows, top_count = route_ids.shape
    capacity = saved_gate.shape[2]
    slot_count = ctx_count * capacity
    expert_count = ctx_count * groups
    tap_count = conv_kernel.shape[0]
    grad_pre = conv_grad.astype(jnp.float32) * silu_slope(conv_pre.astype(jnp.float32))
    following = passed_along(grad_pre[: tap_count - 1], "ctx", -1)
    extended = jnp.concatenate([grad_pre, following], 0)
    key_sum = conv_kernel[0][None, :] * extended[0:tok_rows]
    for offset in range(1, tap_count):
        key_sum = key_sum + conv_kernel[offset][None, :] * extended[offset : offset + tok_rows]
    key_grad = key_sum.astype(jnp.bfloat16)
    key_input = contract_last(lax.all_gather(key_grad, "exp", axis=1, tiled=True), w_key)
    flat_ids = route_ids.reshape(-1)
    expert_hot = (flat_ids[:, None] == jnp.arange(expert_count, dtype=jnp.int32)[None, :]).astype(
        jnp.int32
    )
    earlier = jnp.cumsum(expert_hot, 0) - expert_hot
    arrival = jnp.sum(earlier * expert_hot, 1)
    expert_group = flat_ids % groups
    slot_index = flat_ids // groups * capacity + arrival
    own_slot = jnp.where(expert_group == my_group, slot_index, -1).reshape(tok_rows, top_count)
    own_hit = own_slot[:, :, None] == jnp.arange(slot_count, dtype=jnp.int32)[None, None, :]
    placement = jnp.sum(own_hit.astype(jnp.float32), 1).astype(jnp.bfloat16)
    slot_probs = jnp.sum(jnp.where(own_hit, route_probs[:, :, None], 0.0), (0, 1))
    picked = lax.dot_general(
        placement, moe_grad, (((0,), (0,)), ((), ())), preferred_element_type=jnp.float32
    )
    scaled_rows = (slot_probs[:, None] * picked).astype(jnp.bfloat16)
    got_rows = lax.all_to_all(scaled_rows, "ctx", split_axis=0, concat_axis=0, tiled=True)
    gate_pre = saved_gate.reshape(slot_count, -1).astype(jnp.float32)
    up_output = saved_up.reshape(slot_count, -1).astype(jnp.float32)
    hidden_grad = contract_last(got_rows, w_down[0])
    gate_grad = (hidden_grad * up_output * silu_slope(gate_pre)).astype(jnp.bfloat16)
    up_grad = (hidden_grad * jax.nn.silu(gate_pre)).astype(jnp.bfloat16)
    partial_rows = contract_last(up_grad, w_up[0]).astype(jnp.bfloat16)
    came_back = lax.all_to_all(partial_rows, "ctx", split_axis=0, concat_axis=0, tiled=True)
    token_rows = jnp.dot(placement, came_back, preferred_element_type=jnp.float32)
    moe_share = lax.psum_scatter(
        token_rows.astype(jnp.bfloat16), "exp", scatter_dimension=1, tiled=True
    ).astype(jnp.float32)
    input_grad = moe_share + key_input
    return (input_grad, gate_grad.reshape(saved_gate.shape))


def solution(mesh):
    return jax.shard_map(
        local,
        mesh=mesh,
        in_specs=(
            P("ctx", None),
            P("ctx", None),
            P("ctx", None),
            P(("ctx", "exp"), None, None, None),
            P(("ctx", "exp"), None, None, None),
            P(("ctx", "exp"), None, None),
            P(("ctx", "exp"), None, None),
            P("ctx", "exp"),
            P("ctx", "exp"),
            P(None, "exp"),
            P("exp", None),
        ),
        out_specs=(P("ctx", "exp"), P(("ctx", "exp"), None, None, None)),
        check_vma=False,
    )
```

profile of v0, /device:TPU:6, one launch (start us, length us, event | category | flops | bytes accessed | tf_op | source)
XLA Modules:
  0.0 680.4 jit_solution(3838509668010951992)
XLA Ops:
  7.2 0.9 copy.42
  8.3 0.1 copy.48
  8.4 0.2 fusion.6
  8.7 0.3 copy.49
  9.1 0.4 fusion.5
  9.6 0.1 copy.50
  9.7 0.6 convert_reduce_fusion
  10.4 0.6 copy-done.3
  11.0 0.7 fusion
  11.7 1.7 all_to_all.16
  13.4 29.4 %all-to-all-start = ((bf16[64,6,2304]{2,1,0:T(8,128)(2,1)}), bf16[64,6,2304]{2,1,0:T(8,128)(2,1)S(1)}, u32[]{:S(2)}, u32[]{:S(2)}) async-start(bf16[64,6,2304]{2,1,0:T(8,128)(2,1)} %all_to_all.16), calls=%async_computation | async-start | bytes 4718592 | tf_op jit(solution)/shard_map/all_to_all | solution.py:72
  42.8 1.8 copy.51
  44.6 1.9 reshape.73
  46.5 1.8 copy.52
  48.3 1.8 reshape.74
  50.2 215.7 %all-to-all-done = bf16[64,6,2304]{2,1,0:T(8,128)(2,1)S(1)} async-done(((bf16[64,6,2304]{2,1,0:T(8,128)(2,1)}), bf16[64,6,2304]{2,1,0:T(8,128)(2,1)S(1)}, u32[]{:S(2)}, u32[]{:S(2)}) %all-to-all-start) | async-done | bytes 1769504 | tf_op jit(solution)/shard_map/all_to_all | solution.py:72
  265.8 1.5 all_to_all.18
  267.4 3.4 multiply_convert_fusion
  270.8 0.7 convolution_convert_fusion
  271.5 1.7 all_to_all.19
  273.2 4.8 all-to-all-start.1
  278.1 0.9 fusion.23
  279.1 1.3 collective-permute-start
  280.4 1.7 collective-permute-done
  282.1 0.7 fusion.14
  282.9 218.2 %all-to-all-done.1 = bf16[64,6,2304]{2,1,0:T(8,128)(2,1)S(1)} async-done(((bf16[64,6,2304]{2,1,0:T(8,128)(2,1)}), bf16[64,6,2304]{2,1,0:T(8,128)(2,1)S(1)}, u32[]{:S(2)}, u32[]{:S(2)}) %all-to-all-start.1) | async-done | bytes 1769504 | tf_op jit(solution)/shard_map/all_to_all | solution.py:79
  501.2 1.5 all_to_all.21
  502.7 3.3 convolution_convert_fusion.1
  506.1 0.7 copy.53
  506.8 51.4 %all-gather.2.cloned.1.call-done = bf16[128,4096]{1,0:T(8,128)(2,1)} async-done(((bf16[128,256]{1,0:T(8,128)(2,1)}), bf16[128,4096]{1,0:T(8,128)(2,1)}) %all-gather.2.cloned.1.call-update) | async-done | bytes 1048592 | tf_op jit(solution)/shard_map/all_gather | solution.py:55
  558.3 113.0 %reduce-scatter.4.cloned.1.call-done = bf16[128,144]{0,1:T(8,128)(2,1)} async-done(((bf16[128,2304]{0,1:T(8,128)(2,1)}), bf16[128,144]{0,1:T(8,128)(2,1)}) %reduce-scatter.4.cloned.1.call-update) | async-done | bytes 36880
  671.2 2.3 convolution_add_fusion
  (30 shorter events, 0.7 us)
Async XLA Ops:
  7.2 263.7 %copy-start = (bf16[1,2304,256]{2,1,0:T(8,128)(2,1)S(1)}, bf16[1,2304,256]{2,1,0:T(8,128)(2,1)}, u32[]{:S(2)}) copy-start(bf16[1,2304,256]{2,1,0:T(8,128)(2,1)} %param.16) | copy-start | bytes 3538948
  8.7 0.9 copy-start.6
  8.7 2.3 copy-start.4
  10.4 0.6 copy-start.3
  13.4 252.4 %all-to-all-start = ((bf16[64,6,2304]{2,1,0:T(8,128)(2,1)}), bf16[64,6,2304]{2,1,0:T(8,128)(2,1)S(1)}, u32[]{:S(2)}, u32[]{:S(2)}) async-start(bf16[64,6,2304]{2,1,0:T(8,128)(2,1)} %all_to_all.16), calls=%async_computation | async-start | bytes 4718592 | tf_op jit(solution)/shard_map/all_to_all | solution.py:72
  267.4 3.5 copy-start.1
  273.2 7.1 %copy-start.7 = (f32[4,256]{1,0:T(4,128)S(1)}, f32[4,256]{1,0:T(4,128)}, u32[]{:S(2)}) copy-start(f32[4,256]{1,0:T(4,128)} %param.20) | copy-start | bytes 12292
  273.2 227.9 %all-to-all-start.1 = ((bf16[64,6,2304]{2,1,0:T(8,128)(2,1)}), bf16[64,6,2304]{2,1,0:T(8,128)(2,1)S(1)}, u32[]{:S(2)}, u32[]{:S(2)}) async-start(bf16[64,6,2304]{2,1,0:T(8,128)(2,1)} %all_to_all.19), calls=%async_computation.1 | async-start | bytes 4718592 | tf_op jit(solution)/shard_map/all_to_all | solution.py:79
  278.1 280.2 %all-gather.2.cloned.1.call-start = ((), (), s32[]{:S(2)}) async-start(), calls=%async_computation.3 | async-start | bytes 1114112 | tf_op jit(solution)/shard_map/all_gather | solution.py:55
  279.1 3.1 collective-permute-start
  282.9 388.3 %reduce-scatter.4.cloned.1.call-start = ((), (), s32[]{:S(2)}) async-start(), calls=%async_computation.4 | async-start | bytes 626688
  502.7 3.3 copy-start.5
  502.7 168.5 %copy-start.2 = (bf16[144,4096]{1,0:T(8,128)(2,1)S(1)}, bf16[144,4096]{1,0:T(8,128)(2,1)}, u32[]{:S(2)}) copy-start(bf16[144,4096]{1,0:T(8,128)(2,1)} %param.21) | copy-start | bytes 3538948
Sparse Core Ops, SparseCore 0:
  283.7 274.5 all-gather.1
  563.5 107.6 reduce-scatter.3
where the time goes:
time: 681 us; the launch traced here: 680 us
  waiting for transfers between devices  600 us (88%)
  starting transfers between devices  35.6 us (5%)
  local copies, waits for them, and re-layouts  17.1 us (3%)
  between operations  14.2 us (2%)
  matrix products  10.4 us (2%)
    all_to_all x1, waiting for transfers between devices, local(): lax.all_to_all(partial_rows, 'ctx', split_axis=0, concat_axis=0, tiled=True)  218 us
    all_to_all x1, waiting for transfers between devices, local(): lax.all_to_all(scaled_rows, 'ctx', split_axis=0, concat_axis=0, tiled=True)  216 us
    unnamed x3, waiting for transfers between devices  113 us
    all_gather x1, waiting for transfers between devices, local(): lax.all_gather(key_grad, 'exp', axis=1, tiled=True)  51.4 us
    all_to_all x1, starting transfers between devices, local(): lax.all_to_all(scaled_rows, 'ctx', split_axis=0, concat_axis=0, tiled=True)  29.4 us
  transfers between devices with their start and end apart: 5, of which 5 were waited for; matrix products, arithmetic and copies ran while one was open for 2% of the time, Pallas kernels for 0%

commit v1 on v0

--- a/solution.py
+++ b/solution.py
@@ -1,6 +1,7 @@
 import jax
 import jax.numpy as jnp
 from jax import lax
+from jax.sharding import Mesh
 from jax.sharding import PartitionSpec as P
 
 SPLIT = 4
@@ -37,10 +38,12 @@
     w_key,
 ):
     ctx_count = lax.axis_size("ctx")
-    exp_count = lax.axis_size("exp")
-    groups = exp_count // SPLIT
-    my_group = lax.axis_index("exp") // SPLIT
+    groups = lax.axis_size("g")
+    split = lax.axis_size("q")
+    my_group = lax.axis_index("g")
+    my_quarter = lax.axis_index("q")
     tok_rows, top_count = route_ids.shape
+    features = moe_grad.shape[1]
     capacity = saved_gate.shape[2]
     slot_count = ctx_count * capacity
     expert_count = ctx_count * groups
@@ -52,7 +55,7 @@
     for offset in range(1, tap_count):
         key_sum = key_sum + conv_kernel[offset][None, :] * extended[offset : offset + tok_rows]
     key_grad = key_sum.astype(jnp.bfloat16)
-    key_input = contract_last(lax.all_gather(key_grad, "exp", axis=1, tiled=True), w_key)
+    key_input = contract_last(lax.all_gather(key_grad, ("g", "q"), axis=1, tiled=True), w_key)
     flat_ids = route_ids.reshape(-1)
     expert_hot = (flat_ids[:, None] == jnp.arange(expert_count, dtype=jnp.int32)[None, :]).astype(
         jnp.int32
@@ -65,43 +68,55 @@
     own_hit = own_slot[:, :, None] == jnp.arange(slot_count, dtype=jnp.int32)[None, None, :]
     placement = jnp.sum(own_hit.astype(jnp.float32), 1).astype(jnp.bfloat16)
     slot_probs = jnp.sum(jnp.where(own_hit, route_probs[:, :, None], 0.0), (0, 1))
+    chunk = features // split
+    grad_chunk = lax.dynamic_slice_in_dim(moe_grad, my_quarter * chunk, chunk, axis=1)
     picked = lax.dot_general(
-        placement, moe_grad, (((0,), (0,)), ((), ())), preferred_element_type=jnp.float32
+        placement, grad_chunk, (((0,), (0,)), ((), ())), preferred_element_type=jnp.float32
     )
     scaled_rows = (slot_probs[:, None] * picked).astype(jnp.bfloat16)
     got_rows = lax.all_to_all(scaled_rows, "ctx", split_axis=0, concat_axis=0, tiled=True)
+    got_rows = lax.all_gather(got_rows, "q", axis=1, tiled=True)
     gate_pre = saved_gate.reshape(slot_count, -1).astype(jnp.float32)
     up_output = saved_up.reshape(slot_count, -1).astype(jnp.float32)
     hidden_grad = contract_last(got_rows, w_down[0])
     gate_grad = (hidden_grad * up_output * silu_slope(gate_pre)).astype(jnp.bfloat16)
     up_grad = (hidden_grad * jax.nn.silu(gate_pre)).astype(jnp.bfloat16)
-    partial_rows = contract_last(up_grad, w_up[0]).astype(jnp.bfloat16)
-    came_back = lax.all_to_all(partial_rows, "ctx", split_axis=0, concat_axis=0, tiled=True)
+    block = features // (groups * split)
+    up_blocks = w_up[0].reshape(groups, split, block, -1)
+    partial_rows = jnp.einsum(
+        "sh,gqfh->qsgf", up_grad, up_blocks, preferred_element_type=jnp.float32
+    ).astype(jnp.bfloat16)
+    partial_rows = partial_rows.reshape(split * slot_count, groups * block)
+    summed_rows = lax.psum_scatter(partial_rows, "q", scatter_dimension=0, tiled=True)
+    came_back = lax.all_to_all(summed_rows, "ctx", split_axis=0, concat_axis=0, tiled=True)
     token_rows = jnp.dot(placement, came_back, preferred_element_type=jnp.float32)
-    moe_share = lax.psum_scatter(
-        token_rows.astype(jnp.bfloat16), "exp", scatter_dimension=1, tiled=True
-    ).astype(jnp.float32)
+    moe_share = lax.psum_scatter(token_rows, "g", scatter_dimension=1, tiled=True)
     input_grad = moe_share + key_input
     return (input_grad, gate_grad.reshape(saved_gate.shape))
 
 
 def solution(mesh):
+    ctx_count, exp_count = mesh.devices.shape
+    split_mesh = Mesh(
+        mesh.devices.reshape(ctx_count, exp_count // SPLIT, SPLIT), ("ctx", "g", "q")
+    )
+    exp = ("g", "q")
     return jax.shard_map(
         local,
-        mesh=mesh,
+        mesh=split_mesh,
         in_specs=(
             P("ctx", None),
             P("ctx", None),
             P("ctx", None),
-            P(("ctx", "exp"), None, None, None),
-            P(("ctx", "exp"), None, None, None),
-            P(("ctx", "exp"), None, None),
-            P(("ctx", "exp"), None, None),
-            P("ctx", "exp"),
-            P("ctx", "exp"),
-            P(None, "exp"),
-            P("exp", None),
+            P(("ctx", *exp), None, None, None),
+            P(("ctx", *exp), None, None, None),
+            P(("ctx", *exp), None, None),
+            P(("ctx", *exp), None, None),
+            P("ctx", exp),
+            P("ctx", exp),
+            P(None, exp),
+            P(exp, None),
         ),
-        out_specs=(P("ctx", "exp"), P(("ctx", "exp"), None, None, None)),
+        out_specs=(P("ctx", exp), P(("ctx", *exp), None, None, None)),
         check_vma=False,
     )

time: 681 us -> 380 us (0.56)
  waiting for transfers between devices: 600 us -> 203 us
  blocking collectives: 0 us -> 106 us
  starting transfers between devices: 35.6 us -> 25 us
    all_to_all x2 -> x1, waiting for transfers between devices: 434 us -> 73 us  [local(): lax.all_to_all(summed_rows, 'ctx', split_axis=0, concat_axis=0, tiled=True)]
    unnamed x3 -> x4, waiting for transfers between devices: 113 us -> 0.07 us
    all_to_all x0 -> x1, blocking collectives: none -> 106 us  [local(): lax.all_to_all(scaled_rows, 'ctx', split_axis=0, concat_axis=0, tiled=True)]
    reduce_scatter x0 -> x2, waiting for transfers between devices: none -> 46.8 us  [the longest x1 46.8 us: local(): lax.psum_scatter(partial_rows, 'q', scatter_dimension=0, tiled=True)]
    all_gather x1 -> x2, waiting for transfers between devices: 51.4 us -> 81.2 us  [the longest x1 54.4 us: local(): lax.all_gather(key_grad, ('g', 'q'), axis=1, tiled=True)]
    all_to_all x2 -> x1, starting transfers between devices: 34.2 us -> 23.5 us  [local(): lax.all_to_all(summed_rows, 'ctx', split_axis=0, concat_axis=0, tiled=True)]
    unnamed x19 -> x23, local copies, waits for them, and re-layouts: 2.36 us -> 11.9 us
  transfers between devices with their start and end apart: 5 -> 6, of which waited for: 5 -> 5; matrix products, arithmetic and copies ran while one was open for 2% -> 1% of each run, Pallas kernels for 0% -> 0%
where the time goes in v1:
time: 380 us
  waiting for transfers between devices  203 us (53%)
  blocking collectives  106 us (28%)
  starting transfers between devices  25 us (7%)
  local copies, waits for them, and re-layouts  18.2 us (5%)
  between operations  15.5 us (4%)
  matrix products  9.83 us (3%)
    all_to_all x1, blocking collectives, local(): lax.all_to_all(scaled_rows, 'ctx', split_axis=0, concat_axis=0, tiled=True)  106 us
    all_to_all x1, waiting for transfers between devices, local(): lax.all_to_all(summed_rows, 'ctx', split_axis=0, concat_axis=0, tiled=True)  73 us
    all_gather x1, waiting for transfers between devices, local(): lax.all_gather(key_grad, ('g', 'q'), axis=1, tiled=True)  54.4 us
    reduce_scatter x1, waiting for transfers between devices, local(): lax.psum_scatter(partial_rows, 'q', scatter_dimension=0, tiled=True)  46.8 us
    all_gather x1, waiting for transfers between devices, local(): got_rows = lax.all_gather(got_rows, 'q', axis=1, tiled=True)  26.7 us
    all_to_all x1, starting transfers between devices, local(): lax.all_to_all(summed_rows, 'ctx', split_axis=0, concat_axis=0, tiled=True)  23.5 us
    unnamed x23, local copies, waits for them, and re-layouts  11.9 us
  transfers between devices with their start and end apart: 6, of which 5 were waited for; matrix products, arithmetic and copies ran while one was open for 1% of the time, Pallas kernels for 0%

profile of v1, /device:TPU:6, one launch (start us, length us, event | category | flops | bytes accessed | tf_op | source)
XLA Modules:
  0.0 379.5 jit_solution(7626585860399786939)
XLA Ops:
  8.1 0.9 copy.49
  9.1 0.1 copy.55
  9.2 0.2 fusion.5
  9.6 0.3 copy.56
  9.9 0.4 fusion.4
  10.6 0.6 convert_reduce_fusion
  11.2 1.4 fusion
  12.7 0.3 copy.58
  13.0 0.2 all_to_all.16
  13.2 106.1 %all_to_all.24 = bf16[64,6,576]{2,1,0:T(8,128)(2,1)S(1)} all-to-all(bf16[64,6,576]{2,1,0:T(8,128)(2,1)S(1)} %all_to_all.16), channel_id=1, replica_groups=mesh['ctx'=64,'g'=4,'q'=4] {'ctx'}, dimensions={0} | all-to-all | bytes 884736 | tf_op jit(solution)/shard_map/all_to_all | solution.py:77
  119.3 0.3 all_to_all.18
  119.6 1.0 copy.59
  120.7 0.1 copy.60
  120.9 0.1 copy.63
  121.1 26.7 %all-gather.3.cloned.1.call-done = bf16[384,2304]{0,1:T(8,128)(2,1)} async-done(((bf16[384,576]{0,1:T(8,128)(2,1)}), bf16[384,2304]{0,1:T(8,128)(2,1)}) %all-gather.3.cloned.1.call-update) | async-done | bytes 1769488 | tf_op jit(solution)/shard_map/all_gather | solution.py:78
  147.8 3.2 multiply_convert_fusion
  151.0 0.9 convert_bitcast_fusion
  151.9 3.8 copy.68
  155.7 6.4 %reshape.80 = bf16[1536,576]{1,0:T(8,128)(2,1)} reshape(bf16[4,384,4,144]{3,2,1,0:T(4,128)(2,1)} %copy.68) | data formatting | bytes 3538944
  162.1 46.8 %reduce-scatter.7.cloned.1.call-done = bf16[384,576]{1,0:T(8,128)(2,1)} async-done(((bf16[1536,576]{1,0:T(8,128)(2,1)}), bf16[384,576]{1,0:T(8,128)(2,1)}) %reduce-scatter.7.cloned.1.call-update) | async-done | bytes 442384 | tf_op jit(solution)/shard_map/reduce_scatter | solution.py:90
  208.9 2.2 all_to_all.19
  211.0 23.5 %all-to-all-start.1 = ((bf16[64,6,576]{2,1,0:T(8,128)(2,1)}), bf16[64,6,576]{2,1,0:T(8,128)(2,1)S(1)}, u32[]{:S(2)}, u32[]{:S(2)}) async-start(bf16[64,6,576]{2,1,0:T(8,128)(2,1)} %all_to_all.19), calls=%async_computation.1 | async-start | bytes 1310720 | tf_op jit(solution)/shard_map/all_to_all | solution.py:91
  234.7 1.3 collective-permute-start
  236.1 1.7 collective-permute-done
  237.8 0.7 fusion.14
  238.6 73.0 %all-to-all-done.1 = bf16[64,6,576]{2,1,0:T(8,128)(2,1)S(1)} async-done(((bf16[64,6,576]{2,1,0:T(8,128)(2,1)}), bf16[64,6,576]{2,1,0:T(8,128)(2,1)S(1)}, u32[]{:S(2)}, u32[]{:S(2)}) %all-to-all-start.1) | async-done | bytes 442400 | tf_op jit(solution)/shard_map/all_to_all | solution.py:91
  311.6 0.3 all_to_all.21
  311.9 2.0 fusion.37
  313.9 1.0 reshape.76
  314.9 0.7 copy.64
  315.6 54.4 %all-gather.5.cloned.1.call-done = bf16[128,4096]{1,0:T(8,128)(2,1)} async-done(((bf16[128,256]{1,0:T(8,128)(2,1)}), bf16[128,4096]{1,0:T(8,128)(2,1)}) %all-gather.5.cloned.1.call-update) | async-done | bytes 1048592 | tf_op jit(solution)/shard_map/all_gather | solution.py:58
  370.0 2.3 convolution_add_fusion
  (41 shorter events, 1.0 us)
Async XLA Ops:
  8.0 143.0 %copy-start = (bf16[1,2304,256]{2,1,0:T(8,128)(2,1)S(1)}, bf16[1,2304,256]{2,1,0:T(8,128)(2,1)}, u32[]{:S(2)}) copy-start(bf16[1,2304,256]{2,1,0:T(8,128)(2,1)} %param.16) | copy-start | bytes 3538948
  8.0 139.8 %all-gather.3.cloned.1.call-start = ((), (), s32[]{:S(2)}) async-start(), calls=%async_computation.4 | async-start | bytes 2211840 | tf_op jit(solution)/shard_map/all_gather | solution.py:78
  9.6 0.8 copy-start.7
  11.2 1.5 copy-start.2
  119.3 1.4 copy-start.3
  119.6 1.3 copy-start.4
  120.6 88.3 %reduce-scatter.7.cloned.1.call-start = ((), (), s32[]{:S(2)}) async-start(), calls=%async_computation.7 | async-start | bytes 2457600 | tf_op jit(solution)/shard_map/reduce_scatter | solution.py:90
  162.1 72.6 %copy-start.5 = (bf16[128,256]{1,0:T(8,128)(2,1)S(1)}, bf16[128,256]{1,0:T(8,128)(2,1)}, u32[]{:S(2)}) copy-start(bf16[128,256]{1,0:T(8,128)(2,1)} %param.19) | copy-start | bytes 196612
  162.1 72.6 %copy-start.6 = (bf16[128,256]{1,0:T(8,128)(2,1)S(1)}, bf16[128,256]{1,0:T(8,128)(2,1)}, u32[]{:S(2)}) copy-start(bf16[128,256]{1,0:T(8,128)(2,1)} %param.18) | copy-start | bytes 196612
  162.1 74.0 %copy-start.8 = (f32[4,256]{1,0:T(4,128)S(1)}, f32[4,256]{1,0:T(4,128)}, u32[]{:S(2)}) copy-start(f32[4,256]{1,0:T(4,128)} %param.20) | copy-start | bytes 12292
  211.0 100.5 %all-to-all-start.1 = ((bf16[64,6,576]{2,1,0:T(8,128)(2,1)}), bf16[64,6,576]{2,1,0:T(8,128)(2,1)S(1)}, u32[]{:S(2)}, u32[]{:S(2)}) async-start(bf16[64,6,576]{2,1,0:T(8,128)(2,1)} %all_to_all.19), calls=%async_computation.1 | async-start | bytes 1310720 | tf_op jit(solution)/shard_map/all_to_all | solution.py:91
  234.6 135.4 %all-gather.5.cloned.1.call-start = ((), (), s32[]{:S(2)}) async-start(), calls=%async_computation.6 | async-start | bytes 1114112 | tf_op jit(solution)/shard_map/all_gather | solution.py:58
  234.7 3.1 collective-permute-start
  238.5 131.5 %copy-start.1 = (bf16[144,4096]{1,0:T(8,128)(2,1)S(1)}, bf16[144,4096]{1,0:T(8,128)(2,1)}, u32[]{:S(2)}) copy-start(bf16[144,4096]{1,0:T(8,128)(2,1)} %param.21) | copy-start | bytes 3538948
  238.5 131.5 %reduce-scatter.5.cloned.1.call-start = ((), (), s32[]{:S(2)}) async-start(), calls=%async_computation.5 | async-start | bytes 368640 | tf_op jit(solution)/shard_map/reduce_scatter | solution.py:93
Sparse Core Ops, SparseCore 0:
  120.7 27.0 all-gather.2
  162.2 46.6 reduce-scatter.6
  314.0 20.4 reduce-scatter.4
Sparse Core Ops, SparseCore 1:
  239.8 130.2 all-gather.4

commit v2 on v1

--- a/solution.py
+++ b/solution.py
@@ -5,12 +5,22 @@
 from jax.sharding import PartitionSpec as P
 
 SPLIT = 4
+CORES = 2
+CTX = ("z", "k")
 
 
 def passed_along(value, axis, steps):
     count = lax.axis_size(axis)
     leading, last = (max(0, -steps), min(count, count - steps))
     return lax.ppermute(value, axis, [(source, source + steps) for source in range(leading, last)])
+
+
+def across_ctx(rows):
+    chips, cores = lax.axis_size("z"), lax.axis_size("k")
+    blocks = rows.reshape(chips, cores, -1, rows.shape[-1])
+    blocks = lax.all_to_all(blocks, "k", split_axis=1, concat_axis=1, tiled=True)
+    blocks = lax.all_to_all(blocks, "z", split_axis=0, concat_axis=0, tiled=True)
+    return blocks.reshape(rows.shape)
 
 
 def silu_slope(values):
@@ -37,7 +47,7 @@
     conv_kernel,
     w_key,
 ):
-    ctx_count = lax.axis_size("ctx")
+    ctx_count = lax.axis_size(CTX)
     groups = lax.axis_size("g")
     split = lax.axis_size("q")
     my_group = lax.axis_index("g")
@@ -49,7 +59,7 @@
     expert_count = ctx_count * groups
     tap_count = conv_kernel.shape[0]
     grad_pre = conv_grad.astype(jnp.float32) * silu_slope(conv_pre.astype(jnp.float32))
-    following = passed_along(grad_pre[: tap_count - 1], "ctx", -1)
+    following = passed_along(grad_pre[: tap_count - 1], CTX, -1)
     extended = jnp.concatenate([grad_pre, following], 0)
     key_sum = conv_kernel[0][None, :] * extended[0:tok_rows]
     for offset in range(1, tap_count):
@@ -74,7 +84,7 @@
         placement, grad_chunk, (((0,), (0,)), ((), ())), preferred_element_type=jnp.float32
     )
     scaled_rows = (slot_probs[:, None] * picked).astype(jnp.bfloat16)
-    got_rows = lax.all_to_all(scaled_rows, "ctx", split_axis=0, concat_axis=0, tiled=True)
+    got_rows = across_ctx(scaled_rows)
     got_rows = lax.all_gather(got_rows, "q", axis=1, tiled=True)
     gate_pre = saved_gate.reshape(slot_count, -1).astype(jnp.float32)
     up_output = saved_up.reshape(slot_count, -1).astype(jnp.float32)
@@ -88,7 +98,7 @@
     ).astype(jnp.bfloat16)
     partial_rows = partial_rows.reshape(split * slot_count, groups * block)
     summed_rows = lax.psum_scatter(partial_rows, "q", scatter_dimension=0, tiled=True)
-    came_back = lax.all_to_all(summed_rows, "ctx", split_axis=0, concat_axis=0, tiled=True)
+    came_back = across_ctx(summed_rows)
     token_rows = jnp.dot(placement, came_back, preferred_element_type=jnp.float32)
     moe_share = lax.psum_scatter(token_rows, "g", scatter_dimension=1, tiled=True)
     input_grad = moe_share + key_input
@@ -98,25 +108,26 @@
 def solution(mesh):
     ctx_count, exp_count = mesh.devices.shape
     split_mesh = Mesh(
-        mesh.devices.reshape(ctx_count, exp_count // SPLIT, SPLIT), ("ctx", "g", "q")
+        mesh.devices.reshape(ctx_count // CORES, CORES, exp_count // SPLIT, SPLIT),
+        (*CTX, "g", "q"),
     )
     exp = ("g", "q")
     return jax.shard_map(
         local,
         mesh=split_mesh,
         in_specs=(
-            P("ctx", None),
-            P("ctx", None),
-            P("ctx", None),
-            P(("ctx", *exp), None, None, None),
-            P(("ctx", *exp), None, None, None),
-            P(("ctx", *exp), None, None),
-            P(("ctx", *exp), None, None),
-            P("ctx", exp),
-            P("ctx", exp),
+            P(CTX, None),
+            P(CTX, None),
+            P(CTX, None),
+            P((*CTX, *exp), None, None, None),
+            P((*CTX, *exp), None, None, None),
+            P((*CTX, *exp), None, None),
+            P((*CTX, *exp), None, None),
+            P(CTX, exp),
+            P(CTX, exp),
             P(None, exp),
             P(exp, None),
         ),
-        out_specs=(P("ctx", exp), P(("ctx", *exp), None, None, None)),
+        out_specs=(P(CTX, exp), P((*CTX, *exp), None, None, None)),
         check_vma=False,
     )

time: 380 us -> 360 us (0.947)
  waiting for transfers between devices: 203 us -> 188 us
  blocking collectives: 106 us -> 99.2 us
    all_to_all x1, waiting for transfers between devices: 73 us -> 58.4 us  [across_ctx(): lax.all_to_all(blocks, 'z', split_axis=0, concat_axis=0, tiled=True)]
    all_to_all x1 -> x3, blocking collectives: 106 us -> 99.2 us  [the longest x1 90.9 us: across_ctx(): lax.all_to_all(blocks, 'z', split_axis=0, concat_axis=0, tiled=True)]
where the time goes in v2:
time: 360 us; the launch traced here: 359 us
  waiting for transfers between devices  188 us (52%)
  blocking collectives  99.2 us (28%)
  starting transfers between devices  24.4 us (7%)
  local copies, waits for them, and re-layouts  19.5 us (5%)
  between operations  15.5 us (4%)
  matrix products  9.88 us (3%)
    all_to_all x1, blocking collectives, across_ctx(): lax.all_to_all(blocks, 'z', split_axis=0, concat_axis=0, tiled=True)  90.9 us
    all_to_all x1, waiting for transfers between devices, across_ctx(): lax.all_to_all(blocks, 'z', split_axis=0, concat_axis=0, tiled=True)  58.4 us
    all_gather x1, waiting for transfers between devices, local(): lax.all_gather(key_grad, ('g', 'q'), axis=1, tiled=True)  54.1 us
    reduce_scatter x1, waiting for transfers between devices, local(): lax.psum_scatter(partial_rows, 'q', scatter_dimension=0, tiled=True)  46.8 us
    all_gather x1, waiting for transfers between devices, local(): got_rows = lax.all_gather(got_rows, 'q', axis=1, tiled=True)  27.1 us
    all_to_all x1, starting transfers between devices, across_ctx(): lax.all_to_all(blocks, 'z', split_axis=0, concat_axis=0, tiled=True)  22.9 us
    unnamed x23, local copies, waits for them, and re-layouts  11.9 us
    all_to_all x2, blocking collectives, across_ctx(): lax.all_to_all(blocks, 'k', split_axis=1, concat_axis=1, tiled=True)  8.35 us
  transfers between devices with their start and end apart: 6, of which 5 were waited for; matrix products, arithmetic and copies ran while one was open for 1% of the time, Pallas kernels for 0%

profile of v2, /device:TPU:6, one launch (start us, length us, event | category | flops | bytes accessed | tf_op | source)
XLA Modules:
  0.0 358.9 jit_solution(4094035454459881601)
XLA Ops:
  8.1 0.9 copy.55
  9.2 0.2 fusion.5
  9.6 0.3 copy.62
  9.9 0.4 fusion.4
  10.6 0.6 convert_reduce_fusion
  11.2 1.4 fusion
  12.7 0.3 copy.64
  13.2 4.1 %all_to_all.20 = bf16[32,2,6,576]{3,0,2,1:T(8,128)(2,1)S(1)} all-to-all(bf16[32,2,6,576]{3,0,2,1:T(8,128)(2,1)S(1)} %copy.65), channel_id=1, replica_groups=mesh['z'=32,'k'=2,'g'=4,'q'=4] {'k'}, dimensions={1} | all-to-all | bytes 884736 | tf_op jit(solution)/shard_map/all_to_all | solution.py:21
  17.4 0.5 copy.66
  17.9 90.9 %all_to_all.21 = bf16[32,2,6,576]{3,1,2,0:T(2,128)(2,1)S(1)} all-to-all(bf16[32,2,6,576]{3,1,2,0:T(2,128)(2,1)S(1)} %copy.66), channel_id=1, replica_groups=mesh['z'=32,'k'=2,'g'=4,'q'=4] {'z'}, dimensions={0} | all-to-all | bytes 884736 | tf_op jit(solution)/shard_map/all_to_all | solution.py:22
  108.9 0.3 reshape.84
  109.2 1.0 copy.68
  110.6 27.1 %all-gather.3.cloned.1.call-done = bf16[384,2304]{0,1:T(8,128)(2,1)} async-done(((bf16[384,576]{0,1:T(8,128)(2,1)}), bf16[384,2304]{0,1:T(8,128)(2,1)}) %all-gather.3.cloned.1.call-update) | async-done | bytes 1769488 | tf_op jit(solution)/shard_map/all_gather | solution.py:88
  137.8 3.2 multiply_convert_fusion
  141.0 0.9 convert_bitcast_fusion
  141.9 3.8 %copy.80 = bf16[4,384,4,144]{3,2,1,0:T(4,128)(2,1)} copy(bf16[4,384,4,144]{1,3,0,2:T(8,128)(2,1)S(1)} %convert_bitcast_fusion) | data formatting | bytes 3538944
  145.6 6.4 %reshape.92 = bf16[1536,576]{1,0:T(8,128)(2,1)} reshape(bf16[4,384,4,144]{3,2,1,0:T(4,128)(2,1)} %copy.80) | data formatting | bytes 3538944
  152.0 46.8 %reduce-scatter.7.cloned.1.call-done = bf16[384,576]{1,0:T(8,128)(2,1)} async-done(((bf16[1536,576]{1,0:T(8,128)(2,1)}), bf16[384,576]{1,0:T(8,128)(2,1)}) %reduce-scatter.7.cloned.1.call-update) | async-done | bytes 442384 | tf_op jit(solution)/shard_map/reduce_scatter | solution.py:100
  198.8 1.3 reshape.86
  200.3 4.2 %all_to_all.22 = bf16[32,2,6,576]{3,0,2,1:T(8,128)(2,1)S(1)} all-to-all(bf16[32,2,6,576]{3,0,2,1:T(8,128)(2,1)S(1)} %copy.72), channel_id=1, replica_groups=mesh['z'=32,'k'=2,'g'=4,'q'=4] {'k'}, dimensions={1} | all-to-all | bytes 884736 | tf_op jit(solution)/shard_map/all_to_all | solution.py:21
  204.6 1.3 copy.73
  205.9 22.9 %all-to-all-start.3 = ((bf16[32,2,6,576]{3,1,2,0:T(2,128)(2,1)}), bf16[32,2,6,576]{3,1,2,0:T(2,128)(2,1)S(1)}, u32[]{:S(2)}, u32[]{:S(2)}) async-start(bf16[32,2,6,576]{3,1,2,0:T(2,128)(2,1)} %copy.73), calls=%async_computation.3 | async-start | bytes 983040 | tf_op jit(solution)/shard_map/all_to_all | solution.py:22
  229.0 1.3 collective-permute-start
  230.3 1.7 collective-permute-done
  232.0 0.7 fusion.14
  232.8 58.4 %all-to-all-done.3 = bf16[32,2,6,576]{3,1,2,0:T(2,128)(2,1)S(1)} async-done(((bf16[32,2,6,576]{3,1,2,0:T(2,128)(2,1)}), bf16[32,2,6,576]{3,1,2,0:T(2,128)(2,1)S(1)}, u32[]{:S(2)}, u32[]{:S(2)}) %all-to-all-start.3) | async-done | bytes 442400 | tf_op jit(solution)/shard_map/all_to_all | solution.py:22
  291.3 0.3 reshape.87
  291.6 2.0 fusion.37
  293.6 1.0 reshape.88
  294.6 0.7 copy.76
  295.3 54.1 %all-gather.5.cloned.1.call-done = bf16[128,4096]{1,0:T(8,128)(2,1)} async-done(((bf16[128,256]{1,0:T(8,128)(2,1)}), bf16[128,4096]{1,0:T(8,128)(2,1)}) %all-gather.5.cloned.1.call-update) | async-done | bytes 1048592 | tf_op jit(solution)/shard_map/all_gather | solution.py:68
  349.4 2.3 convolution_add_fusion
  (49 shorter events, 1.9 us)
Async XLA Ops:
  8.0 133.0 %copy-start = (bf16[1,2304,256]{2,1,0:T(8,128)(2,1)S(1)}, bf16[1,2304,256]{2,1,0:T(8,128)(2,1)}, u32[]{:S(2)}) copy-start(bf16[1,2304,256]{2,1,0:T(8,128)(2,1)} %param.16) | copy-start | bytes 3538948
  8.0 129.8 %all-gather.3.cloned.1.call-start = ((), (), s32[]{:S(2)}) async-start(), calls=%async_computation.6 | async-start | bytes 2211840 | tf_op jit(solution)/shard_map/all_gather | solution.py:88
  9.6 0.8 copy-start.7
  11.2 1.5 copy-start.2
  108.8 1.5 copy-start.3
  109.2 1.3 copy-start.4
  110.2 88.7 %reduce-scatter.7.cloned.1.call-start = ((), (), s32[]{:S(2)}) async-start(), calls=%async_computation.9 | async-start | bytes 2457600 | tf_op jit(solution)/shard_map/reduce_scatter | solution.py:100
  200.3 28.6 %copy-start.5 = (bf16[128,256]{1,0:T(8,128)(2,1)S(1)}, bf16[128,256]{1,0:T(8,128)(2,1)}, u32[]{:S(2)}) copy-start(bf16[128,256]{1,0:T(8,128)(2,1)} %param.19) | copy-start | bytes 196612
  200.3 28.6 %copy-start.6 = (bf16[128,256]{1,0:T(8,128)(2,1)S(1)}, bf16[128,256]{1,0:T(8,128)(2,1)}, u32[]{:S(2)}) copy-start(bf16[128,256]{1,0:T(8,128)(2,1)} %param.18) | copy-start | bytes 196612
  200.3 29.9 %copy-start.8 = (f32[4,256]{1,0:T(4,128)S(1)}, f32[4,256]{1,0:T(4,128)}, u32[]{:S(2)}) copy-start(f32[4,256]{1,0:T(4,128)} %param.20) | copy-start | bytes 12292
  205.9 85.3 %all-to-all-start.3 = ((bf16[32,2,6,576]{3,1,2,0:T(2,128)(2,1)}), bf16[32,2,6,576]{3,1,2,0:T(2,128)(2,1)S(1)}, u32[]{:S(2)}, u32[]{:S(2)}) async-start(bf16[32,2,6,576]{3,1,2,0:T(2,128)(2,1)} %copy.73), calls=%async_computation.3 | async-start | bytes 983040 | tf_op jit(solution)/shard_map/all_to_all | solution.py:22
  228.8 120.6 %all-gather.5.cloned.1.call-start = ((), (), s32[]{:S(2)}) async-start(), calls=%async_computation.8 | async-start | bytes 1114112 | tf_op jit(solution)/shard_map/all_gather | solution.py:68
  229.0 3.1 collective-permute-start
  232.7 116.7 %reduce-scatter.5.cloned.1.call-start = ((), (), s32[]{:S(2)}) async-start(), calls=%async_computation.7 | async-start | bytes 368640 | tf_op jit(solution)/shard_map/reduce_scatter | solution.py:103
  291.2 58.1 %copy-start.1 = (bf16[144,4096]{1,0:T(8,128)(2,1)S(1)}, bf16[144,4096]{1,0:T(8,128)(2,1)}, u32[]{:S(2)}) copy-start(bf16[144,4096]{1,0:T(8,128)(2,1)} %param.21) | copy-start | bytes 3538948
Sparse Core Ops, SparseCore 0:
  110.3 27.4 all-gather.2
  152.1 46.6 reduce-scatter.6
  293.7 20.0 reduce-scatter.4
Sparse Core Ops, SparseCore 1:
  234.0 115.3 all-gather.4

commit v3 on v2

--- a/solution.py
+++ b/solution.py
@@ -65,7 +65,6 @@
     for offset in range(1, tap_count):
         key_sum = key_sum + conv_kernel[offset][None, :] * extended[offset : offset + tok_rows]
     key_grad = key_sum.astype(jnp.bfloat16)
-    key_input = contract_last(lax.all_gather(key_grad, ("g", "q"), axis=1, tiled=True), w_key)
     flat_ids = route_ids.reshape(-1)
     expert_hot = (flat_ids[:, None] == jnp.arange(expert_count, dtype=jnp.int32)[None, :]).astype(
         jnp.int32
@@ -84,7 +83,11 @@
         placement, grad_chunk, (((0,), (0,)), ((), ())), preferred_element_type=jnp.float32
     )
     scaled_rows = (slot_probs[:, None] * picked).astype(jnp.bfloat16)
+    key_grad, scaled_rows = lax.optimization_barrier((key_grad, scaled_rows))
+    key_all = lax.all_gather(key_grad, ("g", "q"), axis=1, tiled=True)
     got_rows = across_ctx(scaled_rows)
+    key_all, got_rows = lax.optimization_barrier((key_all, got_rows))
+    key_input = contract_last(key_all, w_key)
     got_rows = lax.all_gather(got_rows, "q", axis=1, tiled=True)
     gate_pre = saved_gate.reshape(slot_count, -1).astype(jnp.float32)
     up_output = saved_up.reshape(slot_count, -1).astype(jnp.float32)
@@ -92,12 +95,9 @@
     gate_grad = (hidden_grad * up_output * silu_slope(gate_pre)).astype(jnp.bfloat16)
     up_grad = (hidden_grad * jax.nn.silu(gate_pre)).astype(jnp.bfloat16)
     block = features // (groups * split)
-    up_blocks = w_up[0].reshape(groups, split, block, -1)
-    partial_rows = jnp.einsum(
-        "sh,gqfh->qsgf", up_grad, up_blocks, preferred_element_type=jnp.float32
-    ).astype(jnp.bfloat16)
-    partial_rows = partial_rows.reshape(split * slot_count, groups * block)
-    summed_rows = lax.psum_scatter(partial_rows, "q", scatter_dimension=0, tiled=True)
+    up_blocks = w_up[0].reshape(groups, split, block, -1).transpose(1, 0, 2, 3)
+    partial_rows = contract_last(up_grad, up_blocks.reshape(features, -1)).astype(jnp.bfloat16)
+    summed_rows = lax.psum_scatter(partial_rows, "q", scatter_dimension=1, tiled=True)
     came_back = across_ctx(summed_rows)
     token_rows = jnp.dot(placement, came_back, preferred_element_type=jnp.float32)
     moe_share = lax.psum_scatter(token_rows, "g", scatter_dimension=1, tiled=True)

time: 360 us -> 357 us (level)
  local copies, waits for them, and re-layouts: 19.5 us -> 13.5 us
  starting transfers between devices: 24.4 us -> 30.2 us
  blocking collectives: 99.2 us -> 93.9 us
    all_gather x1, waiting for transfers between devices: 54.1 us -> 22.2 us  [local(): key_all = lax.all_gather(key_grad, ('g', 'q'), axis=1, tiled=True)]
    all_gather x1, waiting for transfers between devices: 27.1 us -> 44.4 us  [local(): got_rows = lax.all_gather(got_rows, 'q', axis=1, tiled=True)]
    reduce_scatter x1, waiting for transfers between devices: 0.01 us -> 17.1 us  [local(): lax.psum_scatter(token_rows, 'g', scatter_dimension=1, tiled=True)]
    unnamed x23 -> x19, local copies, waits for them, and re-layouts: 11.9 us -> 2.96 us
    all_to_all x1, starting transfers between devices: 22.9 us -> 28.7 us  [across_ctx(): lax.all_to_all(blocks, 'z', split_axis=0, concat_axis=0, tiled=True)]
    all_to_all x1, blocking collectives: 90.9 us -> 85.1 us  [across_ctx(): lax.all_to_all(blocks, 'z', split_axis=0, concat_axis=0, tiled=True)]
    dot_general x2 -> x3, matrix products: 5.56 us -> 7.34 us  [contract_last(): lax.dot_general(first_operand, second_operand, (((1,), (1,)), ((), ())),...]
  transfers between devices with their start and end apart: 6 -> 6, of which waited for: 5 -> 5; matrix products, arithmetic and copies ran while one was open for 1% -> 3% of each run, Pallas kernels for 0% -> 0%
where the time goes in v3:
time: 357 us
  waiting for transfers between devices  191 us (54%)
  blocking collectives  93.9 us (26%)
  starting transfers between devices  30.2 us (8%)
  between operations  14 us (4%)
  local copies, waits for them, and re-layouts  13.5 us (4%)
  matrix products  10.7 us (3%)
    all_to_all x1, blocking collectives, across_ctx(): lax.all_to_all(blocks, 'z', split_axis=0, concat_axis=0, tiled=True)  85.1 us
    all_to_all x1, waiting for transfers between devices, across_ctx(): lax.all_to_all(blocks, 'z', split_axis=0, concat_axis=0, tiled=True)  61.6 us
    reduce_scatter x1, waiting for transfers between devices, local(): lax.psum_scatter(partial_rows, 'q', scatter_dimension=1, tiled=True)  45.2 us
    all_gather x1, waiting for transfers between devices, local(): got_rows = lax.all_gather(got_rows, 'q', axis=1, tiled=True)  44.4 us
    all_to_all x1, starting transfers between devices, across_ctx(): lax.all_to_all(blocks, 'z', split_axis=0, concat_axis=0, tiled=True)  28.7 us
    all_gather x1, waiting for transfers between devices, local(): key_all = lax.all_gather(key_grad, ('g', 'q'), axis=1, tiled=True)  22.2 us
    reduce_scatter x1, waiting for transfers between devices, local(): lax.psum_scatter(token_rows, 'g', scatter_dimension=1, tiled=True)  17.1 us
    all_to_all x2, blocking collectives, across_ctx(): lax.all_to_all(blocks, 'k', split_axis=1, concat_axis=1, tiled=True)  8.84 us
  transfers between devices with their start and end apart: 6, of which 5 were waited for; matrix products, arithmetic and copies ran while one was open for 3% of the time, Pallas kernels for 0%

profile of v3, /device:TPU:6, one launch (start us, length us, event | category | flops | bytes accessed | tf_op | source)
XLA Modules:
  0.0 356.6 jit_solution(15470221437777099026)
XLA Ops:
  7.2 1.0 fusion.23
  8.2 1.3 collective-permute-start
  9.5 0.8 copy.69
  10.6 0.8 copy.77
  12.1 0.4 fusion.4
  12.6 0.6 convert_reduce_fusion
  13.3 0.6 copy-done.4
  13.9 1.4 fusion
  15.4 0.7 fusion.14
  16.6 4.7 %all_to_all.20 = bf16[32,2,6,576]{3,0,2,1:T(8,128)(2,1)S(1)} all-to-all(bf16[32,2,6,576]{3,0,2,1:T(8,128)(2,1)S(1)} %copy.79), channel_id=1, replica_groups=mesh['z'=32,'k'=2,'g'=4,'q'=4] {'k'}, dimensions={1} | all-to-all | bytes 884736 | tf_op jit(solution)/shard_map/all_to_all | solution.py:21
  21.3 1.3 copy.80
  22.6 28.7 %all-to-all-start.1 = ((bf16[32,2,6,576]{3,1,2,0:T(2,128)(2,1)}), bf16[32,2,6,576]{3,1,2,0:T(2,128)(2,1)S(1)}, u32[]{:S(2)}, u32[]{:S(2)}) async-start(bf16[32,2,6,576]{3,1,2,0:T(2,128)(2,1)} %copy.80), calls=%async_computation.1 | async-start | bytes 983040 | tf_op jit(solution)/shard_map/all_to_all | solution.py:22
  51.4 0.7 all-gather.3.cloned.1.call-update
  52.2 61.6 %all-to-all-done.1 = bf16[32,2,6,576]{3,1,2,0:T(2,128)(2,1)S(1)} async-done(((bf16[32,2,6,576]{3,1,2,0:T(2,128)(2,1)}), bf16[32,2,6,576]{3,1,2,0:T(2,128)(2,1)S(1)}, u32[]{:S(2)}, u32[]{:S(2)}) %all-to-all-start.1) | async-done | bytes 442400 | tf_op jit(solution)/shard_map/all_to_all | solution.py:22
  114.1 22.2 %all-gather.3.cloned.1.call-done = bf16[128,4096]{1,0:T(8,128)(2,1)} async-done(((bf16[128,256]{1,0:T(8,128)(2,1)}), bf16[128,4096]{1,0:T(8,128)(2,1)}) %all-gather.3.cloned.1.call-update) | async-done | bytes 1048592 | tf_op jit(solution)/shard_map/all_gather | solution.py:87
  136.4 1.0 copy.82
  137.6 1.1 copy.89
  138.8 0.8 reshape.90
  139.6 1.1 copy.84
  140.7 44.4 %all-gather.5.cloned.1.call-done = bf16[384,2304]{0,1:T(8,128)(2,1)} async-done(((bf16[384,576]{0,1:T(8,128)(2,1)}), bf16[384,2304]{0,1:T(8,128)(2,1)}) %all-gather.5.cloned.1.call-update) | async-done | bytes 1769488 | tf_op jit(solution)/shard_map/all_gather | solution.py:91
  185.1 2.9 multiply_convert_fusion
  188.0 2.1 convolution_convert_fusion
  190.2 45.2 %reduce-scatter.3.cloned.1.call-done = bf16[384,576]{0,1:T(8,128)(2,1)} async-done(((bf16[384,2304]{0,1:T(8,128)(2,1)}), bf16[384,576]{0,1:T(8,128)(2,1)}) %reduce-scatter.3.cloned.1.call-update) | async-done | bytes 442384 | tf_op jit(solution)/shard_map/reduce_scatter | solution.py:100
  235.3 1.3 copy.85
  236.9 4.1 %all_to_all.21 = bf16[32,2,6,576]{3,0,2,1:T(8,128)(2,1)S(1)} all-to-all(bf16[32,2,6,576]{3,0,2,1:T(8,128)(2,1)S(1)} %copy.86), channel_id=1, replica_groups=mesh['z'=32,'k'=2,'g'=4,'q'=4] {'k'}, dimensions={1} | all-to-all | bytes 884736 | tf_op jit(solution)/shard_map/all_to_all | solution.py:21
  241.0 0.5 copy.87
  241.5 85.1 %all_to_all.22 = bf16[32,2,6,576]{3,1,2,0:T(2,128)(2,1)S(1)} all-to-all(bf16[32,2,6,576]{3,1,2,0:T(2,128)(2,1)S(1)} %copy.87), channel_id=1, replica_groups=mesh['z'=32,'k'=2,'g'=4,'q'=4] {'z'}, dimensions={0} | all-to-all | bytes 884736 | tf_op jit(solution)/shard_map/all_to_all | solution.py:22
  327.0 2.0 fusion.37
  329.0 1.0 reshape.88
  330.0 0.7 copy.90
  330.7 17.1 %reduce-scatter.5.cloned.1.call-done = f32[128,144]{0,1:T(8,128)} async-done(((f32[128,576]{0,1:T(8,128)}), f32[128,144]{0,1:T(8,128)}) %reduce-scatter.5.cloned.1.call-update) | async-done | bytes 73744 | tf_op jit(solution)/shard_map/reduce_scatter | solution.py:103
  347.8 2.3 convolution_add_fusion
  (47 shorter events, 3.1 us)
Async XLA Ops:
  7.2 177.9 %copy-start = (bf16[1,256,2304]{2,1,0:T(8,128)(2,1)S(1)}, bf16[1,256,2304]{2,1,0:T(8,128)(2,1)}, u32[]{:S(2)}) copy-start(bf16[1,256,2304]{2,1,0:T(8,128)(2,1)} %param.17) | copy-start | bytes 3538948
  8.2 7.1 %collective-permute-start = (f32[3,256]{1,0:T(4,128)S(1)}, f32[3,256]{1,0:T(4,128)S(1)}, u32[]{:S(2)}, u32[]{:S(2)}) collective-permute-start(f32[3,256]{1,0:T(4,128)S(1)} %slice.42), channel_id=1, source_target_pairs={{16,0},{32,16},{48,32},{64,48},{80,64},{96,80},{112,96},{128,112},... | collective-permute-start | bytes 9224 | tf_op jit(solution)/shard_map/ppermute | solution.py:15
  12.1 3.2 copy-start.7
  13.3 0.6 copy-start.4
  22.6 91.1 %all-to-all-start.1 = ((bf16[32,2,6,576]{3,1,2,0:T(2,128)(2,1)}), bf16[32,2,6,576]{3,1,2,0:T(2,128)(2,1)S(1)}, u32[]{:S(2)}, u32[]{:S(2)}) async-start(bf16[32,2,6,576]{3,1,2,0:T(2,128)(2,1)} %copy.80), calls=%async_computation.1 | async-start | bytes 983040 | tf_op jit(solution)/shard_map/all_to_all | solution.py:22
  51.4 85.0 %all-gather.3.cloned.1.call-start = ((), (), s32[]{:S(2)}) async-start(), calls=%async_computation.6 | async-start | bytes 1114112 | tf_op jit(solution)/shard_map/all_gather | solution.py:87
  52.1 85.3 %copy-start.6 = (bf16[1,64,6,256]{3,1,2,0:T(8,128)(2,1)S(1)}, bf16[1,64,6,256]{3,1,2,0:T(8,128)(2,1)}, u32[]{:S(2)}) copy-start(bf16[1,64,6,256]{3,1,2,0:T(8,128)(2,1)} %param.14) | copy-start | bytes 589828
  52.1 132.9 %all-gather.5.cloned.1.call-start = ((), (), s32[]{:S(2)}) async-start(), calls=%async_computation.7 | async-start | bytes 2211840 | tf_op jit(solution)/shard_map/all_gather | solution.py:91
  137.3 2.2 copy-start.1
  137.4 97.9 %reduce-scatter.3.cloned.1.call-start = ((), (), s32[]{:S(2)}) async-start(), calls=%async_computation.8 | async-start | bytes 2211840 | tf_op jit(solution)/shard_map/reduce_scatter | solution.py:100
  139.6 45.5 %copy-start.5 = (f32[384,256]{1,0:T(8,128)S(1)}, f32[384,256]{1,0:T(8,128)}, u32[]{:S(2)}) copy-start(f32[384,256]{1,0:T(8,128)} %reshape.90) | copy-start | bytes 1179652
  140.7 47.3 %copy-start.3 = (bf16[4,4,144,256]{3,2,1,0:T(8,128)(2,1)S(1)}, bf16[4,4,144,256]{3,2,1,0:T(8,128)(2,1)}, u32[]{:S(2)}) copy-start(bf16[4,4,144,256]{3,2,1,0:T(8,128)(2,1)} %copy.84) | copy-start | bytes 3538948
  190.1 157.7 %reduce-scatter.5.cloned.1.call-start = ((), (), s32[]{:S(2)}) async-start(), calls=%async_computation.9 | async-start | bytes 368640 | tf_op jit(solution)/shard_map/reduce_scatter | solution.py:103
  326.7 21.1 %copy-start.2 = (bf16[144,4096]{1,0:T(8,128)(2,1)S(1)}, bf16[144,4096]{1,0:T(8,128)(2,1)}, u32[]{:S(2)}) copy-start(bf16[144,4096]{1,0:T(8,128)(2,1)} %param.21) | copy-start | bytes 3538948
Sparse Core Ops, SparseCore 0:
  56.9 79.3 all-gather.2
  139.0 45.9 all-gather.4
  190.2 45.0 reduce-scatter.2
  329.1 18.6 reduce-scatter.4

commit v4 on v3

--- a/solution.py
+++ b/solution.py
@@ -88,16 +88,25 @@
     got_rows = across_ctx(scaled_rows)
     key_all, got_rows = lax.optimization_barrier((key_all, got_rows))
     key_input = contract_last(key_all, w_key)
-    got_rows = lax.all_gather(got_rows, "q", axis=1, tiled=True)
+    got_rows = lax.all_to_all(
+        jnp.broadcast_to(got_rows[None], (split, *got_rows.shape)), "q", 0, 0, tiled=True
+    )
     gate_pre = saved_gate.reshape(slot_count, -1).astype(jnp.float32)
     up_output = saved_up.reshape(slot_count, -1).astype(jnp.float32)
-    hidden_grad = contract_last(got_rows, w_down[0])
+    hidden_grad = jnp.einsum(
+        "qsf,hqf->sh",
+        got_rows,
+        w_down[0].reshape(-1, split, chunk),
+        preferred_element_type=jnp.float32,
+    )
     gate_grad = (hidden_grad * up_output * silu_slope(gate_pre)).astype(jnp.bfloat16)
     up_grad = (hidden_grad * jax.nn.silu(gate_pre)).astype(jnp.bfloat16)
     block = features // (groups * split)
     up_blocks = w_up[0].reshape(groups, split, block, -1).transpose(1, 0, 2, 3)
     partial_rows = contract_last(up_grad, up_blocks.reshape(features, -1)).astype(jnp.bfloat16)
-    summed_rows = lax.psum_scatter(partial_rows, "q", scatter_dimension=1, tiled=True)
+    partial_rows = partial_rows.reshape(slot_count, split, -1)
+    partial_rows = lax.all_to_all(partial_rows, "q", 1, 1, tiled=True)
+    summed_rows = jnp.sum(partial_rows.astype(jnp.float32), 1).astype(jnp.bfloat16)
     came_back = across_ctx(summed_rows)
     token_rows = jnp.dot(placement, came_back, preferred_element_type=jnp.float32)
     moe_share = lax.psum_scatter(token_rows, "g", scatter_dimension=1, tiled=True)

time: 357 us -> 312 us (0.87)
  waiting for transfers between devices: 191 us -> 114 us
  blocking collectives: 93.9 us -> 118 us
  local copies, waits for them, and re-layouts: 13.5 us -> 19.4 us
    reduce_scatter x1 -> x0, waiting for transfers between devices: 45.2 us -> none  [local(): lax.psum_scatter(partial_rows, 'q', scatter_dimension=1, tiled=True)]
    all_gather x1 -> x0, waiting for transfers between devices: 44.4 us -> none  [local(): got_rows = lax.all_gather(got_rows, 'q', axis=1, tiled=True)]
    all_to_all x0 -> x1, blocking collectives: none -> 24.1 us  [local(): partial_rows = lax.all_to_all(partial_rows, 'q', 1, 1, tiled=True)]
    all_to_all x0 -> x1, waiting for transfers between devices: none -> 12.8 us  [local(): lax.all_to_all(jnp.broadcast_to(got_rows[None], (split, *got_rows.shape))...]
    dot_general x3 -> x2, matrix products: 7.34 us -> 2.66 us  [contract_last(): lax.dot_general(first_operand, second_operand, (((1,), (1,)), ((), ())),...]
    all_to_all x0 -> x1, starting transfers between devices: none -> 3.58 us  [local(): lax.all_to_all(jnp.broadcast_to(got_rows[None], (split, *got_rows.shape))...]
  transfers between devices with their start and end apart: 6 -> 5, of which waited for: 5 -> 4; matrix products, arithmetic and copies ran while one was open for 3% -> 5% of each run, Pallas kernels for 0% -> 0%
where the time goes in v4:
time: 312 us; the launch traced here: 311 us
  blocking collectives  118 us (38%)
  waiting for transfers between devices  114 us (37%)
  starting transfers between devices  33.7 us (11%)
  local copies, waits for them, and re-layouts  19.4 us (6%)
  between operations  14.3 us (5%)
  matrix products  7.99 us (3%)
  other arithmetic  3.63 us (1%)
    all_to_all x1, blocking collectives, across_ctx(): lax.all_to_all(blocks, 'z', split_axis=0, concat_axis=0, tiled=True)  85.2 us
    all_to_all x1, waiting for transfers between devices, across_ctx(): lax.all_to_all(blocks, 'z', split_axis=0, concat_axis=0, tiled=True)  61.6 us
    all_to_all x1, starting transfers between devices, across_ctx(): lax.all_to_all(blocks, 'z', split_axis=0, concat_axis=0, tiled=True)  28.7 us
    all_to_all x1, blocking collectives, local(): partial_rows = lax.all_to_all(partial_rows, 'q', 1, 1, tiled=True)  24.1 us
    all_gather x1, waiting for transfers between devices, local(): key_all = lax.all_gather(key_grad, ('g', 'q'), axis=1, tiled=True)  22.2 us
    reduce_scatter x1, waiting for transfers between devices, local(): lax.psum_scatter(token_rows, 'g', scatter_dimension=1, tiled=True)  16.5 us
    all_to_all x1, waiting for transfers between devices, local(): lax.all_to_all(jnp.broadcast_to(got_rows[None], (split, *got_rows.shape))...  12.8 us
    all_to_all x2, blocking collectives, across_ctx(): lax.all_to_all(blocks, 'k', split_axis=1, concat_axis=1, tiled=True)  8.84 us
  transfers between devices with their start and end apart: 5, of which 4 were waited for; matrix products, arithmetic and copies ran while one was open for 5% of the time, Pallas kernels for 0%

profile of v4, /device:TPU:6, one launch (start us, length us, event | category | flops | bytes accessed | tf_op | source)
XLA Modules:
  0.0 311.0 jit_solution(9973389972326736294)
XLA Ops:
  7.2 1.0 fusion.21
  8.2 1.3 collective-permute-start
  9.5 0.8 copy.76
  12.0 0.6 convert_reduce_fusion
  12.6 1.4 fusion
  14.1 0.7 fusion.12
  15.4 4.7 %all_to_all.30 = bf16[32,2,6,576]{3,0,2,1:T(8,128)(2,1)S(1)} all-to-all(bf16[32,2,6,576]{3,0,2,1:T(8,128)(2,1)S(1)} %copy.86), channel_id=1, replica_groups=mesh['z'=32,'k'=2,'g'=4,'q'=4] {'k'}, dimensions={1} | all-to-all | bytes 884736 | tf_op jit(solution)/shard_map/all_to_all | solution.py:21
  20.1 1.3 copy.87
  21.4 28.7 %all-to-all-start.1 = ((bf16[32,2,6,576]{3,1,2,0:T(2,128)(2,1)}), bf16[32,2,6,576]{3,1,2,0:T(2,128)(2,1)S(1)}, u32[]{:S(2)}, u32[]{:S(2)}) async-start(bf16[32,2,6,576]{3,1,2,0:T(2,128)(2,1)} %copy.87), calls=%async_computation.1 | async-start | bytes 983040 | tf_op jit(solution)/shard_map/all_to_all | solution.py:22
  50.2 0.7 all-gather.2.cloned.1.call-update
  50.9 61.6 %all-to-all-done.1 = bf16[32,2,6,576]{3,1,2,0:T(2,128)(2,1)S(1)} async-done(((bf16[32,2,6,576]{3,1,2,0:T(2,128)(2,1)}), bf16[32,2,6,576]{3,1,2,0:T(2,128)(2,1)S(1)}, u32[]{:S(2)}, u32[]{:S(2)}) %all-to-all-start.1) | async-done | bytes 442400 | tf_op jit(solution)/shard_map/all_to_all | solution.py:22
  112.9 22.2 %all-gather.2.cloned.1.call-done = bf16[128,4096]{1,0:T(8,128)(2,1)} async-done(((bf16[128,256]{1,0:T(8,128)(2,1)}), bf16[128,4096]{1,0:T(8,128)(2,1)}) %all-gather.2.cloned.1.call-update) | async-done | bytes 1048592 | tf_op jit(solution)/shard_map/all_gather | solution.py:87
  135.4 1.4 broadcast_in_dim.26
  136.8 3.6 %all-to-all-start.2 = ((bf16[4,384,576]{1,2,0:T(8,128)(2,1)}), bf16[4,384,576]{1,2,0:T(8,128)(2,1)S(1)}, u32[]{:S(2)}, u32[]{:S(2)}) async-start(bf16[4,384,576]{1,2,0:T(8,128)(2,1)} %broadcast_in_dim.26), calls=%async_computation.2 | async-start | bytes 3538944 | tf_op jit(solution)/shard_map/all_to_all | solution.py:91
  140.4 1.1 copy.91
  141.4 0.8 reshape.94
  142.3 2.4 copy.90
  144.6 1.0 copy.98
  145.7 0.8 reshape.95
  146.5 2.4 copy.92
  148.9 12.8 %all-to-all-done.2 = bf16[4,384,576]{1,2,0:T(8,128)(2,1)S(1)} async-done(((bf16[4,384,576]{1,2,0:T(8,128)(2,1)}), bf16[4,384,576]{1,2,0:T(8,128)(2,1)S(1)}, u32[]{:S(2)}, u32[]{:S(2)}) %all-to-all-start.2) | async-done | bytes 1769504 | tf_op jit(solution)/shard_map/all_to_all | solution.py:91
  161.8 2.8 multiply_convert_fusion
  164.6 0.7 convolution_convert_fusion
  165.3 2.3 copy.93
  167.5 24.1 %all_to_all.31 = bf16[384,4,576]{0,2,1:T(8,128)(2,1)S(1)} all-to-all(bf16[384,4,576]{0,2,1:T(8,128)(2,1)} %bitcast.30), channel_id=1, replica_groups=mesh['z'=32,'k'=2,'g'=4,'q'=4] {'q'}, dimensions={1} | all-to-all | bytes 3538944 | tf_op jit(solution)/shard_map/all_to_all | solution.py:108
  192.7 4.1 %all_to_all.32 = bf16[32,2,6,576]{3,0,2,1:T(8,128)(2,1)S(1)} all-to-all(bf16[32,2,6,576]{3,0,2,1:T(8,128)(2,1)S(1)} %copy.95), channel_id=1, replica_groups=mesh['z'=32,'k'=2,'g'=4,'q'=4] {'k'}, dimensions={1} | all-to-all | bytes 884736 | tf_op jit(solution)/shard_map/all_to_all | solution.py:21
  197.3 85.2 %all_to_all.33 = bf16[32,2,6,576]{3,1,2,0:T(2,128)(2,1)S(1)} all-to-all(bf16[32,2,6,576]{3,1,2,0:T(2,128)(2,1)S(1)} %copy.96), channel_id=1, replica_groups=mesh['z'=32,'k'=2,'g'=4,'q'=4] {'z'}, dimensions={0} | all-to-all | bytes 884736 | tf_op jit(solution)/shard_map/all_to_all | solution.py:22
  282.9 1.1 fusion.35
  284.0 1.0 reshape.93
  285.0 0.7 copy.99
  285.7 16.5 %reduce-scatter.2.cloned.1.call-done = f32[128,144]{0,1:T(8,128)} async-done(((f32[128,576]{0,1:T(8,128)}), f32[128,144]{0,1:T(8,128)}) %reduce-scatter.2.cloned.1.call-update) | async-done | bytes 73744 | tf_op jit(solution)/shard_map/reduce_scatter | solution.py:112
  302.2 2.0 convolution_add_fusion
  (50 shorter events, 4.8 us)
Async XLA Ops:
  7.2 295.0 %copy-start = (bf16[144,4096]{1,0:T(8,128)(2,1)S(1)}, bf16[144,4096]{1,0:T(8,128)(2,1)}, u32[]{:S(2)}) copy-start(bf16[144,4096]{1,0:T(8,128)(2,1)} %param.21) | copy-start | bytes 3538948
  8.2 5.9 %collective-permute-start = (f32[3,256]{1,0:T(4,128)S(1)}, f32[3,256]{1,0:T(4,128)S(1)}, u32[]{:S(2)}, u32[]{:S(2)}) collective-permute-start(f32[3,256]{1,0:T(4,128)S(1)} %slice.42), channel_id=1, source_target_pairs={{16,0},{32,16},{48,32},{64,48},{80,64},{96,80},{112,96},{128,112},... | collective-permute-start | bytes 9224 | tf_op jit(solution)/shard_map/ppermute | solution.py:15
  10.9 0.9 copy-start.7
  11.3 2.8 copy-start.8
  12.6 2.2 copy-start.5
  21.4 91.1 %all-to-all-start.1 = ((bf16[32,2,6,576]{3,1,2,0:T(2,128)(2,1)}), bf16[32,2,6,576]{3,1,2,0:T(2,128)(2,1)S(1)}, u32[]{:S(2)}, u32[]{:S(2)}) async-start(bf16[32,2,6,576]{3,1,2,0:T(2,128)(2,1)} %copy.87), calls=%async_computation.1 | async-start | bytes 983040 | tf_op jit(solution)/shard_map/all_to_all | solution.py:22
  50.1 85.0 %all-gather.2.cloned.1.call-start = ((), (), s32[]{:S(2)}) async-start(), calls=%async_computation.7 | async-start | bytes 1114112 | tf_op jit(solution)/shard_map/all_gather | solution.py:87
  136.8 25.0 %all-to-all-start.2 = ((bf16[4,384,576]{1,2,0:T(8,128)(2,1)}), bf16[4,384,576]{1,2,0:T(8,128)(2,1)S(1)}, u32[]{:S(2)}, u32[]{:S(2)}) async-start(bf16[4,384,576]{1,2,0:T(8,128)(2,1)} %broadcast_in_dim.26), calls=%async_computation.2 | async-start | bytes 3538944 | tf_op jit(solution)/shard_map/all_to_all | solution.py:91
  140.3 161.9 %reduce-scatter.2.cloned.1.call-start = ((), (), s32[]{:S(2)}) async-start(), calls=%async_computation.8 | async-start | bytes 368640 | tf_op jit(solution)/shard_map/reduce_scatter | solution.py:112
  146.5 15.2 %copy-start.2 = (f32[384,256]{1,0:T(8,128)S(1)}, f32[384,256]{1,0:T(8,128)}, u32[]{:S(2)}) copy-start(f32[384,256]{1,0:T(8,128)} %reshape.94) | copy-start | bytes 1179652
  161.7 2.8 copy-start.1
  161.8 2.8 copy-start.3
  197.3 85.6 %copy-start.6 = (bf16[128,384]{1,0:T(8,128)(2,1)S(1)}, bf16[128,384]{1,0:T(8,128)(2,1)}, u32[]{:S(2)}) copy-start(bf16[128,384]{1,0:T(8,128)(2,1)} %copy-done.5) | copy-start | bytes 294916
  282.6 19.6 %copy-start.4 = (bf16[128,4096]{1,0:T(8,128)(2,1)S(1)}, bf16[128,4096]{1,0:T(8,128)(2,1)}, u32[]{:S(2)}) copy-start(bf16[128,4096]{1,0:T(8,128)(2,1)} %all-gather.2.cloned.1.call-done) | copy-start | bytes 3145732
Sparse Core Ops, SparseCore 0:
  55.7 79.3 all-gather.1
  284.1 18.0 reduce-scatter.1

commit v5 on v4

--- a/solution.py
+++ b/solution.py
@@ -84,7 +84,8 @@
     )
     scaled_rows = (slot_probs[:, None] * picked).astype(jnp.bfloat16)
     key_grad, scaled_rows = lax.optimization_barrier((key_grad, scaled_rows))
-    key_all = lax.all_gather(key_grad, ("g", "q"), axis=1, tiled=True)
+    key_all = lax.all_gather(key_grad, "q", axis=1, tiled=True)
+    key_all = lax.all_gather(key_all, "g", axis=1, tiled=True)
     got_rows = across_ctx(scaled_rows)
     key_all, got_rows = lax.optimization_barrier((key_all, got_rows))
     key_input = contract_last(key_all, w_key)
@@ -109,7 +110,8 @@
     summed_rows = jnp.sum(partial_rows.astype(jnp.float32), 1).astype(jnp.bfloat16)
     came_back = across_ctx(summed_rows)
     token_rows = jnp.dot(placement, came_back, preferred_element_type=jnp.float32)
-    moe_share = lax.psum_scatter(token_rows, "g", scatter_dimension=1, tiled=True)
+    token_rows = lax.all_to_all(token_rows.reshape(tok_rows, groups, -1), "g", 1, 1, tiled=True)
+    moe_share = jnp.sum(token_rows, 1)
     input_grad = moe_share + key_input
     return (input_grad, gate_grad.reshape(saved_gate.shape))
 

time: 312 us -> 274 us (0.88)
  waiting for transfers between devices: 114 us -> 66.3 us
  starting transfers between devices: 33.7 us -> 40 us
  blocking collectives: 118 us -> 123 us
    all_gather x1, waiting for transfers between devices: 22.2 us -> 0.02 us  [local(): key_all = lax.all_gather(key_all, 'g', axis=1, tiled=True)]
    reduce_scatter x1 -> x0, waiting for transfers between devices: 16.5 us -> none  [local(): lax.psum_scatter(token_rows, 'g', scatter_dimension=1, tiled=True)]
    all_gather x0 -> x1, blocking collectives: none -> 13.5 us  [local(): key_all = lax.all_gather(key_grad, 'q', axis=1, tiled=True)]
    all_to_all x1, waiting for transfers between devices: 61.6 us -> 48.8 us  [across_ctx(): lax.all_to_all(blocks, 'z', split_axis=0, concat_axis=0, tiled=True)]
    all_to_all x1, blocking collectives: 85.2 us -> 76.1 us  [across_ctx(): lax.all_to_all(blocks, 'z', split_axis=0, concat_axis=0, tiled=True)]
    all_to_all x0 -> x1, starting transfers between devices: none -> 5.46 us  [local(): lax.all_to_all(token_rows.reshape(tok_rows, groups, -1), 'g', 1, 1, tiled...]
    all_to_all x0 -> x1, waiting for transfers between devices: none -> 4 us  [local(): lax.all_to_all(token_rows.reshape(tok_rows, groups, -1), 'g', 1, 1, tiled...]
  transfers between devices with their start and end apart: 5 -> 5, of which waited for: 4 -> 3; matrix products, arithmetic and copies ran while one was open for 5% -> 5% of each run, Pallas kernels for 0% -> 0%
where the time goes in v5:
time: 274 us; the launch traced here: 273 us
  blocking collectives  123 us (45%)
  waiting for transfers between devices  66.3 us (24%)
  starting transfers between devices  40 us (15%)
  local copies, waits for them, and re-layouts  19 us (7%)
  between operations  14.3 us (5%)
  matrix products  7.02 us (3%)
  other arithmetic  3.02 us (1%)
    all_to_all x1, blocking collectives, across_ctx(): lax.all_to_all(blocks, 'z', split_axis=0, concat_axis=0, tiled=True)  76.1 us
    all_to_all x1, waiting for transfers between devices, across_ctx(): lax.all_to_all(blocks, 'z', split_axis=0, concat_axis=0, tiled=True)  48.8 us
    all_to_all x1, starting transfers between devices, across_ctx(): lax.all_to_all(blocks, 'z', split_axis=0, concat_axis=0, tiled=True)  28.7 us
    all_to_all x1, blocking collectives, local(): partial_rows = lax.all_to_all(partial_rows, 'q', 1, 1, tiled=True)  24.7 us
    all_gather x1, blocking collectives, local(): key_all = lax.all_gather(key_grad, 'q', axis=1, tiled=True)  13.5 us
    all_to_all x1, waiting for transfers between devices, local(): lax.all_to_all(jnp.broadcast_to(got_rows[None], (split, *got_rows.shape))...  13.5 us
    all_to_all x2, blocking collectives, across_ctx(): lax.all_to_all(blocks, 'k', split_axis=1, concat_axis=1, tiled=True)  8.84 us
  transfers between devices with their start and end apart: 5, of which 3 were waited for; matrix products, arithmetic and copies ran while one was open for 5% of the time, Pallas kernels for 0%

profile of v5, /device:TPU:6, one launch (start us, length us, event | category | flops | bytes accessed | tf_op | source)
XLA Modules:
  0.0 272.8 jit_solution(16070091387626356310)
XLA Ops:
  7.2 1.0 fusion.21
  8.2 1.3 collective-permute-start
  9.5 0.8 copy.79
  12.0 0.6 convert_reduce_fusion
  12.6 1.4 fusion
  14.8 4.7 %all_to_all.35 = bf16[32,2,6,576]{3,0,2,1:T(8,128)(2,1)S(1)} all-to-all(bf16[32,2,6,576]{3,0,2,1:T(8,128)(2,1)S(1)} %copy.89), channel_id=1, replica_groups=mesh['z'=32,'k'=2,'g'=4,'q'=4] {'k'}, dimensions={1} | all-to-all | bytes 884736 | tf_op jit(solution)/shard_map/all_to_all | solution.py:21
  19.5 1.3 copy.90
  20.8 28.7 %all-to-all-start.1 = ((bf16[32,2,6,576]{3,1,2,0:T(2,128)(2,1)}), bf16[32,2,6,576]{3,1,2,0:T(2,128)(2,1)S(1)}, u32[]{:S(2)}, u32[]{:S(2)}) async-start(bf16[32,2,6,576]{3,1,2,0:T(2,128)(2,1)} %copy.90), calls=%async_computation.1 | async-start | bytes 983040 | tf_op jit(solution)/shard_map/all_to_all | solution.py:22
  49.6 13.5 %all_gather.6 = bf16[128,1024]{1,0:T(8,128)(2,1)} all-gather(bf16[128,256]{1,0:T(8,128)(2,1)S(1)} %fusion.12), channel_id=1, replica_groups=mesh['z'=32,'k'=2,'g'=4,'q'=4] {'q'}, dimensions={1}, use_global_device_ids=true | all-gather | bytes 327680 | tf_op jit(solution)/shard_map/all_gather | solution.py:87
  63.1 48.8 %all-to-all-done.1 = bf16[32,2,6,576]{3,1,2,0:T(2,128)(2,1)S(1)} async-done(((bf16[32,2,6,576]{3,1,2,0:T(2,128)(2,1)}), bf16[32,2,6,576]{3,1,2,0:T(2,128)(2,1)S(1)}, u32[]{:S(2)}, u32[]{:S(2)}) %all-to-all-start.1) | async-done | bytes 442400 | tf_op jit(solution)/shard_map/all_to_all | solution.py:22
  112.5 1.4 broadcast_in_dim.26
  113.9 4.5 %all-to-all-start.2 = ((bf16[4,384,576]{1,2,0:T(8,128)(2,1)}), bf16[4,384,576]{1,2,0:T(8,128)(2,1)S(1)}, u32[]{:S(2)}, u32[]{:S(2)}) async-start(bf16[4,384,576]{1,2,0:T(8,128)(2,1)} %broadcast_in_dim.26), calls=%async_computation.2 | async-start | bytes 3538944 | tf_op jit(solution)/shard_map/all_to_all | solution.py:92
  118.4 1.0 copy.94
  119.4 0.8 reshape.96
  120.2 2.4 copy.93
  122.6 1.0 copy.102
  123.7 0.8 reshape.97
  124.5 2.4 copy.95
  126.9 13.5 %all-to-all-done.2 = bf16[4,384,576]{1,2,0:T(8,128)(2,1)S(1)} async-done(((bf16[4,384,576]{1,2,0:T(8,128)(2,1)}), bf16[4,384,576]{1,2,0:T(8,128)(2,1)S(1)}, u32[]{:S(2)}, u32[]{:S(2)}) %all-to-all-start.2) | async-done | bytes 1769504 | tf_op jit(solution)/shard_map/all_to_all | solution.py:92
  140.4 2.8 %multiply_convert_fusion = (bf16[384,256]{1,0:T(8,128)(2,1)}, f32[384,256]{1,0:T(8,128)S(1)}) fusion(f32[384,256]{1,0:T(8,128)S(1)} %copy-done.2, f32[384,256]{1,0:T(8,128)} %reshape.97, bf16[4,384,576]{1,2,0:T(8,128)(2,1)S(1)} %all-to-all-done.2, bf16[256,4,576]{0,2,1:T(8,128)(2,1)} %bitcast.39), kind=kOutput, calls=%fused_computation.17 | convolution fusion | flops 453967872 | bytes 4325376 | tf_op jit(solution)/shard_map/qsf,hqf->sh/dot_general | solution.py:97
  143.3 0.7 convolution_convert_fusion
  143.9 2.3 copy.96
  146.2 24.7 %all_to_all.36 = bf16[384,4,576]{0,2,1:T(8,128)(2,1)S(1)} all-to-all(bf16[384,4,576]{0,2,1:T(8,128)(2,1)} %bitcast.34), channel_id=1, replica_groups=mesh['z'=32,'k'=2,'g'=4,'q'=4] {'q'}, dimensions={1} | all-to-all | bytes 3538944 | tf_op jit(solution)/shard_map/all_to_all | solution.py:109
  170.9 0.5 reduce_sum.54
  172.0 4.1 %all_to_all.37 = bf16[32,2,6,576]{3,0,2,1:T(8,128)(2,1)S(1)} all-to-all(bf16[32,2,6,576]{3,0,2,1:T(8,128)(2,1)S(1)} %copy.98), channel_id=1, replica_groups=mesh['z'=32,'k'=2,'g'=4,'q'=4] {'k'}, dimensions={1} | all-to-all | bytes 884736 | tf_op jit(solution)/shard_map/all_to_all | solution.py:21
  176.1 0.5 copy.99
  176.6 76.1 %all_to_all.38 = bf16[32,2,6,576]{3,1,2,0:T(2,128)(2,1)S(1)} all-to-all(bf16[32,2,6,576]{3,1,2,0:T(2,128)(2,1)S(1)} %copy.99), channel_id=1, replica_groups=mesh['z'=32,'k'=2,'g'=4,'q'=4] {'z'}, dimensions={0} | all-to-all | bytes 884736 | tf_op jit(solution)/shard_map/all_to_all | solution.py:22
  253.5 1.0 fusion.23
  254.5 5.5 %all-to-all-start.6 = ((f32[128,4,144]{0,2,1:T(8,128)}), f32[128,4,144]{0,2,1:T(8,128)S(1)}, u32[]{:S(2)}, u32[]{:S(2)}) async-start(f32[128,4,144]{0,2,1:T(8,128)} %fusion.23), calls=%async_computation.6 | async-start | bytes 589824 | tf_op jit(solution)/shard_map/all_to_all | solution.py:113
  260.1 0.7 copy.103
  260.8 4.0 %all-to-all-done.6 = f32[128,4,144]{0,2,1:T(8,128)S(1)} async-done(((f32[128,4,144]{0,2,1:T(8,128)}), f32[128,4,144]{0,2,1:T(8,128)S(1)}, u32[]{:S(2)}, u32[]{:S(2)}) %all-to-all-start.6) | async-done | bytes 294944 | tf_op jit(solution)/shard_map/all_to_all | solution.py:113
  264.8 1.1 convolution_add_fusion
  (54 shorter events, 4.4 us)
Async XLA Ops:
  7.2 257.6 %copy-start = (bf16[144,4096]{1,0:T(8,128)(2,1)S(1)}, bf16[144,4096]{1,0:T(8,128)(2,1)}, u32[]{:S(2)}) copy-start(bf16[144,4096]{1,0:T(8,128)(2,1)} %param.21) | copy-start | bytes 3538948
  8.2 5.9 %collective-permute-start = (f32[3,256]{1,0:T(4,128)S(1)}, f32[3,256]{1,0:T(4,128)S(1)}, u32[]{:S(2)}, u32[]{:S(2)}) collective-permute-start(f32[3,256]{1,0:T(4,128)S(1)} %slice.42), channel_id=1, source_target_pairs={{16,0},{32,16},{48,32},{64,48},{80,64},{96,80},{112,96},{128,112},... | collective-permute-start | bytes 9224 | tf_op jit(solution)/shard_map/ppermute | solution.py:15
  10.9 0.9 copy-start.8
  11.3 2.8 %copy-start.9 = (f32[4,256]{1,0:T(4,128)S(1)}, f32[4,256]{1,0:T(4,128)}, u32[]{:S(2)}) copy-start(f32[4,256]{1,0:T(4,128)} %param.20) | copy-start | bytes 12292
  12.6 1.6 copy-start.5
  20.8 91.1 %all-to-all-start.1 = ((bf16[32,2,6,576]{3,1,2,0:T(2,128)(2,1)}), bf16[32,2,6,576]{3,1,2,0:T(2,128)(2,1)S(1)}, u32[]{:S(2)}, u32[]{:S(2)}) async-start(bf16[32,2,6,576]{3,1,2,0:T(2,128)(2,1)} %copy.90), calls=%async_computation.1 | async-start | bytes 983040 | tf_op jit(solution)/shard_map/all_to_all | solution.py:22
  49.5 62.8 %all-gather.2.cloned.1.call-start = ((), (), s32[]{:S(2)}) async-start(), calls=%async_computation.7 | async-start | bytes 1310720 | tf_op jit(solution)/shard_map/all_gather | solution.py:88
  113.9 26.5 %all-to-all-start.2 = ((bf16[4,384,576]{1,2,0:T(8,128)(2,1)}), bf16[4,384,576]{1,2,0:T(8,128)(2,1)S(1)}, u32[]{:S(2)}, u32[]{:S(2)}) async-start(bf16[4,384,576]{1,2,0:T(8,128)(2,1)} %broadcast_in_dim.26), calls=%async_computation.2 | async-start | bytes 3538944 | tf_op jit(solution)/shard_map/all_to_all | solution.py:92
  124.5 15.9 %copy-start.2 = (f32[384,256]{1,0:T(8,128)S(1)}, f32[384,256]{1,0:T(8,128)}, u32[]{:S(2)}) copy-start(f32[384,256]{1,0:T(8,128)} %reshape.96) | copy-start | bytes 1179652
  140.4 2.8 %copy-start.1 = (bf16[4,4,144,256]{3,2,1,0:T(8,128)(2,1)S(1)}, bf16[4,4,144,256]{3,2,1,0:T(8,128)(2,1)}, u32[]{:S(2)}) copy-start(bf16[4,4,144,256]{3,2,1,0:T(8,128)(2,1)} %copy.95) | copy-start | bytes 3538948
  140.4 2.8 %copy-start.3 = (f32[384,256]{1,0:T(8,128)S(1)}, f32[384,256]{1,0:T(8,128)}, u32[]{:S(2)}) copy-start(f32[384,256]{1,0:T(8,128)} %reshape.96) | copy-start | bytes 1179652
  252.6 0.9 copy-start.6
  252.7 7.2 %copy-start.7 = (bf16[384,256]{1,0:T(8,128)(2,1)S(1)}, bf16[384,256]{1,0:T(8,128)(2,1)}, u32[]{:S(2)}) copy-start(bf16[384,256]{1,0:T(8,128)(2,1)} %get-tuple-element.26) | copy-start | bytes 589828
  253.3 11.5 %copy-start.4 = (bf16[128,4096]{1,0:T(8,128)(2,1)S(1)}, bf16[128,4096]{1,0:T(8,128)(2,1)}, u32[]{:S(2)}) copy-start(bf16[128,4096]{1,0:T(8,128)(2,1)} %all-gather.2.cloned.1.call-done) | copy-start | bytes 3145732
  254.5 10.2 %all-to-all-start.6 = ((f32[128,4,144]{0,2,1:T(8,128)}), f32[128,4,144]{0,2,1:T(8,128)S(1)}, u32[]{:S(2)}, u32[]{:S(2)}) async-start(f32[128,4,144]{0,2,1:T(8,128)} %fusion.23), calls=%async_computation.6 | async-start | bytes 589824 | tf_op jit(solution)/shard_map/all_to_all | solution.py:113
Sparse Core Ops, SparseCore 0:
  63.2 41.6 all-gather.1

commit v6 on v5

--- a/solution.py
+++ b/solution.py
@@ -13,14 +13,6 @@
     count = lax.axis_size(axis)
     leading, last = (max(0, -steps), min(count, count - steps))
     return lax.ppermute(value, axis, [(source, source + steps) for source in range(leading, last)])
-
-
-def across_ctx(rows):
-    chips, cores = lax.axis_size("z"), lax.axis_size("k")
-    blocks = rows.reshape(chips, cores, -1, rows.shape[-1])
-    blocks = lax.all_to_all(blocks, "k", split_axis=1, concat_axis=1, tiled=True)
-    blocks = lax.all_to_all(blocks, "z", split_axis=0, concat_axis=0, tiled=True)
-    return blocks.reshape(rows.shape)
 
 
 def silu_slope(values):
@@ -86,29 +78,35 @@
     key_grad, scaled_rows = lax.optimization_barrier((key_grad, scaled_rows))
     key_all = lax.all_gather(key_grad, "q", axis=1, tiled=True)
     key_all = lax.all_gather(key_all, "g", axis=1, tiled=True)
-    got_rows = across_ctx(scaled_rows)
+    chips, cores = lax.axis_size("z"), lax.axis_size("k")
+    got_rows = scaled_rows.reshape(chips, cores, capacity, chunk)
+    got_rows = lax.all_to_all(got_rows, "z", 0, 0, tiled=True).transpose(1, 0, 2, 3)
     key_all, got_rows = lax.optimization_barrier((key_all, got_rows))
     key_input = contract_last(key_all, w_key)
-    got_rows = lax.all_to_all(
-        jnp.broadcast_to(got_rows[None], (split, *got_rows.shape)), "q", 0, 0, tiled=True
-    )
+    got_rows = jnp.broadcast_to(got_rows[:, None], (cores, split, chips, capacity, chunk))
+    got_rows = got_rows.reshape(cores * split, chips, capacity, chunk)
+    got_rows = lax.all_to_all(got_rows, ("k", "q"), 0, 0, tiled=True)
+    got_rows = got_rows.reshape(cores, split, chips, capacity, chunk)
     gate_pre = saved_gate.reshape(slot_count, -1).astype(jnp.float32)
     up_output = saved_up.reshape(slot_count, -1).astype(jnp.float32)
     hidden_grad = jnp.einsum(
-        "qsf,hqf->sh",
+        "kqzsf,hqf->zksh",
         got_rows,
         w_down[0].reshape(-1, split, chunk),
         preferred_element_type=jnp.float32,
-    )
+    ).reshape(slot_count, -1)
     gate_grad = (hidden_grad * up_output * silu_slope(gate_pre)).astype(jnp.bfloat16)
     up_grad = (hidden_grad * jax.nn.silu(gate_pre)).astype(jnp.bfloat16)
     block = features // (groups * split)
     up_blocks = w_up[0].reshape(groups, split, block, -1).transpose(1, 0, 2, 3)
     partial_rows = contract_last(up_grad, up_blocks.reshape(features, -1)).astype(jnp.bfloat16)
-    partial_rows = partial_rows.reshape(slot_count, split, -1)
-    partial_rows = lax.all_to_all(partial_rows, "q", 1, 1, tiled=True)
+    partial_rows = partial_rows.reshape(chips, cores, capacity, split, chunk)
+    partial_rows = partial_rows.transpose(1, 3, 0, 2, 4).reshape(cores * split, chips, capacity, chunk)
+    partial_rows = lax.all_to_all(partial_rows, ("k", "q"), 0, 0, tiled=True)
+    partial_rows = partial_rows.reshape(cores, split, chips, capacity, chunk)
     summed_rows = jnp.sum(partial_rows.astype(jnp.float32), 1).astype(jnp.bfloat16)
-    came_back = across_ctx(summed_rows)
+    summed_rows = summed_rows.transpose(1, 0, 2, 3)
+    came_back = lax.all_to_all(summed_rows, "z", 0, 0, tiled=True).reshape(slot_count, chunk)
     token_rows = jnp.dot(placement, came_back, preferred_element_type=jnp.float32)
     token_rows = lax.all_to_all(token_rows.reshape(tok_rows, groups, -1), "g", 1, 1, tiled=True)
     moe_share = jnp.sum(token_rows, 1)

time: 274 us -> 276 us (level)
  blocking collectives: 123 us -> 41.6 us
  waiting for transfers between devices: 66.3 us -> 137 us
  starting transfers between devices: 40 us -> 54.7 us
  local copies, waits for them, and re-layouts: 19 us -> 15.6 us
    all_to_all x4 -> x1, blocking collectives: 110 us -> 28.1 us  [local(): partial_rows = lax.all_to_all(partial_rows, ('k', 'q'), 0, 0, tiled=True)]
    all_gather x1, waiting for transfers between devices: 0.02 us -> 41.6 us  [local(): key_all = lax.all_gather(key_all, 'g', axis=1, tiled=True)]
    all_to_all x2 -> x3, waiting for transfers between devices: 62.3 us -> 91.1 us  [the longest x1 61.7 us: local(): lax.all_to_all(summed_rows, 'z', 0, 0, tiled=True)]
    all_to_all x2 -> x3, starting transfers between devices: 33.2 us -> 48.5 us  [the longest x1 29.4 us: local(): lax.all_to_all(got_rows, 'z', 0, 0, tiled=True).transpose(1, 0, 2, 3)]
    reshape x7 -> x6, local copies, waits for them, and re-layouts: 1.22 us -> 6.64 us  [the longest x2 4.72 us: local(): partial_rows = partial_rows.reshape(chips, cores, capacity, split, chunk)]
    convert_element_type x3 -> x2, local copies, waits for them, and re-layouts: 4.14 us -> 0.19 us  [local(): up_grad = (hidden_grad * jax.nn.silu(gate_pre)).astype(jnp.bfloat16)]
  transfers between devices with their start and end apart: 5 -> 6, of which waited for: 3 -> 5; matrix products, arithmetic and copies ran while one was open for 5% -> 3% of each run, Pallas kernels for 0% -> 0%
where the time goes in v6:
time: 276 us; the launch traced here: 275 us
  waiting for transfers between devices  137 us (50%)
  starting transfers between devices  54.7 us (20%)
  blocking collectives  41.6 us (15%)
  local copies, waits for them, and re-layouts  15.6 us (6%)
  between operations  14.4 us (5%)
  matrix products  8.04 us (3%)
  other arithmetic  3.67 us (1%)
    all_to_all x1, waiting for transfers between devices, local(): lax.all_to_all(summed_rows, 'z', 0, 0, tiled=True)  61.7 us
    all_gather x1, waiting for transfers between devices, local(): key_all = lax.all_gather(key_all, 'g', axis=1, tiled=True)  41.6 us
    all_to_all x1, starting transfers between devices, local(): lax.all_to_all(got_rows, 'z', 0, 0, tiled=True).transpose(1, 0, 2, 3)  29.4 us
    all_to_all x1, blocking collectives, local(): partial_rows = lax.all_to_all(partial_rows, ('k', 'q'), 0, 0, tiled=True)  28.1 us
    all_to_all x1, waiting for transfers between devices, local(): got_rows = lax.all_to_all(got_rows, ('k', 'q'), 0, 0, tiled=True)  21.9 us
    all_to_all x1, starting transfers between devices, local(): lax.all_to_all(summed_rows, 'z', 0, 0, tiled=True)  14.6 us
    all_gather x1, blocking collectives, local(): key_all = lax.all_gather(key_grad, 'q', axis=1, tiled=True)  13.5 us
    all_to_all x1, waiting for transfers between devices, local(): lax.all_to_all(got_rows, 'z', 0, 0, tiled=True).transpose(1, 0, 2, 3)  7.49 us
  transfers between devices with their start and end apart: 6, of which 5 were waited for; matrix products, arithmetic and copies ran while one was open for 3% of the time, Pallas kernels for 0%

profile of v6, /device:TPU:6, one launch (start us, length us, event | category | flops | bytes accessed | tf_op | source)
XLA Modules:
  0.0 274.7 jit_solution(14315908679783932784)
XLA Ops:
  7.2 1.0 fusion.20
  8.2 1.3 collective-permute-start
  9.5 0.8 copy.79
  10.9 0.3 copy.86
  11.3 0.4 fusion.2
  12.0 0.6 convert_reduce_fusion
  12.6 1.4 fusion
  14.6 1.2 copy.89
  15.8 29.4 %all-to-all-start = ((bf16[32,2,6,576]{3,1,2,0:T(2,128)(2,1)}), bf16[32,2,6,576]{3,1,2,0:T(2,128)(2,1)S(1)}, u32[]{:S(2)}, u32[]{:S(2)}) async-start(bf16[32,2,6,576]{3,1,2,0:T(2,128)(2,1)} %copy.89), calls=%async_computation | async-start | bytes 983040 | tf_op jit(solution)/shard_map/all_to_all | solution.py:83
  45.2 13.5 %all_gather.6 = bf16[128,1024]{1,0:T(8,128)(2,1)} all-gather(bf16[128,256]{1,0:T(8,128)(2,1)S(1)} %fusion.11), channel_id=1, replica_groups=mesh['z'=32,'k'=2,'g'=4,'q'=4] {'q'}, dimensions={1}, use_global_device_ids=true | all-gather | bytes 327680 | tf_op jit(solution)/shard_map/all_gather | solution.py:79
  58.8 41.6 %all-gather.2.cloned.1.call-done = bf16[128,4096]{1,0:T(8,128)(2,1)} async-done(((bf16[128,1024]{1,0:T(8,128)(2,1)}), bf16[128,4096]{1,0:T(8,128)(2,1)}) %all-gather.2.cloned.1.call-update) | async-done | bytes 1048592 | tf_op jit(solution)/shard_map/all_gather | solution.py:80
  100.4 7.5 %all-to-all-done = bf16[32,2,6,576]{3,1,2,0:T(2,128)(2,1)S(1)} async-done(((bf16[32,2,6,576]{3,1,2,0:T(2,128)(2,1)}), bf16[32,2,6,576]{3,1,2,0:T(2,128)(2,1)S(1)}, u32[]{:S(2)}, u32[]{:S(2)}) %all-to-all-start) | async-done | bytes 442400 | tf_op jit(solution)/shard_map/all_to_all | solution.py:83
  107.9 1.5 broadcast_in_dim.26
  109.4 4.6 %all-to-all-start.1 = ((bf16[8,32,6,576]{3,1,2,0:T(8,128)(2,1)}), bf16[8,32,6,576]{3,1,2,0:T(8,128)(2,1)}, u32[]{:S(2)}, u32[]{:S(2)}) async-start(bf16[8,32,6,576]{3,1,2,0:T(8,128)(2,1)} %bitcast.9), calls=%async_computation.1 | async-start | bytes 3932160 | tf_op jit(solution)/shard_map/all_to_all | solution.py:88
  114.0 1.4 copy.91
  115.5 1.9 reshape.106
  117.4 21.9 %all-to-all-done.1 = bf16[8,32,6,576]{3,1,2,0:T(8,128)(2,1)} async-done(((bf16[8,32,6,576]{3,1,2,0:T(8,128)(2,1)}), bf16[8,32,6,576]{3,1,2,0:T(8,128)(2,1)}, u32[]{:S(2)}, u32[]{:S(2)}) %all-to-all-start.1) | async-done | bytes 1769504 | tf_op jit(solution)/shard_map/all_to_all | solution.py:88
  139.3 2.6 multiply_convert_fusion.1
  142.1 1.9 convolution_convert_fusion
  144.0 4.3 %reshape.101 = bf16[32,2,6,4,576]{4,3,2,1,0:T(4,128)(2,1)S(1)} reshape(bf16[384,2304]{1,0:T(8,128)(2,1)} %convolution_convert_fusion) | data formatting | bytes 3538944 | tf_op jit(solution)/shard_map/reshape | solution.py:103
  148.3 0.4 copy.97
  148.7 28.1 %all_to_all.25 = bf16[8,32,6,576]{3,1,2,0:T(8,128)(2,1)S(1)} all-to-all(bf16[8,32,6,576]{3,1,2,0:T(8,128)(2,1)S(1)} %bitcast.60), channel_id=1, replica_groups=mesh['z'=32,'k'=2,'g'=4,'q'=4] {'k','q'}, dimensions={0} | all-to-all | bytes 3538944 | tf_op jit(solution)/shard_map/all_to_all | solution.py:105
  176.8 0.3 bitcast_reduce_fusion
  177.1 1.3 copy.98
  178.4 14.6 %all-to-all-start.3 = ((bf16[32,2,6,576]{3,1,2,0:T(2,128)(2,1)}), bf16[32,2,6,576]{3,1,2,0:T(2,128)(2,1)S(1)}, u32[]{:S(2)}, u32[]{:S(2)}) async-start(bf16[32,2,6,576]{3,1,2,0:T(2,128)(2,1)} %copy.98), calls=%async_computation.3 | async-start | bytes 983040 | tf_op jit(solution)/shard_map/all_to_all | solution.py:109
  193.0 0.3 copy.101
  193.6 61.7 %all-to-all-done.3 = bf16[32,2,6,576]{3,1,2,0:T(2,128)(2,1)S(1)} async-done(((bf16[32,2,6,576]{3,1,2,0:T(2,128)(2,1)}), bf16[32,2,6,576]{3,1,2,0:T(2,128)(2,1)S(1)}, u32[]{:S(2)}, u32[]{:S(2)}) %all-to-all-start.3) | async-done | bytes 442400 | tf_op jit(solution)/shard_map/all_to_all | solution.py:109
  256.0 1.0 fusion.22
  257.0 4.9 %all-to-all-start.4 = ((f32[128,4,144]{0,2,1:T(8,128)}), f32[128,4,144]{0,2,1:T(8,128)S(1)}, u32[]{:S(2)}, u32[]{:S(2)}) async-start(f32[128,4,144]{0,2,1:T(8,128)} %fusion.22), calls=%async_computation.4 | async-start | bytes 589824 | tf_op jit(solution)/shard_map/all_to_all | solution.py:111
  261.9 0.8 multiply_convert_fusion
  262.7 3.9 %all-to-all-done.4 = f32[128,4,144]{0,2,1:T(8,128)S(1)} async-done(((f32[128,4,144]{0,2,1:T(8,128)}), f32[128,4,144]{0,2,1:T(8,128)S(1)}, u32[]{:S(2)}, u32[]{:S(2)}) %all-to-all-start.4) | async-done | bytes 294944 | tf_op jit(solution)/shard_map/all_to_all | solution.py:111
  266.7 1.1 convolution_add_fusion
  (48 shorter events, 2.7 us)
Async XLA Ops:
  7.2 259.5 %copy-start = (bf16[144,4096]{1,0:T(8,128)(2,1)S(1)}, bf16[144,4096]{1,0:T(8,128)(2,1)}, u32[]{:S(2)}) copy-start(bf16[144,4096]{1,0:T(8,128)(2,1)} %param.21) | copy-start | bytes 3538948
  8.2 5.9 %collective-permute-start = (f32[3,256]{1,0:T(4,128)S(1)}, f32[3,256]{1,0:T(4,128)S(1)}, u32[]{:S(2)}, u32[]{:S(2)}) collective-permute-start(f32[3,256]{1,0:T(4,128)S(1)} %slice.42), channel_id=1, source_target_pairs={{16,0},{32,16},{48,32},{64,48},{80,64},{96,80},{112,96},{128,112},... | collective-permute-start | bytes 9224 | tf_op jit(solution)/shard_map/ppermute | solution.py:15
  10.9 0.9 copy-start.8
  11.3 2.8 %copy-start.9 = (f32[4,256]{1,0:T(4,128)S(1)}, f32[4,256]{1,0:T(4,128)}, u32[]{:S(2)}) copy-start(f32[4,256]{1,0:T(4,128)} %param.20) | copy-start | bytes 12292
  12.6 1.6 copy-start.4
  15.8 92.1 %all-to-all-start = ((bf16[32,2,6,576]{3,1,2,0:T(2,128)(2,1)}), bf16[32,2,6,576]{3,1,2,0:T(2,128)(2,1)S(1)}, u32[]{:S(2)}, u32[]{:S(2)}) async-start(bf16[32,2,6,576]{3,1,2,0:T(2,128)(2,1)} %copy.89), calls=%async_computation | async-start | bytes 983040 | tf_op jit(solution)/shard_map/all_to_all | solution.py:83
  45.2 55.2 %all-gather.2.cloned.1.call-start = ((), (), s32[]{:S(2)}) async-start(), calls=%async_computation.5 | async-start | bytes 1310720 | tf_op jit(solution)/shard_map/all_gather | solution.py:80
  109.4 4.6 %copy-start.1 = (bf16[1,256,2304]{2,1,0:T(8,128)(2,1)S(1)}, bf16[1,256,2304]{2,1,0:T(8,128)(2,1)}, u32[]{:S(2)}) copy-start(bf16[1,256,2304]{2,1,0:T(8,128)(2,1)} %param.17) | copy-start | bytes 3538948
  109.4 29.9 %all-to-all-start.1 = ((bf16[8,32,6,576]{3,1,2,0:T(8,128)(2,1)}), bf16[8,32,6,576]{3,1,2,0:T(8,128)(2,1)}, u32[]{:S(2)}, u32[]{:S(2)}) async-start(bf16[8,32,6,576]{3,1,2,0:T(8,128)(2,1)} %bitcast.9), calls=%async_computation.1 | async-start | bytes 3932160 | tf_op jit(solution)/shard_map/all_to_all | solution.py:88
  114.0 3.3 %copy-start.2 = (bf16[1,2304,256]{2,1,0:T(8,128)(2,1)S(1)}, bf16[1,2304,256]{2,1,0:T(8,128)(2,1)}, u32[]{:S(2)}) copy-start(bf16[1,2304,256]{2,1,0:T(8,128)(2,1)} %param.16) | copy-start | bytes 3538948
  178.4 76.9 %all-to-all-start.3 = ((bf16[32,2,6,576]{3,1,2,0:T(2,128)(2,1)}), bf16[32,2,6,576]{3,1,2,0:T(2,128)(2,1)S(1)}, u32[]{:S(2)}, u32[]{:S(2)}) async-start(bf16[32,2,6,576]{3,1,2,0:T(2,128)(2,1)} %copy.98), calls=%async_computation.3 | async-start | bytes 983040 | tf_op jit(solution)/shard_map/all_to_all | solution.py:109
  193.6 62.4 %copy-start.5 = (bf16[128,384]{1,0:T(8,128)(2,1)S(1)}, bf16[128,384]{1,0:T(8,128)(2,1)}, u32[]{:S(2)}) copy-start(bf16[128,384]{1,0:T(8,128)(2,1)} %copy-done.4) | copy-start | bytes 294916
  255.7 6.2 %copy-start.6 = (bf16[1,64,6,256]{3,1,2,0:T(8,128)(2,1)S(1)}, bf16[1,64,6,256]{3,1,2,0:T(8,128)(2,1)}, u32[]{:S(2)}) copy-start(bf16[1,64,6,256]{3,1,2,0:T(8,128)(2,1)} %param.14) | copy-start | bytes 589828
  255.7 6.1 %copy-start.7 = (bf16[1,64,6,256]{3,1,2,0:T(8,128)(2,1)S(1)}, bf16[1,64,6,256]{3,1,2,0:T(8,128)(2,1)}, u32[]{:S(2)}) copy-start(bf16[1,64,6,256]{3,1,2,0:T(8,128)(2,1)} %param.15) | copy-start | bytes 589828
  256.0 10.7 %copy-start.3 = (bf16[128,4096]{1,0:T(8,128)(2,1)S(1)}, bf16[128,4096]{1,0:T(8,128)(2,1)}, u32[]{:S(2)}) copy-start(bf16[128,4096]{1,0:T(8,128)(2,1)} %all-gather.2.cloned.1.call-done) | copy-start | bytes 3145732
  257.0 9.7 %all-to-all-start.4 = ((f32[128,4,144]{0,2,1:T(8,128)}), f32[128,4,144]{0,2,1:T(8,128)S(1)}, u32[]{:S(2)}, u32[]{:S(2)}) async-start(f32[128,4,144]{0,2,1:T(8,128)} %fusion.22), calls=%async_computation.4 | async-start | bytes 589824 | tf_op jit(solution)/shard_map/all_to_all | solution.py:111
Sparse Core Ops, SparseCore 0:
  58.9 41.4 all-gather.1

commit v7 on v3

--- a/solution.py
+++ b/solution.py
@@ -21,6 +21,11 @@
     blocks = lax.all_to_all(blocks, "k", split_axis=1, concat_axis=1, tiled=True)
     blocks = lax.all_to_all(blocks, "z", split_axis=0, concat_axis=0, tiled=True)
     return blocks.reshape(rows.shape)
+
+
+def around(value, steps):
+    count = lax.axis_size("q")
+    return lax.ppermute(value, "q", [(source, (source + steps) % count) for source in range(count)])
 
 
 def silu_slope(values):
@@ -84,23 +89,43 @@
     )
     scaled_rows = (slot_probs[:, None] * picked).astype(jnp.bfloat16)
     key_grad, scaled_rows = lax.optimization_barrier((key_grad, scaled_rows))
-    key_all = lax.all_gather(key_grad, ("g", "q"), axis=1, tiled=True)
+    key_all = lax.all_gather(key_grad, "q", axis=1, tiled=True)
+    key_all = lax.all_gather(key_all, "g", axis=1, tiled=True)
+    hidden = w_down.shape[1]
+    block = features // (groups * split)
+    down_own = w_down[0].reshape(hidden, split, chunk)
+    up_own = w_up[0].reshape(groups, split, block, hidden)
+
+    def down_slice(index):
+        return lax.dynamic_index_in_dim(down_own, index, 1, keepdims=False)
+
+    def up_slice(index):
+        return lax.dynamic_index_in_dim(up_own, index, 1, keepdims=False).reshape(chunk, hidden)
+
+    down_got = [down_slice(my_quarter)]
+    up_got = [up_slice(my_quarter)]
+    for shift in range(1, split):
+        down_got.append(around(down_slice((my_quarter + shift) % split), shift))
+        up_got.append(around(up_slice((my_quarter + shift) % split), shift))
     got_rows = across_ctx(scaled_rows)
     key_all, got_rows = lax.optimization_barrier((key_all, got_rows))
     key_input = contract_last(key_all, w_key)
-    got_rows = lax.all_gather(got_rows, "q", axis=1, tiled=True)
     gate_pre = saved_gate.reshape(slot_count, -1).astype(jnp.float32)
     up_output = saved_up.reshape(slot_count, -1).astype(jnp.float32)
-    hidden_grad = contract_last(got_rows, w_down[0])
+    hidden_grad = contract_last(got_rows, down_got[0])
+    for shift in range(1, split):
+        share = contract_last(got_rows, down_got[shift]).astype(jnp.bfloat16)
+        hidden_grad = hidden_grad + around(share, -shift).astype(jnp.float32)
     gate_grad = (hidden_grad * up_output * silu_slope(gate_pre)).astype(jnp.bfloat16)
     up_grad = (hidden_grad * jax.nn.silu(gate_pre)).astype(jnp.bfloat16)
-    block = features // (groups * split)
-    up_blocks = w_up[0].reshape(groups, split, block, -1).transpose(1, 0, 2, 3)
-    partial_rows = contract_last(up_grad, up_blocks.reshape(features, -1)).astype(jnp.bfloat16)
-    summed_rows = lax.psum_scatter(partial_rows, "q", scatter_dimension=1, tiled=True)
+    summed_rows = contract_last(up_grad, up_got[0])
+    for shift in range(1, split):
+        summed_rows = summed_rows + contract_last(around(up_grad, shift), up_got[shift])
+    summed_rows = summed_rows.astype(jnp.bfloat16)
     came_back = across_ctx(summed_rows)
     token_rows = jnp.dot(placement, came_back, preferred_element_type=jnp.float32)
-    moe_share = lax.psum_scatter(token_rows, "g", scatter_dimension=1, tiled=True)
+    token_rows = lax.all_to_all(token_rows.reshape(tok_rows, groups, -1), "g", 1, 1, tiled=True)
+    moe_share = jnp.sum(token_rows, 1)
     input_grad = moe_share + key_input
     return (input_grad, gate_grad.reshape(saved_gate.shape))
 

time: 357 us -> 266 us (0.75)
  waiting for transfers between devices: 191 us -> 46 us
  starting transfers between devices: 30.2 us -> 75.6 us
  blocking collectives: 93.9 us -> 99.2 us
    all_gather x2 -> x1, waiting for transfers between devices: 66.6 us -> 0.02 us  [local(): key_all = lax.all_gather(key_all, 'g', axis=1, tiled=True)]
    reduce_scatter x2 -> x0, waiting for transfers between devices: 62.2 us -> none  [the longest x1 45.2 us: local(): lax.psum_scatter(partial_rows, 'q', scatter_dimension=1, tiled=True)]
    ppermute x0 -> x12, starting transfers between devices: none -> 40.7 us  [around(): lax.ppermute(value, 'q', [(source, (source + steps) % count) for source i...]
    all_to_all x1, waiting for transfers between devices: 61.6 us -> 27.2 us  [across_ctx(): lax.all_to_all(blocks, 'z', split_axis=0, concat_axis=0, tiled=True)]
    ppermute x0 -> x12, waiting for transfers between devices: none -> 14.7 us  [around(): lax.ppermute(value, 'q', [(source, (source + steps) % count) for source i...]
    all_gather x0 -> x1, blocking collectives: none -> 13.5 us  [local(): key_all = lax.all_gather(key_grad, 'q', axis=1, tiled=True)]
    all_to_all x1, blocking collectives: 85.1 us -> 76.8 us  [across_ctx(): lax.all_to_all(blocks, 'z', split_axis=0, concat_axis=0, tiled=True)]
    all_to_all x0 -> x1, starting transfers between devices: none -> 4.83 us  [local(): lax.all_to_all(token_rows.reshape(tok_rows, groups, -1), 'g', 1, 1, tiled...]
  transfers between devices with their start and end apart: 6 -> 16, of which waited for: 5 -> 6; matrix products, arithmetic and copies ran while one was open for 3% -> 7% of each run, Pallas kernels for 0% -> 0%
where the time goes in v7:
time: 266 us; the launch traced here: 263 us
  blocking collectives  99.2 us (37%)
  starting transfers between devices  75.6 us (28%)
  waiting for transfers between devices  46 us (17%)
  between operations  14.7 us (6%)
  local copies, waits for them, and re-layouts  14.4 us (5%)
  matrix products  10 us (4%)
  other arithmetic  2.77 us (1%)
    all_to_all x1, blocking collectives, across_ctx(): lax.all_to_all(blocks, 'z', split_axis=0, concat_axis=0, tiled=True)  76.8 us
    ppermute x12, starting transfers between devices, around(): lax.ppermute(value, 'q', [(source, (source + steps) % count) for source i...  40.7 us
    all_to_all x1, starting transfers between devices, across_ctx(): lax.all_to_all(blocks, 'z', split_axis=0, concat_axis=0, tiled=True)  28.7 us
    all_to_all x1, waiting for transfers between devices, across_ctx(): lax.all_to_all(blocks, 'z', split_axis=0, concat_axis=0, tiled=True)  27.2 us
    ppermute x12, waiting for transfers between devices, around(): lax.ppermute(value, 'q', [(source, (source + steps) % count) for source i...  14.7 us
    all_gather x1, blocking collectives, local(): key_all = lax.all_gather(key_grad, 'q', axis=1, tiled=True)  13.5 us
    all_to_all x2, blocking collectives, across_ctx(): lax.all_to_all(blocks, 'k', split_axis=1, concat_axis=1, tiled=True)  8.86 us
    dot_general x9, matrix products, contract_last(): lax.dot_general(first_operand, second_operand, (((1,), (1,)), ((), ())),...  7.59 us
  transfers between devices with their start and end apart: 16, of which 6 were waited for; matrix products, arithmetic and copies ran while one was open for 7% of the time, Pallas kernels for 0%

profile of v7, /device:TPU:6, one launch (start us, length us, event | category | flops | bytes accessed | tf_op | source)
XLA Modules:
  0.0 262.6 jit_solution(14100892021857140554)
XLA Ops:
  8.2 1.3 collective-permute-start
  12.6 1.4 fusion.1
  14.7 4.7 %all_to_all.25 = bf16[32,2,6,576]{3,0,2,1:T(8,128)(2,1)S(1)} all-to-all(bf16[32,2,6,576]{3,0,2,1:T(8,128)(2,1)S(1)} %copy.66), channel_id=1, replica_groups=mesh['z'=32,'k'=2,'g'=4,'q'=4] {'k'}, dimensions={1} | all-to-all | bytes 884736 | tf_op jit(solution)/shard_map/all_to_all | solution.py:21
  19.5 1.3 copy.67
  20.8 28.7 %all-to-all-start.1 = ((bf16[32,2,6,576]{3,1,2,0:T(2,128)(2,1)}), bf16[32,2,6,576]{3,1,2,0:T(2,128)(2,1)S(1)}, u32[]{:S(2)}, u32[]{:S(2)}) async-start(bf16[32,2,6,576]{3,1,2,0:T(2,128)(2,1)} %copy.67), calls=%async_computation.1 | async-start | bytes 983040 | tf_op jit(solution)/shard_map/all_to_all | solution.py:22
  49.6 13.5 %all_gather.6 = bf16[128,1024]{1,0:T(8,128)(2,1)} all-gather(bf16[128,256]{1,0:T(8,128)(2,1)S(1)} %fusion.16), channel_id=1, replica_groups=mesh['z'=32,'k'=2,'g'=4,'q'=4] {'q'}, dimensions={1}, use_global_device_ids=true | all-gather | bytes 327680 | tf_op jit(solution)/shard_map/all_gather | solution.py:92
  63.2 1.6 copy.69
  65.7 3.4 %collective-permute-start.1 = (bf16[256,576]{0,1:T(8,128)(2,1)}, bf16[256,576]{0,1:T(8,128)(2,1)}, u32[]{:S(2)}, u32[]{:S(2)}) collective-permute-start(bf16[256,576]{0,1:T(8,128)(2,1)} %get-tuple-element.26), channel_id=1, source_target_pairs={{0,1},{1,2},{2,3},{3,0},{4,5},{5,6},{6,7},{7,4},{8,9},{9,10},{10,1... | collective-permute-start | bytes 884744 | tf_op jit(solution)/shard_map/ppermute | solution.py:28
  69.1 4.6 %collective-permute-start.3 = (bf16[256,576]{0,1:T(8,128)(2,1)}, bf16[256,576]{0,1:T(8,128)(2,1)}, u32[]{:S(2)}, u32[]{:S(2)}) collective-permute-start(bf16[256,576]{0,1:T(8,128)(2,1)} %get-tuple-element.28), channel_id=1, source_target_pairs={{0,2},{1,3},{2,0},{3,1},{4,6},{5,7},{6,4},{7,5},{8,10},{9,11},{10,... | collective-permute-start | bytes 884744 | tf_op jit(solution)/shard_map/ppermute | solution.py:28
  73.7 1.9 collective-permute-start.5
  75.6 2.3 constant_dynamic-slice_fusion
  78.0 3.9 %collective-permute-start.8 = (bf16[576,256]{1,0:T(8,128)(2,1)}, bf16[576,256]{1,0:T(8,128)(2,1)}, u32[]{:S(2)}, u32[]{:S(2)}) collective-permute-start(bf16[576,256]{1,0:T(8,128)(2,1)} %bitcast.15), channel_id=1, source_target_pairs={{0,1},{1,2},{2,3},{3,0},{4,5},{5,6},{6,7},{7,4},{8,9},{9,10},{10,1... | collective-permute-start | bytes 884744 | tf_op jit(solution)/shard_map/ppermute | solution.py:28
  84.7 27.2 %all-to-all-done.1 = bf16[32,2,6,576]{3,1,2,0:T(2,128)(2,1)S(1)} async-done(((bf16[32,2,6,576]{3,1,2,0:T(2,128)(2,1)}), bf16[32,2,6,576]{3,1,2,0:T(2,128)(2,1)S(1)}, u32[]{:S(2)}, u32[]{:S(2)}) %all-to-all-start.1) | async-done | bytes 442400 | tf_op jit(solution)/shard_map/all_to_all | solution.py:22
  112.3 1.3 convolution_convert_fusion.2
  113.6 4.9 %collective-permute-start.2 = (bf16[384,256]{1,0:T(8,128)(2,1)S(1)}, bf16[384,256]{1,0:T(8,128)(2,1)S(1)}, u32[]{:S(2)}, u32[]{:S(2)}) collective-permute-start(bf16[384,256]{1,0:T(8,128)(2,1)S(1)} %convolution_convert_fusion.2), channel_id=1, source_target_pairs={{0,3},{1,0},{2,1},{3,2},{4,7},{5,4},{6,5},{7,6},{8,11},{9,8},{10,9... | collective-permute-start | bytes 589832 | tf_op jit(solution)/shard_map/ppermute | solution.py:28
  118.5 1.3 convolution_convert_fusion.1
  119.9 2.7 %collective-permute-start.4 = (bf16[384,256]{1,0:T(8,128)(2,1)S(1)}, bf16[384,256]{1,0:T(8,128)(2,1)S(1)}, u32[]{:S(2)}, u32[]{:S(2)}) collective-permute-start(bf16[384,256]{1,0:T(8,128)(2,1)S(1)} %convolution_convert_fusion.1), channel_id=1, source_target_pairs={{0,2},{1,3},{2,0},{3,1},{4,6},{5,7},{6,4},{7,5},{8,10},{9,11},{10,... | collective-permute-start | bytes 589832 | tf_op jit(solution)/shard_map/ppermute | solution.py:28
  123.8 2.9 %collective-permute-start.6 = (bf16[384,256]{1,0:T(8,128)(2,1)S(1)}, bf16[384,256]{1,0:T(8,128)(2,1)S(1)}, u32[]{:S(2)}, u32[]{:S(2)}) collective-permute-start(bf16[384,256]{1,0:T(8,128)(2,1)S(1)} %convolution_convert_fusion), channel_id=1, source_target_pairs={{0,1},{1,2},{2,3},{3,0},{4,5},{5,6},{6,7},{7,4},{8,9},{9,10},{10,1... | collective-permute-start | bytes 589832 | tf_op jit(solution)/shard_map/ppermute | solution.py:28
  127.1 3.0 %collective-permute-done.4 = bf16[384,256]{1,0:T(8,128)(2,1)S(1)} collective-permute-done((bf16[384,256]{1,0:T(8,128)(2,1)S(1)}, bf16[384,256]{1,0:T(8,128)(2,1)S(1)}, u32[]{:S(2)}, u32[]{:S(2)}) %collective-permute-start.4) | collective-permute-done | bytes 196640 | tf_op jit(solution)/shard_map/ppermute | solution.py:28
  130.1 3.2 %collective-permute-done.6 = bf16[384,256]{1,0:T(8,128)(2,1)S(1)} collective-permute-done((bf16[384,256]{1,0:T(8,128)(2,1)S(1)}, bf16[384,256]{1,0:T(8,128)(2,1)S(1)}, u32[]{:S(2)}, u32[]{:S(2)}) %collective-permute-start.6) | collective-permute-done | bytes 196640 | tf_op jit(solution)/shard_map/ppermute | solution.py:28
  133.6 2.1 collective-permute-start.7
  135.6 5.1 %collective-permute-start.12 = (bf16[576,256]{1,0:T(8,128)(2,1)S(1)}, bf16[576,256]{1,0:T(8,128)(2,1)S(1)}, u32[]{:S(2)}, u32[]{:S(2)}) collective-permute-start(bf16[576,256]{1,0:T(8,128)(2,1)S(1)} %bitcast.60), channel_id=1, source_target_pairs={{0,3},{1,0},{2,1},{3,2},{4,7},{5,4},{6,5},{7,6},{8,11},{9,8},{10,9... | collective-permute-start | bytes 884744 | tf_op jit(solution)/shard_map/ppermute | solution.py:28
  140.8 1.9 collective-permute-start.10
  142.7 3.4 %collective-permute-start.11 = (bf16[384,256]{1,0:T(8,128)(2,1)S(1)}, bf16[384,256]{1,0:T(8,128)(2,1)S(1)}, u32[]{:S(2)}, u32[]{:S(2)}) collective-permute-start(bf16[384,256]{1,0:T(8,128)(2,1)S(1)} %get-tuple-element.21), channel_id=1, source_target_pairs={{0,3},{1,0},{2,1},{3,2},{4,7},{5,4},{6,5},{7,6},{8,11},{9,8},{10,9... | collective-permute-start | bytes 589832 | tf_op jit(solution)/shard_map/ppermute | solution.py:28
  146.1 4.0 %collective-permute-start.9 = (bf16[384,256]{1,0:T(8,128)(2,1)S(1)}, bf16[384,256]{1,0:T(8,128)(2,1)S(1)}, u32[]{:S(2)}, u32[]{:S(2)}) collective-permute-start(bf16[384,256]{1,0:T(8,128)(2,1)S(1)} %get-tuple-element.21), channel_id=1, source_target_pairs={{0,2},{1,3},{2,0},{3,1},{4,6},{5,7},{6,4},{7,5},{8,10},{9,11},{10,... | collective-permute-start | bytes 589832 | tf_op jit(solution)/shard_map/ppermute | solution.py:28
  150.1 1.3 fusion.40
  151.8 3.8 %collective-permute-done.12 = bf16[576,256]{1,0:T(8,128)(2,1)S(1)} collective-permute-done((bf16[576,256]{1,0:T(8,128)(2,1)S(1)}, bf16[576,256]{1,0:T(8,128)(2,1)S(1)}, u32[]{:S(2)}, u32[]{:S(2)}) %collective-permute-start.12) | collective-permute-done | bytes 294944 | tf_op jit(solution)/shard_map/ppermute | solution.py:28
  155.6 4.7 %collective-permute-done.11 = bf16[384,256]{1,0:T(8,128)(2,1)S(1)} collective-permute-done((bf16[384,256]{1,0:T(8,128)(2,1)S(1)}, bf16[384,256]{1,0:T(8,128)(2,1)S(1)}, u32[]{:S(2)}, u32[]{:S(2)}) %collective-permute-start.11) | collective-permute-done | bytes 196640 | tf_op jit(solution)/shard_map/ppermute | solution.py:28
  161.6 4.1 %all_to_all.26 = bf16[32,2,6,576]{3,0,2,1:T(8,128)(2,1)S(1)} all-to-all(bf16[32,2,6,576]{3,0,2,1:T(8,128)(2,1)S(1)} %copy.72), channel_id=1, replica_groups=mesh['z'=32,'k'=2,'g'=4,'q'=4] {'k'}, dimensions={1} | all-to-all | bytes 884736 | tf_op jit(solution)/shard_map/all_to_all | solution.py:21
  166.2 76.8 %all_to_all.27 = bf16[32,2,6,576]{3,1,2,0:T(2,128)(2,1)S(1)} all-to-all(bf16[32,2,6,576]{3,1,2,0:T(2,128)(2,1)S(1)} %copy.73), channel_id=1, replica_groups=mesh['z'=32,'k'=2,'g'=4,'q'=4] {'z'}, dimensions={0} | all-to-all | bytes 884736 | tf_op jit(solution)/shard_map/all_to_all | solution.py:22
  245.0 4.8 %all-to-all-start.4 = ((f32[128,4,144]{0,2,1:T(8,128)}), f32[128,4,144]{0,2,1:T(8,128)S(1)}, u32[]{:S(2)}, u32[]{:S(2)}) async-start(f32[128,4,144]{0,2,1:T(8,128)} %fusion.27), calls=%async_computation.4 | async-start | bytes 589824 | tf_op jit(solution)/shard_map/all_to_all | solution.py:127
  250.6 4.0 %all-to-all-done.4 = f32[128,4,144]{0,2,1:T(8,128)S(1)} async-done(((f32[128,4,144]{0,2,1:T(8,128)}), f32[128,4,144]{0,2,1:T(8,128)S(1)}, u32[]{:S(2)}, u32[]{:S(2)}) %all-to-all-start.4) | async-done | bytes 294944 | tf_op jit(solution)/shard_map/all_to_all | solution.py:127
  (83 shorter events, 16.8 us)
Async XLA Ops:
  7.2 247.5 %copy-start = (bf16[144,4096]{1,0:T(8,128)(2,1)S(1)}, bf16[144,4096]{1,0:T(8,128)(2,1)}, u32[]{:S(2)}) copy-start(bf16[144,4096]{1,0:T(8,128)(2,1)} %param.21) | copy-start | bytes 3538948
  8.2 5.9 %collective-permute-start = (f32[3,256]{1,0:T(4,128)S(1)}, f32[3,256]{1,0:T(4,128)S(1)}, u32[]{:S(2)}, u32[]{:S(2)}) collective-permute-start(f32[3,256]{1,0:T(4,128)S(1)} %slice.42), channel_id=1, source_target_pairs={{16,0},{32,16},{48,32},{64,48},{80,64},{96,80},{112,96},{128,112},... | collective-permute-start | bytes 9224 | tf_op jit(solution)/shard_map/ppermute | solution.py:15
  10.9 0.9 copy-start.10
  11.3 2.8 %copy-start.11 = (f32[4,256]{1,0:T(4,128)S(1)}, f32[4,256]{1,0:T(4,128)}, u32[]{:S(2)}) copy-start(f32[4,256]{1,0:T(4,128)} %param.20) | copy-start | bytes 12292
  12.6 1.5 copy-start.5
  20.8 91.1 %all-to-all-start.1 = ((bf16[32,2,6,576]{3,1,2,0:T(2,128)(2,1)}), bf16[32,2,6,576]{3,1,2,0:T(2,128)(2,1)S(1)}, u32[]{:S(2)}, u32[]{:S(2)}) async-start(bf16[32,2,6,576]{3,1,2,0:T(2,128)(2,1)} %copy.67), calls=%async_computation.1 | async-start | bytes 983040 | tf_op jit(solution)/shard_map/all_to_all | solution.py:22
  49.5 62.8 %all-gather.2.cloned.1.call-start = ((), (), s32[]{:S(2)}) async-start(), calls=%async_computation.5 | async-start | bytes 1310720 | tf_op jit(solution)/shard_map/all_gather | solution.py:93
  65.7 46.6 %collective-permute-start.1 = (bf16[256,576]{0,1:T(8,128)(2,1)}, bf16[256,576]{0,1:T(8,128)(2,1)}, u32[]{:S(2)}, u32[]{:S(2)}) collective-permute-start(bf16[256,576]{0,1:T(8,128)(2,1)} %get-tuple-element.26), channel_id=1, source_target_pairs={{0,1},{1,2},{2,3},{3,0},{4,5},{5,6},{6,7},{7,4},{8,9},{9,10},{10,1... | collective-permute-start | bytes 884744 | tf_op jit(solution)/shard_map/ppermute | solution.py:28
  69.1 49.4 %collective-permute-start.3 = (bf16[256,576]{0,1:T(8,128)(2,1)}, bf16[256,576]{0,1:T(8,128)(2,1)}, u32[]{:S(2)}, u32[]{:S(2)}) collective-permute-start(bf16[256,576]{0,1:T(8,128)(2,1)} %get-tuple-element.28), channel_id=1, source_target_pairs={{0,2},{1,3},{2,0},{3,1},{4,6},{5,7},{6,4},{7,5},{8,10},{9,11},{10,... | collective-permute-start | bytes 884744 | tf_op jit(solution)/shard_map/ppermute | solution.py:28
  73.7 48.8 %collective-permute-start.5 = (bf16[256,576]{0,1:T(8,128)(2,1)}, bf16[256,576]{0,1:T(8,128)(2,1)}, u32[]{:S(2)}, u32[]{:S(2)}) collective-permute-start(bf16[256,576]{0,1:T(8,128)(2,1)} %get-tuple-element.27), channel_id=1, source_target_pairs={{0,3},{1,0},{2,1},{3,2},{4,7},{5,4},{6,5},{7,6},{8,11},{9,8},{10,9... | collective-permute-start | bytes 884744 | tf_op jit(solution)/shard_map/ppermute | solution.py:28
  75.6 6.3 %copy-start.9 = (bf16[1,64,6,256]{3,1,2,0:T(8,128)(2,1)S(1)}, bf16[1,64,6,256]{3,1,2,0:T(8,128)(2,1)}, u32[]{:S(2)}) copy-start(bf16[1,64,6,256]{3,1,2,0:T(8,128)(2,1)} %param.14) | copy-start | bytes 589828
  78.0 68.1 %collective-permute-start.8 = (bf16[576,256]{1,0:T(8,128)(2,1)}, bf16[576,256]{1,0:T(8,128)(2,1)}, u32[]{:S(2)}, u32[]{:S(2)}) collective-permute-start(bf16[576,256]{1,0:T(8,128)(2,1)} %bitcast.15), channel_id=1, source_target_pairs={{0,1},{1,2},{2,3},{3,0},{4,5},{5,6},{6,7},{7,4},{8,9},{9,10},{10,1... | collective-permute-start | bytes 884744 | tf_op jit(solution)/shard_map/ppermute | solution.py:28
  113.6 13.5 %collective-permute-start.2 = (bf16[384,256]{1,0:T(8,128)(2,1)S(1)}, bf16[384,256]{1,0:T(8,128)(2,1)S(1)}, u32[]{:S(2)}, u32[]{:S(2)}) collective-permute-start(bf16[384,256]{1,0:T(8,128)(2,1)S(1)} %convolution_convert_fusion.2), channel_id=1, source_target_pairs={{0,3},{1,0},{2,1},{3,2},{4,7},{5,4},{6,5},{7,6},{8,11},{9,8},{10,9... | collective-permute-start | bytes 589832 | tf_op jit(solution)/shard_map/ppermute | solution.py:28
  119.8 13.5 %copy-start.1 = (f32[384,256]{1,0:T(8,128)S(1)}, f32[384,256]{1,0:T(8,128)}, u32[]{:S(2)}) copy-start(f32[384,256]{1,0:T(8,128)} %reshape.107) | copy-start | bytes 1179652
  119.8 13.5 %copy-start.2 = (f32[384,256]{1,0:T(8,128)S(1)}, f32[384,256]{1,0:T(8,128)}, u32[]{:S(2)}) copy-start(f32[384,256]{1,0:T(8,128)} %reshape.108) | copy-start | bytes 1179652
  119.9 10.3 %collective-permute-start.4 = (bf16[384,256]{1,0:T(8,128)(2,1)S(1)}, bf16[384,256]{1,0:T(8,128)(2,1)S(1)}, u32[]{:S(2)}, u32[]{:S(2)}) collective-permute-start(bf16[384,256]{1,0:T(8,128)(2,1)S(1)} %convolution_convert_fusion.1), channel_id=1, source_target_pairs={{0,2},{1,3},{2,0},{3,1},{4,6},{5,7},{6,4},{7,5},{8,10},{9,11},{10,... | collective-permute-start | bytes 589832 | tf_op jit(solution)/shard_map/ppermute | solution.py:28
  123.8 9.5 %collective-permute-start.6 = (bf16[384,256]{1,0:T(8,128)(2,1)S(1)}, bf16[384,256]{1,0:T(8,128)(2,1)S(1)}, u32[]{:S(2)}, u32[]{:S(2)}) collective-permute-start(bf16[384,256]{1,0:T(8,128)(2,1)S(1)} %convolution_convert_fusion), channel_id=1, source_target_pairs={{0,1},{1,2},{2,3},{3,0},{4,5},{5,6},{6,7},{7,4},{8,9},{9,10},{10,1... | collective-permute-start | bytes 589832 | tf_op jit(solution)/shard_map/ppermute | solution.py:28
  127.1 8.6 %copy-start.8 = (bf16[4,1,144,256]{3,2,1,0:T(8,128)(2,1)S(1)}, bf16[4,1,144,256]{3,2,1,0:T(8,128)(2,1)}, u32[]{:S(2)}) copy-start(bf16[4,1,144,256]{3,2,1,0:T(8,128)(2,1)} %get-tuple-element.23) | copy-start | bytes 884740
  127.1 13.7 %copy-start.7 = (bf16[4,1,144,256]{3,2,1,0:T(8,128)(2,1)S(1)}, bf16[4,1,144,256]{3,2,1,0:T(8,128)(2,1)}, u32[]{:S(2)}) copy-start(bf16[4,1,144,256]{3,2,1,0:T(8,128)(2,1)} %get-tuple-element.22) | copy-start | bytes 884740
  133.6 17.8 %copy-start.3 = (bf16[4,1,144,256]{3,2,1,0:T(8,128)(2,1)S(1)}, bf16[4,1,144,256]{3,2,1,0:T(8,128)(2,1)}, u32[]{:S(2)}) copy-start(bf16[4,1,144,256]{3,2,1,0:T(8,128)(2,1)} %get-tuple-element.25) | copy-start | bytes 884740
  133.6 16.5 %collective-permute-start.7 = (bf16[384,256]{1,0:T(8,128)(2,1)S(1)}, bf16[384,256]{1,0:T(8,128)(2,1)S(1)}, u32[]{:S(2)}, u32[]{:S(2)}) collective-permute-start(bf16[384,256]{1,0:T(8,128)(2,1)S(1)} %get-tuple-element.21), channel_id=1, source_target_pairs={{0,1},{1,2},{2,3},{3,0},{4,5},{5,6},{6,7},{7,4},{8,9},{9,10},{10,1... | collective-permute-start | bytes 589832 | tf_op jit(solution)/shard_map/ppermute | solution.py:28
  135.6 19.9 %collective-permute-start.12 = (bf16[576,256]{1,0:T(8,128)(2,1)S(1)}, bf16[576,256]{1,0:T(8,128)(2,1)S(1)}, u32[]{:S(2)}, u32[]{:S(2)}) collective-permute-start(bf16[576,256]{1,0:T(8,128)(2,1)S(1)} %bitcast.60), channel_id=1, source_target_pairs={{0,3},{1,0},{2,1},{3,2},{4,7},{5,4},{6,5},{7,6},{8,11},{9,8},{10,9... | collective-permute-start | bytes 884744 | tf_op jit(solution)/shard_map/ppermute | solution.py:28
  140.8 19.8 %collective-permute-start.10 = (bf16[576,256]{1,0:T(8,128)(2,1)S(1)}, bf16[576,256]{1,0:T(8,128)(2,1)S(1)}, u32[]{:S(2)}, u32[]{:S(2)}) collective-permute-start(bf16[576,256]{1,0:T(8,128)(2,1)S(1)} %bitcast.59), channel_id=1, source_target_pairs={{0,2},{1,3},{2,0},{3,1},{4,6},{5,7},{6,4},{7,5},{8,10},{9,11},{10,... | collective-permute-start | bytes 884744 | tf_op jit(solution)/shard_map/ppermute | solution.py:28
  142.7 17.6 %collective-permute-start.11 = (bf16[384,256]{1,0:T(8,128)(2,1)S(1)}, bf16[384,256]{1,0:T(8,128)(2,1)S(1)}, u32[]{:S(2)}, u32[]{:S(2)}) collective-permute-start(bf16[384,256]{1,0:T(8,128)(2,1)S(1)} %get-tuple-element.21), channel_id=1, source_target_pairs={{0,3},{1,0},{2,1},{3,2},{4,7},{5,4},{6,5},{7,6},{8,11},{9,8},{10,9... | collective-permute-start | bytes 589832 | tf_op jit(solution)/shard_map/ppermute | solution.py:28
  146.1 14.5 %collective-permute-start.9 = (bf16[384,256]{1,0:T(8,128)(2,1)S(1)}, bf16[384,256]{1,0:T(8,128)(2,1)S(1)}, u32[]{:S(2)}, u32[]{:S(2)}) collective-permute-start(bf16[384,256]{1,0:T(8,128)(2,1)S(1)} %get-tuple-element.21), channel_id=1, source_target_pairs={{0,2},{1,3},{2,0},{3,1},{4,6},{5,7},{6,4},{7,5},{8,10},{9,11},{10,... | collective-permute-start | bytes 589832 | tf_op jit(solution)/shard_map/ppermute | solution.py:28
  243.1 0.9 copy-start.6
  244.0 10.6 %copy-start.4 = (bf16[128,4096]{1,0:T(8,128)(2,1)S(1)}, bf16[128,4096]{1,0:T(8,128)(2,1)}, u32[]{:S(2)}) copy-start(bf16[128,4096]{1,0:T(8,128)(2,1)} %all-gather.2.cloned.1.call-done) | copy-start | bytes 3145732
  245.0 9.6 %all-to-all-start.4 = ((f32[128,4,144]{0,2,1:T(8,128)}), f32[128,4,144]{0,2,1:T(8,128)S(1)}, u32[]{:S(2)}, u32[]{:S(2)}) async-start(f32[128,4,144]{0,2,1:T(8,128)} %fusion.27), calls=%async_computation.4 | async-start | bytes 589824 | tf_op jit(solution)/shard_map/all_to_all | solution.py:127
Sparse Core Ops, SparseCore 0:
  63.3 41.6 all-gather.1

commit v8 on v7

--- a/solution.py
+++ b/solution.py
@@ -107,21 +107,28 @@
     for shift in range(1, split):
         down_got.append(around(down_slice((my_quarter + shift) % split), shift))
         up_got.append(around(up_slice((my_quarter + shift) % split), shift))
+    by_block = (my_quarter - jnp.arange(split)) % split
+    down_got = jnp.take(jnp.stack(down_got), by_block, axis=0)
+    up_got = jnp.take(jnp.stack(up_got), by_block, axis=0)
     got_rows = across_ctx(scaled_rows)
-    key_all, got_rows = lax.optimization_barrier((key_all, got_rows))
+    key_all, down_got, up_got, got_rows = lax.optimization_barrier(
+        (key_all, down_got, up_got, got_rows)
+    )
     key_input = contract_last(key_all, w_key)
     gate_pre = saved_gate.reshape(slot_count, -1).astype(jnp.float32)
     up_output = saved_up.reshape(slot_count, -1).astype(jnp.float32)
-    hidden_grad = contract_last(got_rows, down_got[0])
-    for shift in range(1, split):
-        share = contract_last(got_rows, down_got[shift]).astype(jnp.bfloat16)
-        hidden_grad = hidden_grad + around(share, -shift).astype(jnp.float32)
+    hidden_parts = jnp.einsum(
+        "sf,qhf->qsh", got_rows, down_got, preferred_element_type=jnp.float32
+    ).astype(jnp.bfloat16)
+    hidden_parts = lax.all_to_all(hidden_parts, "q", 0, 0, tiled=True)
+    hidden_grad = jnp.sum(hidden_parts.astype(jnp.float32), 0)
     gate_grad = (hidden_grad * up_output * silu_slope(gate_pre)).astype(jnp.bfloat16)
     up_grad = (hidden_grad * jax.nn.silu(gate_pre)).astype(jnp.bfloat16)
-    summed_rows = contract_last(up_grad, up_got[0])
-    for shift in range(1, split):
-        summed_rows = summed_rows + contract_last(around(up_grad, shift), up_got[shift])
-    summed_rows = summed_rows.astype(jnp.bfloat16)
+    up_all = jnp.broadcast_to(up_grad[None], (split, *up_grad.shape))
+    up_all = lax.all_to_all(up_all, "q", 0, 0, tiled=True)
+    summed_rows = jnp.einsum(
+        "qsh,qfh->sf", up_all, up_got, preferred_element_type=jnp.float32
+    ).astype(jnp.bfloat16)
     came_back = across_ctx(summed_rows)
     token_rows = jnp.dot(placement, came_back, preferred_element_type=jnp.float32)
     token_rows = lax.all_to_all(token_rows.reshape(tok_rows, groups, -1), "g", 1, 1, tiled=True)

time: 266 us -> 249 us (0.936)
  blocking collectives: 99.2 us -> 35.2 us
  waiting for transfers between devices: 46 us -> 94.5 us
  other arithmetic: 2.77 us -> 8.31 us
  matrix products: 10 us -> 6.17 us
    all_to_all x1, blocking collectives: 76.8 us -> 12.8 us  [local(): up_all = lax.all_to_all(up_all, 'q', 0, 0, tiled=True)]
    all_to_all x1 -> x2, waiting for transfers between devices: 27.2 us -> 74 us  [across_ctx(): lax.all_to_all(blocks, 'z', split_axis=0, concat_axis=0, tiled=True)]
    ppermute x12 -> x6, starting transfers between devices: 40.7 us -> 20.2 us  [around(): lax.ppermute(value, 'q', [(source, (source + steps) % count) for source i...]
    all_to_all x1 -> x2, starting transfers between devices: 28.7 us -> 41.5 us  [across_ctx(): lax.all_to_all(blocks, 'z', split_axis=0, concat_axis=0, tiled=True)]
    all_to_all x0 -> x1, waiting for transfers between devices: none -> 11.2 us  [local(): hidden_parts = lax.all_to_all(hidden_parts, 'q', 0, 0, tiled=True)]
    ppermute x12 -> x6, waiting for transfers between devices: 14.7 us -> 5.54 us  [around(): lax.ppermute(value, 'q', [(source, (source + steps) % count) for source i...]
    dot_general x9 -> x1, matrix products: 7.59 us -> 1.11 us  [contract_last(): lax.dot_general(first_operand, second_operand, (((1,), (1,)), ((), ())),...]
    all_to_all x0 -> x1, starting transfers between devices: none -> 4.6 us  [local(): hidden_parts = lax.all_to_all(hidden_parts, 'q', 0, 0, tiled=True)]
  transfers between devices with their start and end apart: 16 -> 12, of which waited for: 6 -> 6; matrix products, arithmetic and copies ran while one was open for 7% -> 7% of each run, Pallas kernels for 0% -> 0%
where the time goes in v8:
time: 249 us; the launch traced here: 247 us
  waiting for transfers between devices  94.5 us (38%)
  starting transfers between devices  73.3 us (29%)
  blocking collectives  35.2 us (14%)
  local copies, waits for them, and re-layouts  14.9 us (6%)
  between operations  14.6 us (6%)
  other arithmetic  8.31 us (3%)
  matrix products  6.17 us (2%)
    all_to_all x2, waiting for transfers between devices, across_ctx(): lax.all_to_all(blocks, 'z', split_axis=0, concat_axis=0, tiled=True)  74 us
    all_to_all x2, starting transfers between devices, across_ctx(): lax.all_to_all(blocks, 'z', split_axis=0, concat_axis=0, tiled=True)  41.5 us
    ppermute x6, starting transfers between devices, around(): lax.ppermute(value, 'q', [(source, (source + steps) % count) for source i...  20.2 us
    all_gather x1, blocking collectives, local(): key_all = lax.all_gather(key_grad, 'q', axis=1, tiled=True)  13.5 us
    all_to_all x1, blocking collectives, local(): up_all = lax.all_to_all(up_all, 'q', 0, 0, tiled=True)  12.8 us
    all_to_all x1, waiting for transfers between devices, local(): hidden_parts = lax.all_to_all(hidden_parts, 'q', 0, 0, tiled=True)  11.2 us
    all_to_all x2, blocking collectives, across_ctx(): lax.all_to_all(blocks, 'k', split_axis=1, concat_axis=1, tiled=True)  8.86 us
    all_to_all x1, starting transfers between devices, local(): lax.all_to_all(token_rows.reshape(tok_rows, groups, -1), 'g', 1, 1, tiled...  5.6 us
  transfers between devices with their start and end apart: 12, of which 6 were waited for; matrix products, arithmetic and copies ran while one was open for 7% of the time, Pallas kernels for 0%

profile of v8, /device:TPU:6, one launch (start us, length us, event | category | flops | bytes accessed | tf_op | source)
XLA Modules:
  0.0 246.9 jit_solution(18335036188636627789)
XLA Ops:
  8.2 1.3 collective-permute-start
  12.6 1.4 fusion.1
  14.7 4.7 %all_to_all.35 = bf16[32,2,6,576]{3,0,2,1:T(8,128)(2,1)S(1)} all-to-all(bf16[32,2,6,576]{3,0,2,1:T(8,128)(2,1)S(1)} %copy.70), channel_id=1, replica_groups=mesh['z'=32,'k'=2,'g'=4,'q'=4] {'k'}, dimensions={1} | all-to-all | bytes 884736 | tf_op jit(solution)/shard_map/all_to_all | solution.py:21
  19.5 1.3 copy.71
  20.8 28.8 %all-to-all-start.1 = ((bf16[32,2,6,576]{3,1,2,0:T(2,128)(2,1)}), bf16[32,2,6,576]{3,1,2,0:T(2,128)(2,1)}, u32[]{:S(2)}, u32[]{:S(2)}) async-start(bf16[32,2,6,576]{3,1,2,0:T(2,128)(2,1)} %copy.71), calls=%async_computation.1 | async-start | bytes 983040 | tf_op jit(solution)/shard_map/all_to_all | solution.py:22
  49.7 13.5 %all_gather.6 = bf16[128,1024]{1,0:T(8,128)(2,1)} all-gather(bf16[128,256]{1,0:T(8,128)(2,1)S(1)} %fusion.14), channel_id=1, replica_groups=mesh['z'=32,'k'=2,'g'=4,'q'=4] {'q'}, dimensions={1}, use_global_device_ids=true | all-gather | bytes 327680 | tf_op jit(solution)/shard_map/all_gather | solution.py:92
  64.3 3.2 %collective-permute-start.4 = (bf16[576,256]{1,0:T(8,128)(2,1)}, bf16[576,256]{1,0:T(8,128)(2,1)S(1)}, u32[]{:S(2)}, u32[]{:S(2)}) collective-permute-start(bf16[576,256]{1,0:T(8,128)(2,1)} %bitcast.19), channel_id=1, source_target_pairs={{0,1},{1,2},{2,3},{3,0},{4,5},{5,6},{6,7},{7,4},{8,9},{9,10},{10,1... | collective-permute-start | bytes 884744 | tf_op jit(solution)/shard_map/ppermute | solution.py:28
  67.5 4.6 %collective-permute-start.5 = (bf16[576,256]{1,0:T(8,128)(2,1)}, bf16[576,256]{1,0:T(8,128)(2,1)S(1)}, u32[]{:S(2)}, u32[]{:S(2)}) collective-permute-start(bf16[576,256]{1,0:T(8,128)(2,1)} %bitcast.21), channel_id=1, source_target_pairs={{0,2},{1,3},{2,0},{3,1},{4,6},{5,7},{6,4},{7,5},{8,10},{9,11},{10,... | collective-permute-start | bytes 884744 | tf_op jit(solution)/shard_map/ppermute | solution.py:28
  72.1 2.0 collective-permute-start.6
  74.1 1.6 copy.68
  76.7 3.8 %collective-permute-start.1 = (bf16[256,576]{0,1:T(8,128)(2,1)}, bf16[256,576]{0,1:T(8,128)(2,1)S(1)}, u32[]{:S(2)}, u32[]{:S(2)}) collective-permute-start(bf16[256,576]{0,1:T(8,128)(2,1)} %get-tuple-element.29), channel_id=1, source_target_pairs={{0,1},{1,2},{2,3},{3,0},{4,5},{5,6},{6,7},{7,4},{8,9},{9,10},{10,1... | collective-permute-start | bytes 884744 | tf_op jit(solution)/shard_map/ppermute | solution.py:28
  80.6 2.8 %collective-permute-start.2 = (bf16[256,576]{0,1:T(8,128)(2,1)}, bf16[256,576]{0,1:T(8,128)(2,1)}, u32[]{:S(2)}, u32[]{:S(2)}) collective-permute-start(bf16[256,576]{0,1:T(8,128)(2,1)} %get-tuple-element.28), channel_id=1, source_target_pairs={{0,2},{1,3},{2,0},{3,1},{4,6},{5,7},{6,4},{7,5},{8,10},{9,11},{10,... | collective-permute-start | bytes 884744 | tf_op jit(solution)/shard_map/ppermute | solution.py:28
  83.4 3.8 %collective-permute-start.3 = (bf16[256,576]{0,1:T(8,128)(2,1)}, bf16[256,576]{0,1:T(8,128)(2,1)}, u32[]{:S(2)}, u32[]{:S(2)}) collective-permute-start(bf16[256,576]{0,1:T(8,128)(2,1)} %get-tuple-element.27), channel_id=1, source_target_pairs={{0,3},{1,0},{2,1},{3,2},{4,7},{5,4},{6,5},{7,6},{8,11},{9,8},{10,9... | collective-permute-start | bytes 884744 | tf_op jit(solution)/shard_map/ppermute | solution.py:28
  87.2 1.1 pad_maximum_fusion.1
  88.3 1.6 gather_fusion.1
  90.0 3.5 %collective-permute-done.1 = bf16[256,576]{0,1:T(8,128)(2,1)S(1)} collective-permute-done((bf16[256,576]{0,1:T(8,128)(2,1)}, bf16[256,576]{0,1:T(8,128)(2,1)S(1)}, u32[]{:S(2)}, u32[]{:S(2)}) %collective-permute-start.1) | collective-permute-done | bytes 294944 | tf_op jit(solution)/shard_map/ppermute | solution.py:28
  93.5 2.0 collective-permute-done.3
  95.5 1.3 pad_maximum_fusion
  97.4 2.5 %broadcast_select_fusion = bf16[4,576,256]{2,1,0:T(8,128)(2,1)} fusion(bf16[4,576,256]{2,1,0:T(8,128)(2,1)} %gather_fusion.1, pred[4]{0:T(512)(128)(4,1)S(1)} %compare_and_fusion), kind=kLoop, calls=%fused_computation.14 | loop fusion | flops 589824 | bytes 2359300 | tf_op jit(solution)/shard_map/jit(_take)/select_n | solution.py:112
  100.1 11.9 %all-to-all-done.1 = bf16[32,2,6,576]{3,1,2,0:T(2,128)(2,1)} async-done(((bf16[32,2,6,576]{3,1,2,0:T(2,128)(2,1)}), bf16[32,2,6,576]{3,1,2,0:T(2,128)(2,1)}, u32[]{:S(2)}, u32[]{:S(2)}) %all-to-all-start.1) | async-done | bytes 442400 | tf_op jit(solution)/shard_map/all_to_all | solution.py:22
  112.0 1.1 copy.72
  113.5 1.9 fusion
  115.3 4.6 %all-to-all-start.2 = ((bf16[4,384,256]{1,2,0:T(8,128)(2,1)}), bf16[4,384,256]{1,2,0:T(8,128)(2,1)S(1)}, u32[]{:S(2)}, u32[]{:S(2)}) async-start(bf16[4,384,256]{1,2,0:T(8,128)(2,1)} %fusion), calls=%async_computation.2 | async-start | bytes 1572864 | tf_op jit(solution)/shard_map/all_to_all | solution.py:123
  120.3 11.2 %all-to-all-done.2 = bf16[4,384,256]{1,2,0:T(8,128)(2,1)S(1)} async-done(((bf16[4,384,256]{1,2,0:T(8,128)(2,1)}), bf16[4,384,256]{1,2,0:T(8,128)(2,1)S(1)}, u32[]{:S(2)}, u32[]{:S(2)}) %all-to-all-start.2) | async-done | bytes 786464 | tf_op jit(solution)/shard_map/all_to_all | solution.py:123
  131.9 12.8 %all_to_all.36 = bf16[4,384,256]{2,1,0:T(8,128)(2,1)S(1)} all-to-all(bf16[4,384,256]{2,1,0:T(8,128)(2,1)S(1)} %broadcast_in_dim.50), channel_id=1, replica_groups=mesh['z'=32,'k'=2,'g'=4,'q'=4] {'q'}, dimensions={0} | all-to-all | bytes 1572864 | tf_op jit(solution)/shard_map/all_to_all | solution.py:128
  146.1 4.1 %all_to_all.37 = bf16[32,2,6,576]{3,0,2,1:T(8,128)(2,1)S(1)} all-to-all(bf16[32,2,6,576]{3,0,2,1:T(8,128)(2,1)S(1)} %copy.79), channel_id=1, replica_groups=mesh['z'=32,'k'=2,'g'=4,'q'=4] {'k'}, dimensions={1} | all-to-all | bytes 884736 | tf_op jit(solution)/shard_map/all_to_all | solution.py:21
  150.2 1.3 copy.80
  151.5 12.7 %all-to-all-start.5 = ((bf16[32,2,6,576]{3,1,2,0:T(2,128)(2,1)}), bf16[32,2,6,576]{3,1,2,0:T(2,128)(2,1)S(1)}, u32[]{:S(2)}, u32[]{:S(2)}) async-start(bf16[32,2,6,576]{3,1,2,0:T(2,128)(2,1)} %copy.80), calls=%async_computation.5 | async-start | bytes 983040 | tf_op jit(solution)/shard_map/all_to_all | solution.py:22
  164.4 62.1 %all-to-all-done.5 = bf16[32,2,6,576]{3,1,2,0:T(2,128)(2,1)S(1)} async-done(((bf16[32,2,6,576]{3,1,2,0:T(2,128)(2,1)}), bf16[32,2,6,576]{3,1,2,0:T(2,128)(2,1)S(1)}, u32[]{:S(2)}, u32[]{:S(2)}) %all-to-all-start.5) | async-done | bytes 442400 | tf_op jit(solution)/shard_map/all_to_all | solution.py:22
  228.6 5.6 %all-to-all-start.6 = ((f32[128,4,144]{0,2,1:T(8,128)}), f32[128,4,144]{0,2,1:T(8,128)S(1)}, u32[]{:S(2)}, u32[]{:S(2)}) async-start(f32[128,4,144]{0,2,1:T(8,128)} %fusion.25), calls=%async_computation.6 | async-start | bytes 589824 | tf_op jit(solution)/shard_map/all_to_all | solution.py:134
  235.2 3.7 %all-to-all-done.6 = f32[128,4,144]{0,2,1:T(8,128)S(1)} async-done(((f32[128,4,144]{0,2,1:T(8,128)}), f32[128,4,144]{0,2,1:T(8,128)S(1)}, u32[]{:S(2)}, u32[]{:S(2)}) %all-to-all-start.6) | async-done | bytes 294944 | tf_op jit(solution)/shard_map/all_to_all | solution.py:134
  239.0 1.1 convolution_add_fusion
  (78 shorter events, 13.3 us)
Async XLA Ops:
  7.2 231.8 %copy-start = (bf16[144,4096]{1,0:T(8,128)(2,1)S(1)}, bf16[144,4096]{1,0:T(8,128)(2,1)}, u32[]{:S(2)}) copy-start(bf16[144,4096]{1,0:T(8,128)(2,1)} %param.21) | copy-start | bytes 3538948
  8.2 5.9 %collective-permute-start = (f32[3,256]{1,0:T(4,128)S(1)}, f32[3,256]{1,0:T(4,128)S(1)}, u32[]{:S(2)}, u32[]{:S(2)}) collective-permute-start(f32[3,256]{1,0:T(4,128)S(1)} %slice.46), channel_id=1, source_target_pairs={{16,0},{32,16},{48,32},{64,48},{80,64},{96,80},{112,96},{128,112},... | collective-permute-start | bytes 9224 | tf_op jit(solution)/shard_map/ppermute | solution.py:15
  10.9 0.9 copy-start.8
  11.3 2.8 %copy-start.9 = (f32[4,256]{1,0:T(4,128)S(1)}, f32[4,256]{1,0:T(4,128)}, u32[]{:S(2)}) copy-start(f32[4,256]{1,0:T(4,128)} %param.20) | copy-start | bytes 12292
  12.6 1.5 copy-start.4
  19.5 43.8 %copy-start.2 = (bf16[1,2304,256]{2,1,0:T(8,128)(2,1)S(1)}, bf16[1,2304,256]{2,1,0:T(8,128)(2,1)}, u32[]{:S(2)}) copy-start(bf16[1,2304,256]{2,1,0:T(8,128)(2,1)} %param.16) | copy-start | bytes 3538948
  20.8 91.2 %all-to-all-start.1 = ((bf16[32,2,6,576]{3,1,2,0:T(2,128)(2,1)}), bf16[32,2,6,576]{3,1,2,0:T(2,128)(2,1)}, u32[]{:S(2)}, u32[]{:S(2)}) async-start(bf16[32,2,6,576]{3,1,2,0:T(2,128)(2,1)} %copy.71), calls=%async_computation.1 | async-start | bytes 983040 | tf_op jit(solution)/shard_map/all_to_all | solution.py:22
  49.7 63.8 %all-gather.2.cloned.1.call-start = ((), (), s32[]{:S(2)}) async-start(), calls=%async_computation.7 | async-start | bytes 1310720 | tf_op jit(solution)/shard_map/all_gather | solution.py:93
  64.3 19.1 %collective-permute-start.4 = (bf16[576,256]{1,0:T(8,128)(2,1)}, bf16[576,256]{1,0:T(8,128)(2,1)S(1)}, u32[]{:S(2)}, u32[]{:S(2)}) collective-permute-start(bf16[576,256]{1,0:T(8,128)(2,1)} %bitcast.19), channel_id=1, source_target_pairs={{0,1},{1,2},{2,3},{3,0},{4,5},{5,6},{6,7},{7,4},{8,9},{9,10},{10,1... | collective-permute-start | bytes 884744 | tf_op jit(solution)/shard_map/ppermute | solution.py:28
  67.5 19.7 %collective-permute-start.5 = (bf16[576,256]{1,0:T(8,128)(2,1)}, bf16[576,256]{1,0:T(8,128)(2,1)S(1)}, u32[]{:S(2)}, u32[]{:S(2)}) collective-permute-start(bf16[576,256]{1,0:T(8,128)(2,1)} %bitcast.21), channel_id=1, source_target_pairs={{0,2},{1,3},{2,0},{3,1},{4,6},{5,7},{6,4},{7,5},{8,10},{9,11},{10,... | collective-permute-start | bytes 884744 | tf_op jit(solution)/shard_map/ppermute | solution.py:28
  72.1 15.1 %collective-permute-start.6 = (bf16[576,256]{1,0:T(8,128)(2,1)}, bf16[576,256]{1,0:T(8,128)(2,1)}, u32[]{:S(2)}, u32[]{:S(2)}) collective-permute-start(bf16[576,256]{1,0:T(8,128)(2,1)} %bitcast.23), channel_id=1, source_target_pairs={{0,3},{1,0},{2,1},{3,2},{4,7},{5,4},{6,5},{7,6},{8,11},{9,8},{10,9... | collective-permute-start | bytes 884744 | tf_op jit(solution)/shard_map/ppermute | solution.py:28
  76.7 16.8 %collective-permute-start.1 = (bf16[256,576]{0,1:T(8,128)(2,1)}, bf16[256,576]{0,1:T(8,128)(2,1)S(1)}, u32[]{:S(2)}, u32[]{:S(2)}) collective-permute-start(bf16[256,576]{0,1:T(8,128)(2,1)} %get-tuple-element.29), channel_id=1, source_target_pairs={{0,1},{1,2},{2,3},{3,0},{4,5},{5,6},{6,7},{7,4},{8,9},{9,10},{10,1... | collective-permute-start | bytes 884744 | tf_op jit(solution)/shard_map/ppermute | solution.py:28
  80.6 12.9 %collective-permute-start.2 = (bf16[256,576]{0,1:T(8,128)(2,1)}, bf16[256,576]{0,1:T(8,128)(2,1)}, u32[]{:S(2)}, u32[]{:S(2)}) collective-permute-start(bf16[256,576]{0,1:T(8,128)(2,1)} %get-tuple-element.28), channel_id=1, source_target_pairs={{0,2},{1,3},{2,0},{3,1},{4,6},{5,7},{6,4},{7,5},{8,10},{9,11},{10,... | collective-permute-start | bytes 884744 | tf_op jit(solution)/shard_map/ppermute | solution.py:28
  83.4 12.2 %collective-permute-start.3 = (bf16[256,576]{0,1:T(8,128)(2,1)}, bf16[256,576]{0,1:T(8,128)(2,1)}, u32[]{:S(2)}, u32[]{:S(2)}) collective-permute-start(bf16[256,576]{0,1:T(8,128)(2,1)} %get-tuple-element.27), channel_id=1, source_target_pairs={{0,3},{1,0},{2,1},{3,2},{4,7},{5,4},{6,5},{7,6},{8,11},{9,8},{10,9... | collective-permute-start | bytes 884744 | tf_op jit(solution)/shard_map/ppermute | solution.py:28
  115.3 4.6 %copy-start.6 = (bf16[1,64,6,256]{3,1,2,0:T(8,128)(2,1)S(1)}, bf16[1,64,6,256]{3,1,2,0:T(8,128)(2,1)}, u32[]{:S(2)}) copy-start(bf16[1,64,6,256]{3,1,2,0:T(8,128)(2,1)} %param.14) | copy-start | bytes 589828
  115.3 16.1 %all-to-all-start.2 = ((bf16[4,384,256]{1,2,0:T(8,128)(2,1)}), bf16[4,384,256]{1,2,0:T(8,128)(2,1)S(1)}, u32[]{:S(2)}, u32[]{:S(2)}) async-start(bf16[4,384,256]{1,2,0:T(8,128)(2,1)} %fusion), calls=%async_computation.2 | async-start | bytes 1572864 | tf_op jit(solution)/shard_map/all_to_all | solution.py:123
  131.8 12.9 %copy-start.1 = (bf16[4,576,256]{2,1,0:T(8,128)(2,1)S(1)}, bf16[4,576,256]{2,1,0:T(8,128)(2,1)}, u32[]{:S(2)}) copy-start(bf16[4,576,256]{2,1,0:T(8,128)(2,1)} %broadcast_select_fusion) | copy-start | bytes 3538948
  151.5 75.1 %all-to-all-start.5 = ((bf16[32,2,6,576]{3,1,2,0:T(2,128)(2,1)}), bf16[32,2,6,576]{3,1,2,0:T(2,128)(2,1)S(1)}, u32[]{:S(2)}, u32[]{:S(2)}) async-start(bf16[32,2,6,576]{3,1,2,0:T(2,128)(2,1)} %copy.80), calls=%async_computation.5 | async-start | bytes 983040 | tf_op jit(solution)/shard_map/all_to_all | solution.py:22
  226.7 0.9 copy-start.5
  227.0 7.2 %copy-start.7 = (bf16[1,64,6,256]{3,1,2,0:T(8,128)(2,1)S(1)}, bf16[1,64,6,256]{3,1,2,0:T(8,128)(2,1)}, u32[]{:S(2)}) copy-start(bf16[1,64,6,256]{3,1,2,0:T(8,128)(2,1)} %param.15) | copy-start | bytes 589828
  228.5 10.4 %copy-start.3 = (bf16[128,4096]{1,0:T(8,128)(2,1)S(1)}, bf16[128,4096]{1,0:T(8,128)(2,1)}, u32[]{:S(2)}) copy-start(bf16[128,4096]{1,0:T(8,128)(2,1)} %all-gather.2.cloned.1.call-done) | copy-start | bytes 3145732
  228.6 10.4 %all-to-all-start.6 = ((f32[128,4,144]{0,2,1:T(8,128)}), f32[128,4,144]{0,2,1:T(8,128)S(1)}, u32[]{:S(2)}, u32[]{:S(2)}) async-start(f32[128,4,144]{0,2,1:T(8,128)} %fusion.25), calls=%async_computation.6 | async-start | bytes 589824 | tf_op jit(solution)/shard_map/all_to_all | solution.py:134
Sparse Core Ops, SparseCore 0:
  63.4 41.4 all-gather.1

commit v9 on v8

--- a/solution.py
+++ b/solution.py
@@ -88,9 +88,6 @@
         placement, grad_chunk, (((0,), (0,)), ((), ())), preferred_element_type=jnp.float32
     )
     scaled_rows = (slot_probs[:, None] * picked).astype(jnp.bfloat16)
-    key_grad, scaled_rows = lax.optimization_barrier((key_grad, scaled_rows))
-    key_all = lax.all_gather(key_grad, "q", axis=1, tiled=True)
-    key_all = lax.all_gather(key_all, "g", axis=1, tiled=True)
     hidden = w_down.shape[1]
     block = features // (groups * split)
     down_own = w_down[0].reshape(hidden, split, chunk)
@@ -111,10 +108,7 @@
     down_got = jnp.take(jnp.stack(down_got), by_block, axis=0)
     up_got = jnp.take(jnp.stack(up_got), by_block, axis=0)
     got_rows = across_ctx(scaled_rows)
-    key_all, down_got, up_got, got_rows = lax.optimization_barrier(
-        (key_all, down_got, up_got, got_rows)
-    )
-    key_input = contract_last(key_all, w_key)
+    down_got, up_got, got_rows = lax.optimization_barrier((down_got, up_got, got_rows))
     gate_pre = saved_gate.reshape(slot_count, -1).astype(jnp.float32)
     up_output = saved_up.reshape(slot_count, -1).astype(jnp.float32)
     hidden_parts = jnp.einsum(
@@ -129,7 +123,22 @@
     summed_rows = jnp.einsum(
         "qsh,qfh->sf", up_all, up_got, preferred_element_type=jnp.float32
     ).astype(jnp.bfloat16)
+    key_grad, summed_rows = lax.optimization_barrier((key_grad, summed_rows))
+    key_group = lax.all_gather(key_grad, "q", axis=1, tiled=True)
+    key_got = [key_group]
+    for shift in range(1, groups):
+        key_got.append(
+            lax.ppermute(key_group, "g", [(i, (i + shift) % groups) for i in range(groups)])
+        )
     came_back = across_ctx(summed_rows)
+    key_got, came_back = lax.optimization_barrier((key_got, came_back))
+    key_got = jnp.take(jnp.stack(key_got), (my_group - jnp.arange(groups)) % groups, axis=0)
+    key_input = jnp.einsum(
+        "gtc,fgc->tf",
+        key_got,
+        w_key.reshape(w_key.shape[0], groups, -1),
+        preferred_element_type=jnp.float32,
+    )
     token_rows = jnp.dot(placement, came_back, preferred_element_type=jnp.float32)
     token_rows = lax.all_to_all(token_rows.reshape(tok_rows, groups, -1), "g", 1, 1, tiled=True)
     moe_share = jnp.sum(token_rows, 1)

time: 249 us -> 227 us (0.912)
  blocking collectives: 35.2 us -> 20.8 us
  between operations: 14.6 us -> 1.27 us
  starting transfers between devices: 73.3 us -> 76.3 us
  waiting for transfers between devices: 94.5 us -> 97.4 us
  matrix products: 6.17 us -> 8.69 us
    all_to_all x1 -> x0, blocking collectives: 12.8 us -> none  [local(): up_all = lax.all_to_all(up_all, 'q', 0, 0, tiled=True)]
    all_to_all x2, waiting for transfers between devices: 74 us -> 61.5 us  [across_ctx(): lax.all_to_all(blocks, 'z', split_axis=0, concat_axis=0, tiled=True)]
    ppermute x0 -> x3, starting transfers between devices: none -> 8.6 us  [local(): lax.ppermute(key_group, 'g', [(i, (i + shift) % groups) for i in range(gr...]
    ppermute x6, waiting for transfers between devices: 5.54 us -> 13.9 us  [around(): lax.ppermute(value, 'q', [(source, (source + steps) % count) for source i...]
    all_to_all x2, starting transfers between devices: 41.5 us -> 33.4 us  [across_ctx(): lax.all_to_all(blocks, 'z', split_axis=0, concat_axis=0, tiled=True)]
    all_to_all x0 -> x1, waiting for transfers between devices: none -> 7.03 us  [local(): up_all = lax.all_to_all(up_all, 'q', 0, 0, tiled=True)]
    all_to_all x0 -> x1, starting transfers between devices: none -> 3.49 us  [local(): up_all = lax.all_to_all(up_all, 'q', 0, 0, tiled=True)]
  transfers between devices with their start and end apart: 12 -> 15, of which waited for: 6 -> 10; matrix products, arithmetic and copies ran while one was open for 7% -> 5% of each run, Pallas kernels for 0% -> 0%
where the time goes in v9:
time: 227 us; the launch traced here: 225 us
  waiting for transfers between devices  97.4 us (43%)
  starting transfers between devices  76.3 us (34%)
  blocking collectives  20.8 us (9%)
  local copies, waits for them, and re-layouts  14.7 us (6%)
  matrix products  8.69 us (4%)
  other arithmetic  6.31 us (3%)
    all_to_all x2, waiting for transfers between devices, across_ctx(): lax.all_to_all(blocks, 'z', split_axis=0, concat_axis=0, tiled=True)  61.5 us
    all_to_all x2, starting transfers between devices, across_ctx(): lax.all_to_all(blocks, 'z', split_axis=0, concat_axis=0, tiled=True)  33.4 us
    ppermute x6, starting transfers between devices, around(): lax.ppermute(value, 'q', [(source, (source + steps) % count) for source i...  20.2 us
    ppermute x6, waiting for transfers between devices, around(): lax.ppermute(value, 'q', [(source, (source + steps) % count) for source i...  13.9 us
    all_gather x1, blocking collectives, local(): key_group = lax.all_gather(key_grad, 'q', axis=1, tiled=True)  12.6 us
    all_to_all x1, waiting for transfers between devices, local(): hidden_parts = lax.all_to_all(hidden_parts, 'q', 0, 0, tiled=True)  11.1 us
    ppermute x3, starting transfers between devices, local(): lax.ppermute(key_group, 'g', [(i, (i + shift) % groups) for i in range(gr...  8.6 us
    all_to_all x2, blocking collectives, across_ctx(): lax.all_to_all(blocks, 'k', split_axis=1, concat_axis=1, tiled=True)  8.22 us
  transfers between devices with their start and end apart: 15, of which 10 were waited for; matrix products, arithmetic and copies ran while one was open for 5% of the time, Pallas kernels for 0%

profile of v9, /device:TPU:6, one launch (start us, length us, event | category | flops | bytes accessed | tf_op | source)
XLA Modules:
  0.0 225.4 jit_solution(4778869169174129767)
XLA Ops:
  5.0 4.1 %all_to_all.35 = bf16[32,2,6,576]{3,0,2,1:T(8,128)(2,1)S(1)} all-to-all(bf16[32,2,6,576]{3,0,2,1:T(8,128)(2,1)S(1)} %copy.71), channel_id=1, replica_groups=mesh['z'=32,'k'=2,'g'=4,'q'=4] {'k'}, dimensions={1} | all-to-all | bytes 884736 | tf_op jit(solution)/shard_map/all_to_all | solution.py:21
  9.1 1.3 copy.72
  10.4 28.7 %all-to-all-start.1 = ((bf16[32,2,6,576]{3,1,2,0:T(2,128)(2,1)}), bf16[32,2,6,576]{3,1,2,0:T(2,128)(2,1)S(1)}, u32[]{:S(2)}, u32[]{:S(2)}) async-start(bf16[32,2,6,576]{3,1,2,0:T(2,128)(2,1)} %copy.72), calls=%async_computation.1 | async-start | bytes 983040 | tf_op jit(solution)/shard_map/all_to_all | solution.py:22
  39.9 5.1 %collective-permute-start.3 = (bf16[256,576]{0,1:T(8,128)(2,1)S(1)}, bf16[256,576]{0,1:T(8,128)(2,1)S(1)}, u32[]{:S(2)}, u32[]{:S(2)}) collective-permute-start(bf16[256,576]{0,1:T(8,128)(2,1)S(1)} %get-tuple-element.35), channel_id=1, source_target_pairs={{0,3},{1,0},{2,1},{3,2},{4,7},{5,4},{6,5},{7,6},{8,11},{9,8},{10,9... | collective-permute-start | bytes 884744 | tf_op jit(solution)/shard_map/ppermute | solution.py:28
  45.0 2.5 %collective-permute-start.2 = (bf16[256,576]{0,1:T(8,128)(2,1)S(1)}, bf16[256,576]{0,1:T(8,128)(2,1)S(1)}, u32[]{:S(2)}, u32[]{:S(2)}) collective-permute-start(bf16[256,576]{0,1:T(8,128)(2,1)S(1)} %get-tuple-element.36), channel_id=1, source_target_pairs={{0,2},{1,3},{2,0},{3,1},{4,6},{5,7},{6,4},{7,5},{8,10},{9,11},{10,... | collective-permute-start | bytes 884744 | tf_op jit(solution)/shard_map/ppermute | solution.py:28
  47.6 2.9 %collective-permute-start.1 = (bf16[256,576]{0,1:T(8,128)(2,1)S(1)}, bf16[256,576]{0,1:T(8,128)(2,1)S(1)}, u32[]{:S(2)}, u32[]{:S(2)}) collective-permute-start(bf16[256,576]{0,1:T(8,128)(2,1)S(1)} %get-tuple-element.37), channel_id=1, source_target_pairs={{0,1},{1,2},{2,3},{3,0},{4,5},{5,6},{6,7},{7,4},{8,9},{9,10},{10,1... | collective-permute-start | bytes 884744 | tf_op jit(solution)/shard_map/ppermute | solution.py:28
  51.5 4.2 %collective-permute-start.6 = (bf16[576,256]{1,0:T(8,128)(2,1)}, bf16[576,256]{1,0:T(8,128)(2,1)}, u32[]{:S(2)}, u32[]{:S(2)}) collective-permute-start(bf16[576,256]{1,0:T(8,128)(2,1)} %bitcast.22), channel_id=1, source_target_pairs={{0,3},{1,0},{2,1},{3,2},{4,7},{5,4},{6,5},{7,6},{8,11},{9,8},{10,9... | collective-permute-start | bytes 884744 | tf_op jit(solution)/shard_map/ppermute | solution.py:28
  55.7 3.6 %collective-permute-start.5 = (bf16[576,256]{1,0:T(8,128)(2,1)}, bf16[576,256]{1,0:T(8,128)(2,1)}, u32[]{:S(2)}, u32[]{:S(2)}) collective-permute-start(bf16[576,256]{1,0:T(8,128)(2,1)} %bitcast.20), channel_id=1, source_target_pairs={{0,2},{1,3},{2,0},{3,1},{4,6},{5,7},{6,4},{7,5},{8,10},{9,11},{10,... | collective-permute-start | bytes 884744 | tf_op jit(solution)/shard_map/ppermute | solution.py:28
  59.3 1.9 collective-permute-start.4
  61.3 3.5 %collective-permute-done.1 = bf16[256,576]{0,1:T(8,128)(2,1)S(1)} collective-permute-done((bf16[256,576]{0,1:T(8,128)(2,1)S(1)}, bf16[256,576]{0,1:T(8,128)(2,1)S(1)}, u32[]{:S(2)}, u32[]{:S(2)}) %collective-permute-start.1) | collective-permute-done | bytes 294944 | tf_op jit(solution)/shard_map/ppermute | solution.py:28
  65.6 4.8 %collective-permute-done.6 = bf16[576,256]{1,0:T(8,128)(2,1)} collective-permute-done((bf16[576,256]{1,0:T(8,128)(2,1)}, bf16[576,256]{1,0:T(8,128)(2,1)}, u32[]{:S(2)}, u32[]{:S(2)}) %collective-permute-start.6) | collective-permute-done | bytes 294944 | tf_op jit(solution)/shard_map/ppermute | solution.py:28
  71.2 4.8 %collective-permute-done.4 = bf16[576,256]{1,0:T(8,128)(2,1)} collective-permute-done((bf16[576,256]{1,0:T(8,128)(2,1)}, bf16[576,256]{1,0:T(8,128)(2,1)}, u32[]{:S(2)}, u32[]{:S(2)}) %collective-permute-start.4) | collective-permute-done | bytes 294944 | tf_op jit(solution)/shard_map/ppermute | solution.py:28
  76.0 1.4 pad_maximum_fusion.1
  77.3 1.6 gather_fusion.1
  80.8 20.7 %all-to-all-done.1 = bf16[32,2,6,576]{3,1,2,0:T(2,128)(2,1)S(1)} async-done(((bf16[32,2,6,576]{3,1,2,0:T(2,128)(2,1)}), bf16[32,2,6,576]{3,1,2,0:T(2,128)(2,1)S(1)}, u32[]{:S(2)}, u32[]{:S(2)}) %all-to-all-start.1) | async-done | bytes 442400 | tf_op jit(solution)/shard_map/all_to_all | solution.py:22
  101.9 3.1 %fusion = bf16[4,384,256]{1,2,0:T(8,128)(2,1)} fusion(bf16[4,256,576]{1,2,0:T(8,128)(2,1)} %broadcast_select_fusion.1, bf16[384,576]{1,0:T(8,128)(2,1)S(1)} %reshape.223), kind=kOutput, calls=%fused_computation.10 | convolution fusion | flops 453378048 | bytes 2408448 | tf_op jit(solution)/shard_map/sf,qhf->qsh/dot_general | solution.py:114
  105.0 4.6 %all-to-all-start.2 = ((bf16[4,384,256]{1,2,0:T(8,128)(2,1)}), bf16[4,384,256]{1,2,0:T(8,128)(2,1)S(1)}, u32[]{:S(2)}, u32[]{:S(2)}) async-start(bf16[4,384,256]{1,2,0:T(8,128)(2,1)} %fusion), calls=%async_computation.2 | async-start | bytes 1572864 | tf_op jit(solution)/shard_map/all_to_all | solution.py:117
  110.0 11.1 %all-to-all-done.2 = bf16[4,384,256]{1,2,0:T(8,128)(2,1)S(1)} async-done(((bf16[4,384,256]{1,2,0:T(8,128)(2,1)}), bf16[4,384,256]{1,2,0:T(8,128)(2,1)S(1)}, u32[]{:S(2)}, u32[]{:S(2)}) %all-to-all-start.2) | async-done | bytes 786464 | tf_op jit(solution)/shard_map/all_to_all | solution.py:117
  122.5 3.5 %all-to-all-start.3 = ((bf16[4,384,256]{2,1,0:T(8,128)(2,1)}), bf16[4,384,256]{2,1,0:T(8,128)(2,1)S(1)}, u32[]{:S(2)}, u32[]{:S(2)}) async-start(bf16[4,384,256]{2,1,0:T(8,128)(2,1)} %broadcast_in_dim.60), calls=%async_computation.3 | async-start | bytes 1572864 | tf_op jit(solution)/shard_map/all_to_all | solution.py:122
  127.4 1.7 collective-permute-done
  129.3 7.0 %all-to-all-done.3 = bf16[4,384,256]{2,1,0:T(8,128)(2,1)S(1)} async-done(((bf16[4,384,256]{2,1,0:T(8,128)(2,1)}), bf16[4,384,256]{2,1,0:T(8,128)(2,1)S(1)}, u32[]{:S(2)}, u32[]{:S(2)}) %all-to-all-start.3) | async-done | bytes 786464 | tf_op jit(solution)/shard_map/all_to_all | solution.py:122
  136.3 1.6 fusion.2
  139.4 4.1 %all_to_all.36 = bf16[32,2,6,576]{3,0,2,1:T(8,128)(2,1)S(1)} all-to-all(bf16[32,2,6,576]{3,0,2,1:T(8,128)(2,1)S(1)} %copy.80), channel_id=1, replica_groups=mesh['z'=32,'k'=2,'g'=4,'q'=4] {'k'}, dimensions={1} | all-to-all | bytes 884736 | tf_op jit(solution)/shard_map/all_to_all | solution.py:21
  144.8 4.7 %all-to-all-start.5 = ((bf16[32,2,6,576]{3,1,2,0:T(2,128)(2,1)}), bf16[32,2,6,576]{3,1,2,0:T(2,128)(2,1)S(1)}, u32[]{:S(2)}, u32[]{:S(2)}) async-start(bf16[32,2,6,576]{3,1,2,0:T(2,128)(2,1)} %copy.81), calls=%async_computation.5 | async-start | bytes 983040 | tf_op jit(solution)/shard_map/all_to_all | solution.py:22
  149.5 12.6 %all_gather.3 = bf16[128,1024]{1,0:T(8,128)(2,1)S(1)} all-gather(bf16[128,256]{1,0:T(8,128)(2,1)S(1)} %fusion.26), channel_id=1, replica_groups=mesh['z'=32,'k'=2,'g'=4,'q'=4] {'q'}, dimensions={1}, use_global_device_ids=true | all-gather | bytes 327680 | tf_op jit(solution)/shard_map/all_gather | solution.py:127
  162.1 2.4 %collective-permute-start.7 = (bf16[128,1024]{1,0:T(8,128)(2,1)S(1)}, bf16[128,1024]{1,0:T(8,128)(2,1)S(1)}, u32[]{:S(2)}, u32[]{:S(2)}) collective-permute-start(bf16[128,1024]{1,0:T(8,128)(2,1)S(1)} %all_gather.3), channel_id=1, source_target_pairs={{0,4},{4,8},{8,12},{12,0},{1,5},{5,9},{9,13},{13,1},{2,6},{6,10},{... | collective-permute-start | bytes 786440 | tf_op jit(solution)/shard_map/ppermute | solution.py:131
  164.4 4.3 %collective-permute-start.8 = (bf16[128,1024]{1,0:T(8,128)(2,1)S(1)}, bf16[128,1024]{1,0:T(8,128)(2,1)S(1)}, u32[]{:S(2)}, u32[]{:S(2)}) collective-permute-start(bf16[128,1024]{1,0:T(8,128)(2,1)S(1)} %all_gather.3), channel_id=1, source_target_pairs={{0,8},{4,12},{8,0},{12,4},{1,9},{5,13},{9,1},{13,5},{2,10},{6,14},... | collective-permute-start | bytes 786440 | tf_op jit(solution)/shard_map/ppermute | solution.py:131
  168.8 1.9 collective-permute-start.9
  171.0 40.9 %all-to-all-done.5 = bf16[32,2,6,576]{3,1,2,0:T(2,128)(2,1)S(1)} async-done(((bf16[32,2,6,576]{3,1,2,0:T(2,128)(2,1)}), bf16[32,2,6,576]{3,1,2,0:T(2,128)(2,1)S(1)}, u32[]{:S(2)}, u32[]{:S(2)}) %all-to-all-start.5) | async-done | bytes 442400 | tf_op jit(solution)/shard_map/all_to_all | solution.py:22
  213.4 4.7 %all-to-all-start.6 = ((f32[128,4,144]{0,2,1:T(8,128)}), f32[128,4,144]{0,2,1:T(8,128)S(1)}, u32[]{:S(2)}, u32[]{:S(2)}) async-start(f32[128,4,144]{0,2,1:T(8,128)} %bitcast.27), calls=%async_computation.6 | async-start | bytes 589824 | tf_op jit(solution)/shard_map/all_to_all | solution.py:143
  221.0 2.0 all-to-all-done.6
  223.0 2.5 %fusion.9 = f32[128,144]{0,1:T(8,128)} fusion(f32[128,144]{0,1:T(8,128)S(1)} %reduce_sum.54, bf16[18,4,8,1024]{3,2,1,0:T(8,128)(2,1)} %bitcast.83, bf16[4,128,1024]{2,1,0:T(8,128)(2,1)S(1)} %gather_fusion.2, pred[4]{0:T(512)(128)(4,1)S(1)} %compare_and_fusion), kind=kOutput, calls=%fused_computation.21 | convolution fusion | flops 151537664 | bytes 2375684 | tf_op jit(solution)/shard_map/gtc,fgc->tf/dot_general | solution.py:136
  (92 shorter events, 20.3 us)
Async XLA Ops:
  0.6 3.2 %copy-start = (bf16[128,2304]{1,0:T(8,128)(2,1)S(1)}, bf16[128,2304]{1,0:T(8,128)(2,1)}, u32[]{:S(2)}) copy-start(bf16[128,2304]{1,0:T(8,128)(2,1)} %param.13) | copy-start | bytes 1769476
  2.1 0.9 copy-start.11
  3.8 0.6 copy-start.4
  9.1 30.1 %copy-start.2 = (bf16[1,256,2304]{2,1,0:T(8,128)(2,1)S(1)}, bf16[1,256,2304]{2,1,0:T(8,128)(2,1)}, u32[]{:S(2)}) copy-start(bf16[1,256,2304]{2,1,0:T(8,128)(2,1)} %param.17) | copy-start | bytes 3538948
  10.4 91.1 %all-to-all-start.1 = ((bf16[32,2,6,576]{3,1,2,0:T(2,128)(2,1)}), bf16[32,2,6,576]{3,1,2,0:T(2,128)(2,1)S(1)}, u32[]{:S(2)}, u32[]{:S(2)}) async-start(bf16[32,2,6,576]{3,1,2,0:T(2,128)(2,1)} %copy.72), calls=%async_computation.1 | async-start | bytes 983040 | tf_op jit(solution)/shard_map/all_to_all | solution.py:22
  39.8 10.6 %copy-start.3 = (bf16[1,2304,256]{2,1,0:T(8,128)(2,1)S(1)}, bf16[1,2304,256]{2,1,0:T(8,128)(2,1)}, u32[]{:S(2)}) copy-start(bf16[1,2304,256]{2,1,0:T(8,128)(2,1)} %param.16) | copy-start | bytes 3538948
  39.9 19.4 %collective-permute-start.3 = (bf16[256,576]{0,1:T(8,128)(2,1)S(1)}, bf16[256,576]{0,1:T(8,128)(2,1)S(1)}, u32[]{:S(2)}, u32[]{:S(2)}) collective-permute-start(bf16[256,576]{0,1:T(8,128)(2,1)S(1)} %get-tuple-element.35), channel_id=1, source_target_pairs={{0,3},{1,0},{2,1},{3,2},{4,7},{5,4},{6,5},{7,6},{8,11},{9,8},{10,9... | collective-permute-start | bytes 884744 | tf_op jit(solution)/shard_map/ppermute | solution.py:28
  45.0 16.3 %collective-permute-start.2 = (bf16[256,576]{0,1:T(8,128)(2,1)S(1)}, bf16[256,576]{0,1:T(8,128)(2,1)S(1)}, u32[]{:S(2)}, u32[]{:S(2)}) collective-permute-start(bf16[256,576]{0,1:T(8,128)(2,1)S(1)} %get-tuple-element.36), channel_id=1, source_target_pairs={{0,2},{1,3},{2,0},{3,1},{4,6},{5,7},{6,4},{7,5},{8,10},{9,11},{10,... | collective-permute-start | bytes 884744 | tf_op jit(solution)/shard_map/ppermute | solution.py:28
  47.6 17.2 %collective-permute-start.1 = (bf16[256,576]{0,1:T(8,128)(2,1)S(1)}, bf16[256,576]{0,1:T(8,128)(2,1)S(1)}, u32[]{:S(2)}, u32[]{:S(2)}) collective-permute-start(bf16[256,576]{0,1:T(8,128)(2,1)S(1)} %get-tuple-element.37), channel_id=1, source_target_pairs={{0,1},{1,2},{2,3},{3,0},{4,5},{5,6},{6,7},{7,4},{8,9},{9,10},{10,1... | collective-permute-start | bytes 884744 | tf_op jit(solution)/shard_map/ppermute | solution.py:28
  51.5 18.8 %collective-permute-start.6 = (bf16[576,256]{1,0:T(8,128)(2,1)}, bf16[576,256]{1,0:T(8,128)(2,1)}, u32[]{:S(2)}, u32[]{:S(2)}) collective-permute-start(bf16[576,256]{1,0:T(8,128)(2,1)} %bitcast.22), channel_id=1, source_target_pairs={{0,3},{1,0},{2,1},{3,2},{4,7},{5,4},{6,5},{7,6},{8,11},{9,8},{10,9... | collective-permute-start | bytes 884744 | tf_op jit(solution)/shard_map/ppermute | solution.py:28
  55.7 15.5 %collective-permute-start.5 = (bf16[576,256]{1,0:T(8,128)(2,1)}, bf16[576,256]{1,0:T(8,128)(2,1)}, u32[]{:S(2)}, u32[]{:S(2)}) collective-permute-start(bf16[576,256]{1,0:T(8,128)(2,1)} %bitcast.20), channel_id=1, source_target_pairs={{0,2},{1,3},{2,0},{3,1},{4,6},{5,7},{6,4},{7,5},{8,10},{9,11},{10,... | collective-permute-start | bytes 884744 | tf_op jit(solution)/shard_map/ppermute | solution.py:28
  59.3 16.7 %collective-permute-start.4 = (bf16[576,256]{1,0:T(8,128)(2,1)}, bf16[576,256]{1,0:T(8,128)(2,1)}, u32[]{:S(2)}, u32[]{:S(2)}) collective-permute-start(bf16[576,256]{1,0:T(8,128)(2,1)} %bitcast.18), channel_id=1, source_target_pairs={{0,1},{1,2},{2,3},{3,0},{4,5},{5,6},{6,7},{7,4},{8,9},{9,10},{10,1... | collective-permute-start | bytes 884744 | tf_op jit(solution)/shard_map/ppermute | solution.py:28
  79.0 1.7 copy-start.1
  105.0 4.6 %copy-start.6 = (bf16[1,64,6,256]{3,1,2,0:T(8,128)(2,1)S(1)}, bf16[1,64,6,256]{3,1,2,0:T(8,128)(2,1)}, u32[]{:S(2)}) copy-start(bf16[1,64,6,256]{3,1,2,0:T(8,128)(2,1)} %param.14) | copy-start | bytes 589828
  105.0 16.1 %all-to-all-start.2 = ((bf16[4,384,256]{1,2,0:T(8,128)(2,1)}), bf16[4,384,256]{1,2,0:T(8,128)(2,1)S(1)}, u32[]{:S(2)}, u32[]{:S(2)}) async-start(bf16[4,384,256]{1,2,0:T(8,128)(2,1)} %fusion), calls=%async_computation.2 | async-start | bytes 1572864 | tf_op jit(solution)/shard_map/all_to_all | solution.py:117
  121.5 4.5 %copy-start.9 = (bf16[128,256]{1,0:T(8,128)(2,1)S(1)}, bf16[128,256]{1,0:T(8,128)(2,1)}, u32[]{:S(2)}) copy-start(bf16[128,256]{1,0:T(8,128)(2,1)} %param.19) | copy-start | bytes 196612
  121.5 4.5 %copy-start.10 = (bf16[128,256]{1,0:T(8,128)(2,1)S(1)}, bf16[128,256]{1,0:T(8,128)(2,1)}, u32[]{:S(2)}) copy-start(bf16[128,256]{1,0:T(8,128)(2,1)} %param.18) | copy-start | bytes 196612
  121.6 5.9 %copy-start.12 = (f32[4,256]{1,0:T(4,128)S(1)}, f32[4,256]{1,0:T(4,128)}, u32[]{:S(2)}) copy-start(f32[4,256]{1,0:T(4,128)} %param.20) | copy-start | bytes 12292
  122.5 13.8 %all-to-all-start.3 = ((bf16[4,384,256]{2,1,0:T(8,128)(2,1)}), bf16[4,384,256]{2,1,0:T(8,128)(2,1)S(1)}, u32[]{:S(2)}, u32[]{:S(2)}) async-start(bf16[4,384,256]{2,1,0:T(8,128)(2,1)} %broadcast_in_dim.60), calls=%async_computation.3 | async-start | bytes 1572864 | tf_op jit(solution)/shard_map/all_to_all | solution.py:122
  126.1 3.1 %collective-permute-start = (f32[3,256]{1,0:T(4,128)S(1)}, f32[3,256]{1,0:T(4,128)S(1)}, u32[]{:S(2)}, u32[]{:S(2)}) collective-permute-start(f32[3,256]{1,0:T(4,128)S(1)} %slice.48), channel_id=1, source_target_pairs={{16,0},{32,16},{48,32},{64,48},{80,64},{96,80},{112,96},{128,112},... | collective-permute-start | bytes 9224 | tf_op jit(solution)/shard_map/ppermute | solution.py:15
  144.8 67.1 %all-to-all-start.5 = ((bf16[32,2,6,576]{3,1,2,0:T(2,128)(2,1)}), bf16[32,2,6,576]{3,1,2,0:T(2,128)(2,1)S(1)}, u32[]{:S(2)}, u32[]{:S(2)}) async-start(bf16[32,2,6,576]{3,1,2,0:T(2,128)(2,1)} %copy.81), calls=%async_computation.5 | async-start | bytes 983040 | tf_op jit(solution)/shard_map/all_to_all | solution.py:22
  162.1 50.2 %collective-permute-start.7 = (bf16[128,1024]{1,0:T(8,128)(2,1)S(1)}, bf16[128,1024]{1,0:T(8,128)(2,1)S(1)}, u32[]{:S(2)}, u32[]{:S(2)}) collective-permute-start(bf16[128,1024]{1,0:T(8,128)(2,1)S(1)} %all_gather.3), channel_id=1, source_target_pairs={{0,4},{4,8},{8,12},{12,0},{1,5},{5,9},{9,13},{13,1},{2,6},{6,10},{... | collective-permute-start | bytes 786440 | tf_op jit(solution)/shard_map/ppermute | solution.py:131
  164.4 47.9 %collective-permute-start.8 = (bf16[128,1024]{1,0:T(8,128)(2,1)S(1)}, bf16[128,1024]{1,0:T(8,128)(2,1)S(1)}, u32[]{:S(2)}, u32[]{:S(2)}) collective-permute-start(bf16[128,1024]{1,0:T(8,128)(2,1)S(1)} %all_gather.3), channel_id=1, source_target_pairs={{0,8},{4,12},{8,0},{12,4},{1,9},{5,13},{9,1},{13,5},{2,10},{6,14},... | collective-permute-start | bytes 786440 | tf_op jit(solution)/shard_map/ppermute | solution.py:131
  168.8 43.6 %collective-permute-start.9 = (bf16[128,1024]{1,0:T(8,128)(2,1)S(1)}, bf16[128,1024]{1,0:T(8,128)(2,1)}, u32[]{:S(2)}, u32[]{:S(2)}) collective-permute-start(bf16[128,1024]{1,0:T(8,128)(2,1)S(1)} %all_gather.3), channel_id=1, source_target_pairs={{0,12},{4,0},{8,4},{12,8},{1,13},{5,1},{9,5},{13,9},{2,14},{6,2},{... | collective-permute-start | bytes 786440 | tf_op jit(solution)/shard_map/ppermute | solution.py:131
  171.0 41.4 %copy-start.5 = (bf16[128,384]{1,0:T(8,128)(2,1)S(1)}, bf16[128,384]{1,0:T(8,128)(2,1)}, u32[]{:S(2)}) copy-start(bf16[128,384]{1,0:T(8,128)(2,1)} %copy-done.4) | copy-start | bytes 294916
  212.0 6.2 %copy-start.7 = (bf16[1,64,6,256]{3,1,2,0:T(8,128)(2,1)S(1)}, bf16[1,64,6,256]{3,1,2,0:T(8,128)(2,1)}, u32[]{:S(2)}) copy-start(bf16[1,64,6,256]{3,1,2,0:T(8,128)(2,1)} %param.14) | copy-start | bytes 589828
  212.0 6.2 %copy-start.8 = (bf16[1,64,6,256]{3,1,2,0:T(8,128)(2,1)S(1)}, bf16[1,64,6,256]{3,1,2,0:T(8,128)(2,1)}, u32[]{:S(2)}) copy-start(bf16[1,64,6,256]{3,1,2,0:T(8,128)(2,1)} %param.15) | copy-start | bytes 589828
  213.4 9.5 %all-to-all-start.6 = ((f32[128,4,144]{0,2,1:T(8,128)}), f32[128,4,144]{0,2,1:T(8,128)S(1)}, u32[]{:S(2)}, u32[]{:S(2)}) async-start(f32[128,4,144]{0,2,1:T(8,128)} %bitcast.27), calls=%async_computation.6 | async-start | bytes 589824 | tf_op jit(solution)/shard_map/all_to_all | solution.py:143

commit v10 on v9

--- a/solution.py
+++ b/solution.py
@@ -108,7 +108,9 @@
     down_got = jnp.take(jnp.stack(down_got), by_block, axis=0)
     up_got = jnp.take(jnp.stack(up_got), by_block, axis=0)
     got_rows = across_ctx(scaled_rows)
-    down_got, up_got, got_rows = lax.optimization_barrier((down_got, up_got, got_rows))
+    key_grad, down_got, up_got, got_rows = lax.optimization_barrier(
+        (key_grad, down_got, up_got, got_rows)
+    )
     gate_pre = saved_gate.reshape(slot_count, -1).astype(jnp.float32)
     up_output = saved_up.reshape(slot_count, -1).astype(jnp.float32)
     hidden_parts = jnp.einsum(

time: 227 us -> 247 us (1.088)
  starting transfers between devices: 76.3 us -> 95 us
  blocking collectives: 20.8 us -> 33.5 us
  waiting for transfers between devices: 97.4 us -> 87 us
    all_to_all x2, starting transfers between devices: 33.4 us -> 55.6 us  [across_ctx(): lax.all_to_all(blocks, 'z', split_axis=0, concat_axis=0, tiled=True)]
    all_to_all x0 -> x1, blocking collectives: none -> 12.7 us  [local(): up_all = lax.all_to_all(up_all, 'q', 0, 0, tiled=True)]
    all_to_all x1 -> x0, waiting for transfers between devices: 7.03 us -> none  [local(): up_all = lax.all_to_all(up_all, 'q', 0, 0, tiled=True)]
    ppermute x6, waiting for transfers between devices: 13.9 us -> 8.75 us  [around(): lax.ppermute(value, 'q', [(source, (source + steps) % count) for source i...]
    all_to_all x2, waiting for transfers between devices: 61.5 us -> 65.1 us  [across_ctx(): lax.all_to_all(blocks, 'z', split_axis=0, concat_axis=0, tiled=True)]
    all_to_all x1 -> x0, starting transfers between devices: 3.49 us -> none  [local(): up_all = lax.all_to_all(up_all, 'q', 0, 0, tiled=True)]
  transfers between devices with their start and end apart: 15 -> 14, of which waited for: 10 -> 7; matrix products, arithmetic and copies ran while one was open for 5% -> 4% of each run, Pallas kernels for 0% -> 0%
where the time goes in v10:
time: 247 us; the launch traced here: 246 us
  starting transfers between devices  95 us (38%)
  waiting for transfers between devices  87 us (35%)
  blocking collectives  33.5 us (14%)
  local copies, waits for them, and re-layouts  13.8 us (6%)
  matrix products  8.69 us (4%)
  other arithmetic  6.31 us (3%)
    all_to_all x2, waiting for transfers between devices, across_ctx(): lax.all_to_all(blocks, 'z', split_axis=0, concat_axis=0, tiled=True)  65.1 us
    all_to_all x2, starting transfers between devices, across_ctx(): lax.all_to_all(blocks, 'z', split_axis=0, concat_axis=0, tiled=True)  55.6 us
    ppermute x6, starting transfers between devices, around(): lax.ppermute(value, 'q', [(source, (source + steps) % count) for source i...  20.2 us
    all_to_all x1, blocking collectives, local(): up_all = lax.all_to_all(up_all, 'q', 0, 0, tiled=True)  12.7 us
    all_gather x1, blocking collectives, local(): key_group = lax.all_gather(key_grad, 'q', axis=1, tiled=True)  12.5 us
    all_to_all x1, waiting for transfers between devices, local(): hidden_parts = lax.all_to_all(hidden_parts, 'q', 0, 0, tiled=True)  11.1 us
    ppermute x6, waiting for transfers between devices, around(): lax.ppermute(value, 'q', [(source, (source + steps) % count) for source i...  8.75 us
    ppermute x3, starting transfers between devices, local(): lax.ppermute(key_group, 'g', [(i, (i + shift) % groups) for i in range(gr...  8.62 us
  transfers between devices with their start and end apart: 14, of which 7 were waited for; matrix products, arithmetic and copies ran while one was open for 4% of the time, Pallas kernels for 0%

profile of v10, /device:TPU:6, one launch (start us, length us, event | category | flops | bytes accessed | tf_op | source)
XLA Modules:
  0.0 245.6 jit_solution(936539595216966985)
XLA Ops:
  5.0 4.1 %all_to_all.35 = bf16[32,2,6,576]{3,0,2,1:T(8,128)(2,1)S(1)} all-to-all(bf16[32,2,6,576]{3,0,2,1:T(8,128)(2,1)S(1)} %copy.71), channel_id=1, replica_groups=mesh['z'=32,'k'=2,'g'=4,'q'=4] {'k'}, dimensions={1} | all-to-all | bytes 884736 | tf_op jit(solution)/shard_map/all_to_all | solution.py:21
  9.1 1.3 copy.72
  10.4 28.7 %all-to-all-start.1 = ((bf16[32,2,6,576]{3,1,2,0:T(2,128)(2,1)}), bf16[32,2,6,576]{3,1,2,0:T(2,128)(2,1)S(1)}, u32[]{:S(2)}, u32[]{:S(2)}) async-start(bf16[32,2,6,576]{3,1,2,0:T(2,128)(2,1)} %copy.72), calls=%async_computation.1 | async-start | bytes 983040 | tf_op jit(solution)/shard_map/all_to_all | solution.py:22
  39.3 1.3 collective-permute-start
  41.4 5.1 %collective-permute-start.3 = (bf16[256,576]{0,1:T(8,128)(2,1)S(1)}, bf16[256,576]{0,1:T(8,128)(2,1)S(1)}, u32[]{:S(2)}, u32[]{:S(2)}) collective-permute-start(bf16[256,576]{0,1:T(8,128)(2,1)S(1)} %get-tuple-element.37), channel_id=1, source_target_pairs={{0,3},{1,0},{2,1},{3,2},{4,7},{5,4},{6,5},{7,6},{8,11},{9,8},{10,9... | collective-permute-start | bytes 884744 | tf_op jit(solution)/shard_map/ppermute | solution.py:28
  46.4 2.5 %collective-permute-start.2 = (bf16[256,576]{0,1:T(8,128)(2,1)S(1)}, bf16[256,576]{0,1:T(8,128)(2,1)S(1)}, u32[]{:S(2)}, u32[]{:S(2)}) collective-permute-start(bf16[256,576]{0,1:T(8,128)(2,1)S(1)} %get-tuple-element.38), channel_id=1, source_target_pairs={{0,2},{1,3},{2,0},{3,1},{4,6},{5,7},{6,4},{7,5},{8,10},{9,11},{10,... | collective-permute-start | bytes 884744 | tf_op jit(solution)/shard_map/ppermute | solution.py:28
  49.0 2.9 %collective-permute-start.1 = (bf16[256,576]{0,1:T(8,128)(2,1)S(1)}, bf16[256,576]{0,1:T(8,128)(2,1)S(1)}, u32[]{:S(2)}, u32[]{:S(2)}) collective-permute-start(bf16[256,576]{0,1:T(8,128)(2,1)S(1)} %get-tuple-element.39), channel_id=1, source_target_pairs={{0,1},{1,2},{2,3},{3,0},{4,5},{5,6},{6,7},{7,4},{8,9},{9,10},{10,1... | collective-permute-start | bytes 884744 | tf_op jit(solution)/shard_map/ppermute | solution.py:28
  53.0 4.2 %collective-permute-start.6 = (bf16[576,256]{1,0:T(8,128)(2,1)}, bf16[576,256]{1,0:T(8,128)(2,1)}, u32[]{:S(2)}, u32[]{:S(2)}) collective-permute-start(bf16[576,256]{1,0:T(8,128)(2,1)} %bitcast.22), channel_id=1, source_target_pairs={{0,3},{1,0},{2,1},{3,2},{4,7},{5,4},{6,5},{7,6},{8,11},{9,8},{10,9... | collective-permute-start | bytes 884744 | tf_op jit(solution)/shard_map/ppermute | solution.py:28
  57.2 3.6 %collective-permute-start.5 = (bf16[576,256]{1,0:T(8,128)(2,1)}, bf16[576,256]{1,0:T(8,128)(2,1)}, u32[]{:S(2)}, u32[]{:S(2)}) collective-permute-start(bf16[576,256]{1,0:T(8,128)(2,1)} %bitcast.20), channel_id=1, source_target_pairs={{0,2},{1,3},{2,0},{3,1},{4,6},{5,7},{6,4},{7,5},{8,10},{9,11},{10,... | collective-permute-start | bytes 884744 | tf_op jit(solution)/shard_map/ppermute | solution.py:28
  60.8 1.9 collective-permute-start.4
  62.9 3.1 %collective-permute-done.1 = bf16[256,576]{0,1:T(8,128)(2,1)S(1)} collective-permute-done((bf16[256,576]{0,1:T(8,128)(2,1)S(1)}, bf16[256,576]{0,1:T(8,128)(2,1)S(1)}, u32[]{:S(2)}, u32[]{:S(2)}) %collective-permute-start.1) | collective-permute-done | bytes 294944 | tf_op jit(solution)/shard_map/ppermute | solution.py:28
  66.7 2.7 %collective-permute-done.6 = bf16[576,256]{1,0:T(8,128)(2,1)} collective-permute-done((bf16[576,256]{1,0:T(8,128)(2,1)}, bf16[576,256]{1,0:T(8,128)(2,1)}, u32[]{:S(2)}, u32[]{:S(2)}) %collective-permute-start.6) | collective-permute-done | bytes 294944 | tf_op jit(solution)/shard_map/ppermute | solution.py:28
  69.4 3.0 %collective-permute-done.4 = bf16[576,256]{1,0:T(8,128)(2,1)} collective-permute-done((bf16[576,256]{1,0:T(8,128)(2,1)}, bf16[576,256]{1,0:T(8,128)(2,1)}, u32[]{:S(2)}, u32[]{:S(2)}) %collective-permute-start.4) | collective-permute-done | bytes 294944 | tf_op jit(solution)/shard_map/ppermute | solution.py:28
  72.4 1.4 pad_maximum_fusion.1
  73.8 1.6 gather_fusion.1
  77.3 24.2 %all-to-all-done.1 = bf16[32,2,6,576]{3,1,2,0:T(2,128)(2,1)S(1)} async-done(((bf16[32,2,6,576]{3,1,2,0:T(2,128)(2,1)}), bf16[32,2,6,576]{3,1,2,0:T(2,128)(2,1)S(1)}, u32[]{:S(2)}, u32[]{:S(2)}) %all-to-all-start.1) | async-done | bytes 442400 | tf_op jit(solution)/shard_map/all_to_all | solution.py:22
  101.9 3.1 %fusion = bf16[4,384,256]{1,2,0:T(8,128)(2,1)} fusion(bf16[4,256,576]{1,2,0:T(8,128)(2,1)} %broadcast_select_fusion.1, bf16[384,576]{1,0:T(8,128)(2,1)S(1)} %reshape.223), kind=kOutput, calls=%fused_computation.10 | convolution fusion | flops 453378048 | bytes 2408448 | tf_op jit(solution)/shard_map/sf,qhf->qsh/dot_general | solution.py:116
  105.1 4.6 %all-to-all-start.2 = ((bf16[4,384,256]{1,2,0:T(8,128)(2,1)}), bf16[4,384,256]{1,2,0:T(8,128)(2,1)S(1)}, u32[]{:S(2)}, u32[]{:S(2)}) async-start(bf16[4,384,256]{1,2,0:T(8,128)(2,1)} %fusion), calls=%async_computation.2 | async-start | bytes 1572864 | tf_op jit(solution)/shard_map/all_to_all | solution.py:119
  110.0 11.1 %all-to-all-done.2 = bf16[4,384,256]{1,2,0:T(8,128)(2,1)S(1)} async-done(((bf16[4,384,256]{1,2,0:T(8,128)(2,1)}), bf16[4,384,256]{1,2,0:T(8,128)(2,1)S(1)}, u32[]{:S(2)}, u32[]{:S(2)}) %all-to-all-start.2) | async-done | bytes 786464 | tf_op jit(solution)/shard_map/all_to_all | solution.py:119
  121.6 12.7 %all_to_all.36 = bf16[4,384,256]{2,1,0:T(8,128)(2,1)S(1)} all-to-all(bf16[4,384,256]{2,1,0:T(8,128)(2,1)S(1)} %broadcast_in_dim.60), channel_id=1, replica_groups=mesh['z'=32,'k'=2,'g'=4,'q'=4] {'q'}, dimensions={0} | all-to-all | bytes 1572864 | tf_op jit(solution)/shard_map/all_to_all | solution.py:124
  134.3 1.6 fusion.2
  137.4 4.1 %all_to_all.37 = bf16[32,2,6,576]{3,0,2,1:T(8,128)(2,1)S(1)} all-to-all(bf16[32,2,6,576]{3,0,2,1:T(8,128)(2,1)S(1)} %copy.80), channel_id=1, replica_groups=mesh['z'=32,'k'=2,'g'=4,'q'=4] {'k'}, dimensions={1} | all-to-all | bytes 884736 | tf_op jit(solution)/shard_map/all_to_all | solution.py:21
  141.5 1.3 copy.81
  142.8 26.9 %all-to-all-start.5 = ((bf16[32,2,6,576]{3,1,2,0:T(2,128)(2,1)}), bf16[32,2,6,576]{3,1,2,0:T(2,128)(2,1)S(1)}, u32[]{:S(2)}, u32[]{:S(2)}) async-start(bf16[32,2,6,576]{3,1,2,0:T(2,128)(2,1)} %copy.81), calls=%async_computation.5 | async-start | bytes 983040 | tf_op jit(solution)/shard_map/all_to_all | solution.py:22
  169.7 12.5 %all_gather.3 = bf16[128,1024]{1,0:T(8,128)(2,1)S(1)} all-gather(bf16[128,256]{1,0:T(8,128)(2,1)S(1)} %fusion.26), channel_id=1, replica_groups=mesh['z'=32,'k'=2,'g'=4,'q'=4] {'q'}, dimensions={1}, use_global_device_ids=true | all-gather | bytes 327680 | tf_op jit(solution)/shard_map/all_gather | solution.py:129
  182.2 2.4 collective-permute-start.7
  184.6 4.3 %collective-permute-start.8 = (bf16[128,1024]{1,0:T(8,128)(2,1)S(1)}, bf16[128,1024]{1,0:T(8,128)(2,1)S(1)}, u32[]{:S(2)}, u32[]{:S(2)}) collective-permute-start(bf16[128,1024]{1,0:T(8,128)(2,1)S(1)} %all_gather.3), channel_id=1, source_target_pairs={{0,8},{4,12},{8,0},{12,4},{1,9},{5,13},{9,1},{13,5},{2,10},{6,14},... | collective-permute-start | bytes 786440 | tf_op jit(solution)/shard_map/ppermute | solution.py:133
  189.0 1.9 collective-permute-start.9
  191.2 40.9 %all-to-all-done.5 = bf16[32,2,6,576]{3,1,2,0:T(2,128)(2,1)S(1)} async-done(((bf16[32,2,6,576]{3,1,2,0:T(2,128)(2,1)}), bf16[32,2,6,576]{3,1,2,0:T(2,128)(2,1)S(1)}, u32[]{:S(2)}, u32[]{:S(2)}) %all-to-all-start.5) | async-done | bytes 442400 | tf_op jit(solution)/shard_map/all_to_all | solution.py:22
  233.6 4.8 %all-to-all-start.6 = ((f32[128,4,144]{0,2,1:T(8,128)}), f32[128,4,144]{0,2,1:T(8,128)S(1)}, u32[]{:S(2)}, u32[]{:S(2)}) async-start(f32[128,4,144]{0,2,1:T(8,128)} %bitcast.27), calls=%async_computation.6 | async-start | bytes 589824 | tf_op jit(solution)/shard_map/all_to_all | solution.py:145
  241.1 2.0 all-to-all-done.6
  243.2 2.5 fusion.9
  (95 shorter events, 16.0 us)
Async XLA Ops:
  0.6 3.2 %copy-start = (bf16[128,2304]{1,0:T(8,128)(2,1)S(1)}, bf16[128,2304]{1,0:T(8,128)(2,1)}, u32[]{:S(2)}) copy-start(bf16[128,2304]{1,0:T(8,128)(2,1)} %param.13) | copy-start | bytes 1769476
  2.1 0.9 copy-start.13
  3.8 0.6 copy-start.4
  9.1 30.0 %copy-start.11 = (bf16[128,256]{1,0:T(8,128)(2,1)S(1)}, bf16[128,256]{1,0:T(8,128)(2,1)}, u32[]{:S(2)}) copy-start(bf16[128,256]{1,0:T(8,128)(2,1)} %param.19) | copy-start | bytes 196612
  9.1 30.1 %copy-start.12 = (bf16[128,256]{1,0:T(8,128)(2,1)S(1)}, bf16[128,256]{1,0:T(8,128)(2,1)}, u32[]{:S(2)}) copy-start(bf16[128,256]{1,0:T(8,128)(2,1)} %param.18) | copy-start | bytes 196612
  9.1 31.5 %copy-start.2 = (bf16[1,256,2304]{2,1,0:T(8,128)(2,1)S(1)}, bf16[1,256,2304]{2,1,0:T(8,128)(2,1)}, u32[]{:S(2)}) copy-start(bf16[1,256,2304]{2,1,0:T(8,128)(2,1)} %param.17) | copy-start | bytes 3538948
  10.4 91.1 %all-to-all-start.1 = ((bf16[32,2,6,576]{3,1,2,0:T(2,128)(2,1)}), bf16[32,2,6,576]{3,1,2,0:T(2,128)(2,1)S(1)}, u32[]{:S(2)}, u32[]{:S(2)}) async-start(bf16[32,2,6,576]{3,1,2,0:T(2,128)(2,1)} %copy.72), calls=%async_computation.1 | async-start | bytes 983040 | tf_op jit(solution)/shard_map/all_to_all | solution.py:22
  39.2 1.4 copy-start.8
  39.3 17.9 %collective-permute-start = (f32[3,256]{1,0:T(4,128)S(1)}, f32[3,256]{1,0:T(4,128)S(1)}, u32[]{:S(2)}, u32[]{:S(2)}) collective-permute-start(f32[3,256]{1,0:T(4,128)S(1)} %slice.48), channel_id=1, source_target_pairs={{16,0},{32,16},{48,32},{64,48},{80,64},{96,80},{112,96},{128,112},... | collective-permute-start | bytes 9224 | tf_op jit(solution)/shard_map/ppermute | solution.py:15
  41.3 10.6 %copy-start.3 = (bf16[1,2304,256]{2,1,0:T(8,128)(2,1)S(1)}, bf16[1,2304,256]{2,1,0:T(8,128)(2,1)}, u32[]{:S(2)}) copy-start(bf16[1,2304,256]{2,1,0:T(8,128)(2,1)} %param.16) | copy-start | bytes 3538948
  41.4 19.4 %collective-permute-start.3 = (bf16[256,576]{0,1:T(8,128)(2,1)S(1)}, bf16[256,576]{0,1:T(8,128)(2,1)S(1)}, u32[]{:S(2)}, u32[]{:S(2)}) collective-permute-start(bf16[256,576]{0,1:T(8,128)(2,1)S(1)} %get-tuple-element.37), channel_id=1, source_target_pairs={{0,3},{1,0},{2,1},{3,2},{4,7},{5,4},{6,5},{7,6},{8,11},{9,8},{10,9... | collective-permute-start | bytes 884744 | tf_op jit(solution)/shard_map/ppermute | solution.py:28
  46.4 16.4 %collective-permute-start.2 = (bf16[256,576]{0,1:T(8,128)(2,1)S(1)}, bf16[256,576]{0,1:T(8,128)(2,1)S(1)}, u32[]{:S(2)}, u32[]{:S(2)}) collective-permute-start(bf16[256,576]{0,1:T(8,128)(2,1)S(1)} %get-tuple-element.38), channel_id=1, source_target_pairs={{0,2},{1,3},{2,0},{3,1},{4,6},{5,7},{6,4},{7,5},{8,10},{9,11},{10,... | collective-permute-start | bytes 884744 | tf_op jit(solution)/shard_map/ppermute | solution.py:28
  49.0 16.9 %collective-permute-start.1 = (bf16[256,576]{0,1:T(8,128)(2,1)S(1)}, bf16[256,576]{0,1:T(8,128)(2,1)S(1)}, u32[]{:S(2)}, u32[]{:S(2)}) collective-permute-start(bf16[256,576]{0,1:T(8,128)(2,1)S(1)} %get-tuple-element.39), channel_id=1, source_target_pairs={{0,1},{1,2},{2,3},{3,0},{4,5},{5,6},{6,7},{7,4},{8,9},{9,10},{10,1... | collective-permute-start | bytes 884744 | tf_op jit(solution)/shard_map/ppermute | solution.py:28
  51.9 5.3 %copy-start.14 = (f32[4,256]{1,0:T(4,128)S(1)}, f32[4,256]{1,0:T(4,128)}, u32[]{:S(2)}) copy-start(f32[4,256]{1,0:T(4,128)} %param.20) | copy-start | bytes 12292
  51.9 10.9 %copy-start.9 = (f32[128,256]{1,0:T(8,128)S(1)}, f32[128,256]{1,0:T(8,128)}, u32[]{:S(2)}) copy-start(f32[128,256]{1,0:T(8,128)} %copy-done.8) | copy-start | bytes 393220
  53.0 16.5 %collective-permute-start.6 = (bf16[576,256]{1,0:T(8,128)(2,1)}, bf16[576,256]{1,0:T(8,128)(2,1)}, u32[]{:S(2)}, u32[]{:S(2)}) collective-permute-start(bf16[576,256]{1,0:T(8,128)(2,1)} %bitcast.22), channel_id=1, source_target_pairs={{0,3},{1,0},{2,1},{3,2},{4,7},{5,4},{6,5},{7,6},{8,11},{9,8},{10,9... | collective-permute-start | bytes 884744 | tf_op jit(solution)/shard_map/ppermute | solution.py:28
  57.2 12.2 %collective-permute-start.5 = (bf16[576,256]{1,0:T(8,128)(2,1)}, bf16[576,256]{1,0:T(8,128)(2,1)}, u32[]{:S(2)}, u32[]{:S(2)}) collective-permute-start(bf16[576,256]{1,0:T(8,128)(2,1)} %bitcast.20), channel_id=1, source_target_pairs={{0,2},{1,3},{2,0},{3,1},{4,6},{5,7},{6,4},{7,5},{8,10},{9,11},{10,... | collective-permute-start | bytes 884744 | tf_op jit(solution)/shard_map/ppermute | solution.py:28
  60.8 11.6 %collective-permute-start.4 = (bf16[576,256]{1,0:T(8,128)(2,1)}, bf16[576,256]{1,0:T(8,128)(2,1)}, u32[]{:S(2)}, u32[]{:S(2)}) collective-permute-start(bf16[576,256]{1,0:T(8,128)(2,1)} %bitcast.18), channel_id=1, source_target_pairs={{0,1},{1,2},{2,3},{3,0},{4,5},{5,6},{6,7},{7,4},{8,9},{9,10},{10,1... | collective-permute-start | bytes 884744 | tf_op jit(solution)/shard_map/ppermute | solution.py:28
  75.4 1.7 copy-start.1
  105.0 4.6 %copy-start.6 = (bf16[1,64,6,256]{3,1,2,0:T(8,128)(2,1)S(1)}, bf16[1,64,6,256]{3,1,2,0:T(8,128)(2,1)}, u32[]{:S(2)}) copy-start(bf16[1,64,6,256]{3,1,2,0:T(8,128)(2,1)} %param.14) | copy-start | bytes 589828
  105.1 16.1 %all-to-all-start.2 = ((bf16[4,384,256]{1,2,0:T(8,128)(2,1)}), bf16[4,384,256]{1,2,0:T(8,128)(2,1)S(1)}, u32[]{:S(2)}, u32[]{:S(2)}) async-start(bf16[4,384,256]{1,2,0:T(8,128)(2,1)} %fusion), calls=%async_computation.2 | async-start | bytes 1572864 | tf_op jit(solution)/shard_map/all_to_all | solution.py:119
  142.8 89.2 %all-to-all-start.5 = ((bf16[32,2,6,576]{3,1,2,0:T(2,128)(2,1)}), bf16[32,2,6,576]{3,1,2,0:T(2,128)(2,1)S(1)}, u32[]{:S(2)}, u32[]{:S(2)}) async-start(bf16[32,2,6,576]{3,1,2,0:T(2,128)(2,1)} %copy.81), calls=%async_computation.5 | async-start | bytes 983040 | tf_op jit(solution)/shard_map/all_to_all | solution.py:22
  182.2 50.2 %collective-permute-start.7 = (bf16[128,1024]{1,0:T(8,128)(2,1)S(1)}, bf16[128,1024]{1,0:T(8,128)(2,1)S(1)}, u32[]{:S(2)}, u32[]{:S(2)}) collective-permute-start(bf16[128,1024]{1,0:T(8,128)(2,1)S(1)} %all_gather.3), channel_id=1, source_target_pairs={{0,4},{4,8},{8,12},{12,0},{1,5},{5,9},{9,13},{13,1},{2,6},{6,10},{... | collective-permute-start | bytes 786440 | tf_op jit(solution)/shard_map/ppermute | solution.py:133
  184.6 47.9 %collective-permute-start.8 = (bf16[128,1024]{1,0:T(8,128)(2,1)S(1)}, bf16[128,1024]{1,0:T(8,128)(2,1)S(1)}, u32[]{:S(2)}, u32[]{:S(2)}) collective-permute-start(bf16[128,1024]{1,0:T(8,128)(2,1)S(1)} %all_gather.3), channel_id=1, source_target_pairs={{0,8},{4,12},{8,0},{12,4},{1,9},{5,13},{9,1},{13,5},{2,10},{6,14},... | collective-permute-start | bytes 786440 | tf_op jit(solution)/shard_map/ppermute | solution.py:133
  189.0 43.5 %collective-permute-start.9 = (bf16[128,1024]{1,0:T(8,128)(2,1)S(1)}, bf16[128,1024]{1,0:T(8,128)(2,1)}, u32[]{:S(2)}, u32[]{:S(2)}) collective-permute-start(bf16[128,1024]{1,0:T(8,128)(2,1)S(1)} %all_gather.3), channel_id=1, source_target_pairs={{0,12},{4,0},{8,4},{12,8},{1,13},{5,1},{9,5},{13,9},{2,14},{6,2},{... | collective-permute-start | bytes 786440 | tf_op jit(solution)/shard_map/ppermute | solution.py:133
  191.2 41.3 %copy-start.5 = (bf16[128,384]{1,0:T(8,128)(2,1)S(1)}, bf16[128,384]{1,0:T(8,128)(2,1)}, u32[]{:S(2)}) copy-start(bf16[128,384]{1,0:T(8,128)(2,1)} %copy-done.4) | copy-start | bytes 294916
  232.2 6.2 %copy-start.7 = (bf16[1,64,6,256]{3,1,2,0:T(8,128)(2,1)S(1)}, bf16[1,64,6,256]{3,1,2,0:T(8,128)(2,1)}, u32[]{:S(2)}) copy-start(bf16[1,64,6,256]{3,1,2,0:T(8,128)(2,1)} %param.14) | copy-start | bytes 589828
  232.2 6.2 %copy-start.10 = (bf16[1,64,6,256]{3,1,2,0:T(8,128)(2,1)S(1)}, bf16[1,64,6,256]{3,1,2,0:T(8,128)(2,1)}, u32[]{:S(2)}) copy-start(bf16[1,64,6,256]{3,1,2,0:T(8,128)(2,1)} %param.15) | copy-start | bytes 589828
  233.6 9.5 %all-to-all-start.6 = ((f32[128,4,144]{0,2,1:T(8,128)}), f32[128,4,144]{0,2,1:T(8,128)S(1)}, u32[]{:S(2)}, u32[]{:S(2)}) async-start(f32[128,4,144]{0,2,1:T(8,128)} %bitcast.27), calls=%async_computation.6 | async-start | bytes 589824 | tf_op jit(solution)/shard_map/all_to_all | solution.py:145

commit v11 on v9

--- a/solution.py
+++ b/solution.py
@@ -140,8 +140,9 @@
         preferred_element_type=jnp.float32,
     )
     token_rows = jnp.dot(placement, came_back, preferred_element_type=jnp.float32)
-    token_rows = lax.all_to_all(token_rows.reshape(tok_rows, groups, -1), "g", 1, 1, tiled=True)
-    moe_share = jnp.sum(token_rows, 1)
+    token_rows = token_rows.astype(jnp.bfloat16).reshape(tok_rows, groups, -1)
+    token_rows = lax.all_to_all(token_rows, "g", 1, 1, tiled=True)
+    moe_share = jnp.sum(token_rows.astype(jnp.float32), 1)
     input_grad = moe_share + key_input
     return (input_grad, gate_grad.reshape(saved_gate.shape))
 

time: 227 us -> 227 us (level)
  waiting for transfers between devices: 97.4 us -> 91.5 us
  other arithmetic: 6.31 us -> 9.45 us
    ppermute x6, waiting for transfers between devices: 13.9 us -> 8.24 us  [around(): lax.ppermute(value, 'q', [(source, (source + steps) % count) for source i...]
  transfers between devices with their start and end apart: 15 -> 15, of which waited for: 10 -> 8; matrix products, arithmetic and copies ran while one was open for 5% -> 7% of each run, Pallas kernels for 0% -> 0%
where the time goes in v11:
time: 227 us; the launch traced here: 225 us
  waiting for transfers between devices  91.5 us (40%)
  starting transfers between devices  76.9 us (34%)
  blocking collectives  20.9 us (9%)
  local copies, waits for them, and re-layouts  16.5 us (7%)
  other arithmetic  9.45 us (4%)
  matrix products  8.66 us (4%)
    all_to_all x2, waiting for transfers between devices, across_ctx(): lax.all_to_all(blocks, 'z', split_axis=0, concat_axis=0, tiled=True)  61 us
    all_to_all x2, starting transfers between devices, across_ctx(): lax.all_to_all(blocks, 'z', split_axis=0, concat_axis=0, tiled=True)  33.5 us
    ppermute x6, starting transfers between devices, around(): lax.ppermute(value, 'q', [(source, (source + steps) % count) for source i...  20.6 us
    all_gather x1, blocking collectives, local(): key_group = lax.all_gather(key_grad, 'q', axis=1, tiled=True)  12.7 us
    all_to_all x1, waiting for transfers between devices, local(): hidden_parts = lax.all_to_all(hidden_parts, 'q', 0, 0, tiled=True)  11.1 us
    ppermute x3, starting transfers between devices, local(): lax.ppermute(key_group, 'g', [(i, (i + shift) % groups) for i in range(gr...  8.62 us
    ppermute x6, waiting for transfers between devices, around(): lax.ppermute(value, 'q', [(source, (source + steps) % count) for source i...  8.24 us
    all_to_all x2, blocking collectives, across_ctx(): lax.all_to_all(blocks, 'k', split_axis=1, concat_axis=1, tiled=True)  8.22 us
  transfers between devices with their start and end apart: 15, of which 8 were waited for; matrix products, arithmetic and copies ran while one was open for 7% of the time, Pallas kernels for 0%

profile of v11, /device:TPU:6, one launch (start us, length us, event | category | flops | bytes accessed | tf_op | source)
XLA Modules:
  0.0 225.1 jit_solution(172141110535210686)
XLA Ops:
  5.4 4.1 %all_to_all.35 = bf16[32,2,6,576]{3,0,2,1:T(8,128)(2,1)S(1)} all-to-all(bf16[32,2,6,576]{3,0,2,1:T(8,128)(2,1)S(1)} %copy.71), channel_id=1, replica_groups=mesh['z'=32,'k'=2,'g'=4,'q'=4] {'k'}, dimensions={1} | all-to-all | bytes 884736 | tf_op jit(solution)/shard_map/all_to_all | solution.py:21
  10.9 28.7 %all-to-all-start.1 = ((bf16[32,2,6,576]{3,1,2,0:T(2,128)(2,1)}), bf16[32,2,6,576]{3,1,2,0:T(2,128)(2,1)S(1)}, u32[]{:S(2)}, u32[]{:S(2)}) async-start(bf16[32,2,6,576]{3,1,2,0:T(2,128)(2,1)} %copy.72), calls=%async_computation.1 | async-start | bytes 983040 | tf_op jit(solution)/shard_map/all_to_all | solution.py:22
  40.6 3.5 %collective-permute-start.4 = (bf16[576,256]{1,0:T(8,128)(2,1)}, bf16[576,256]{1,0:T(8,128)(2,1)S(1)}, u32[]{:S(2)}, u32[]{:S(2)}) collective-permute-start(bf16[576,256]{1,0:T(8,128)(2,1)} %bitcast.18), channel_id=1, source_target_pairs={{0,1},{1,2},{2,3},{3,0},{4,5},{5,6},{6,7},{7,4},{8,9},{9,10},{10,1... | collective-permute-start | bytes 884744 | tf_op jit(solution)/shard_map/ppermute | solution.py:28
  44.1 4.8 %collective-permute-start.5 = (bf16[576,256]{1,0:T(8,128)(2,1)}, bf16[576,256]{1,0:T(8,128)(2,1)S(1)}, u32[]{:S(2)}, u32[]{:S(2)}) collective-permute-start(bf16[576,256]{1,0:T(8,128)(2,1)} %bitcast.20), channel_id=1, source_target_pairs={{0,2},{1,3},{2,0},{3,1},{4,6},{5,7},{6,4},{7,5},{8,10},{9,11},{10,... | collective-permute-start | bytes 884744 | tf_op jit(solution)/shard_map/ppermute | solution.py:28
  48.9 3.3 %collective-permute-start.6 = (bf16[576,256]{1,0:T(8,128)(2,1)}, bf16[576,256]{1,0:T(8,128)(2,1)}, u32[]{:S(2)}, u32[]{:S(2)}) collective-permute-start(bf16[576,256]{1,0:T(8,128)(2,1)} %bitcast.22), channel_id=1, source_target_pairs={{0,3},{1,0},{2,1},{3,2},{4,7},{5,4},{6,5},{7,6},{8,11},{9,8},{10,9... | collective-permute-start | bytes 884744 | tf_op jit(solution)/shard_map/ppermute | solution.py:28
  52.2 1.6 copy.68
  54.8 2.6 %collective-permute-start.1 = (bf16[256,576]{0,1:T(8,128)(2,1)}, bf16[256,576]{0,1:T(8,128)(2,1)S(1)}, u32[]{:S(2)}, u32[]{:S(2)}) collective-permute-start(bf16[256,576]{0,1:T(8,128)(2,1)} %get-tuple-element.37), channel_id=1, source_target_pairs={{0,1},{1,2},{2,3},{3,0},{4,5},{5,6},{6,7},{7,4},{8,9},{9,10},{10,1... | collective-permute-start | bytes 884744 | tf_op jit(solution)/shard_map/ppermute | solution.py:28
  57.4 2.7 %collective-permute-start.2 = (bf16[256,576]{0,1:T(8,128)(2,1)}, bf16[256,576]{0,1:T(8,128)(2,1)}, u32[]{:S(2)}, u32[]{:S(2)}) collective-permute-start(bf16[256,576]{0,1:T(8,128)(2,1)} %get-tuple-element.36), channel_id=1, source_target_pairs={{0,2},{1,3},{2,0},{3,1},{4,6},{5,7},{6,4},{7,5},{8,10},{9,11},{10,... | collective-permute-start | bytes 884744 | tf_op jit(solution)/shard_map/ppermute | solution.py:28
  60.1 3.8 %collective-permute-start.3 = (bf16[256,576]{0,1:T(8,128)(2,1)}, bf16[256,576]{0,1:T(8,128)(2,1)}, u32[]{:S(2)}, u32[]{:S(2)}) collective-permute-start(bf16[256,576]{0,1:T(8,128)(2,1)} %get-tuple-element.35), channel_id=1, source_target_pairs={{0,3},{1,0},{2,1},{3,2},{4,7},{5,4},{6,5},{7,6},{8,11},{9,8},{10,9... | collective-permute-start | bytes 884744 | tf_op jit(solution)/shard_map/ppermute | solution.py:28
  65.1 1.7 gather_fusion.1
  66.8 6.4 %collective-permute-done.1 = bf16[256,576]{0,1:T(8,128)(2,1)S(1)} collective-permute-done((bf16[256,576]{0,1:T(8,128)(2,1)}, bf16[256,576]{0,1:T(8,128)(2,1)S(1)}, u32[]{:S(2)}, u32[]{:S(2)}) %collective-permute-start.1) | collective-permute-done | bytes 294944 | tf_op jit(solution)/shard_map/ppermute | solution.py:28
  73.2 1.8 collective-permute-done.3
  75.0 1.4 pad_maximum_fusion
  77.0 1.4 broadcast_select_fusion
  79.7 22.3 %all-to-all-done.1 = bf16[32,2,6,576]{3,1,2,0:T(2,128)(2,1)S(1)} async-done(((bf16[32,2,6,576]{3,1,2,0:T(2,128)(2,1)}), bf16[32,2,6,576]{3,1,2,0:T(2,128)(2,1)S(1)}, u32[]{:S(2)}, u32[]{:S(2)}) %all-to-all-start.1) | async-done | bytes 442400 | tf_op jit(solution)/shard_map/all_to_all | solution.py:22
  102.4 3.2 %fusion = bf16[4,384,256]{1,2,0:T(8,128)(2,1)} fusion(bf16[4,256,576]{1,2,0:T(8,128)(2,1)} %broadcast_select_fusion.1, bf16[384,576]{1,0:T(8,128)(2,1)S(1)} %reshape.223), kind=kOutput, calls=%fused_computation.10 | convolution fusion | flops 453378048 | bytes 2408448 | tf_op jit(solution)/shard_map/sf,qhf->qsh/dot_general | solution.py:114
  105.5 4.6 %all-to-all-start.2 = ((bf16[4,384,256]{1,2,0:T(8,128)(2,1)}), bf16[4,384,256]{1,2,0:T(8,128)(2,1)S(1)}, u32[]{:S(2)}, u32[]{:S(2)}) async-start(bf16[4,384,256]{1,2,0:T(8,128)(2,1)} %fusion), calls=%async_computation.2 | async-start | bytes 1572864 | tf_op jit(solution)/shard_map/all_to_all | solution.py:117
  110.5 11.1 %all-to-all-done.2 = bf16[4,384,256]{1,2,0:T(8,128)(2,1)S(1)} async-done(((bf16[4,384,256]{1,2,0:T(8,128)(2,1)}), bf16[4,384,256]{1,2,0:T(8,128)(2,1)S(1)}, u32[]{:S(2)}, u32[]{:S(2)}) %all-to-all-start.2) | async-done | bytes 786464 | tf_op jit(solution)/shard_map/all_to_all | solution.py:117
  123.0 3.5 %all-to-all-start.3 = ((bf16[4,384,256]{2,1,0:T(8,128)(2,1)}), bf16[4,384,256]{2,1,0:T(8,128)(2,1)S(1)}, u32[]{:S(2)}, u32[]{:S(2)}) async-start(bf16[4,384,256]{2,1,0:T(8,128)(2,1)} %broadcast_in_dim.60), calls=%async_computation.3 | async-start | bytes 1572864 | tf_op jit(solution)/shard_map/all_to_all | solution.py:122
  127.9 1.7 collective-permute-done
  129.7 7.0 %all-to-all-done.3 = bf16[4,384,256]{2,1,0:T(8,128)(2,1)S(1)} async-done(((bf16[4,384,256]{2,1,0:T(8,128)(2,1)}), bf16[4,384,256]{2,1,0:T(8,128)(2,1)S(1)}, u32[]{:S(2)}, u32[]{:S(2)}) %all-to-all-start.3) | async-done | bytes 786464 | tf_op jit(solution)/shard_map/all_to_all | solution.py:122
  136.8 1.6 fusion.2
  139.9 4.1 %all_to_all.36 = bf16[32,2,6,576]{3,0,2,1:T(8,128)(2,1)S(1)} all-to-all(bf16[32,2,6,576]{3,0,2,1:T(8,128)(2,1)S(1)} %copy.80), channel_id=1, replica_groups=mesh['z'=32,'k'=2,'g'=4,'q'=4] {'k'}, dimensions={1} | all-to-all | bytes 884736 | tf_op jit(solution)/shard_map/all_to_all | solution.py:21
  145.3 4.7 %all-to-all-start.5 = ((bf16[32,2,6,576]{3,1,2,0:T(2,128)(2,1)}), bf16[32,2,6,576]{3,1,2,0:T(2,128)(2,1)S(1)}, u32[]{:S(2)}, u32[]{:S(2)}) async-start(bf16[32,2,6,576]{3,1,2,0:T(2,128)(2,1)} %copy.81), calls=%async_computation.5 | async-start | bytes 983040 | tf_op jit(solution)/shard_map/all_to_all | solution.py:22
  150.1 12.7 %all_gather.3 = bf16[128,1024]{1,0:T(8,128)(2,1)S(1)} all-gather(bf16[128,256]{1,0:T(8,128)(2,1)S(1)} %fusion.26), channel_id=1, replica_groups=mesh['z'=32,'k'=2,'g'=4,'q'=4] {'q'}, dimensions={1}, use_global_device_ids=true | all-gather | bytes 327680 | tf_op jit(solution)/shard_map/all_gather | solution.py:127
  162.7 2.4 %collective-permute-start.7 = (bf16[128,1024]{1,0:T(8,128)(2,1)S(1)}, bf16[128,1024]{1,0:T(8,128)(2,1)S(1)}, u32[]{:S(2)}, u32[]{:S(2)}) collective-permute-start(bf16[128,1024]{1,0:T(8,128)(2,1)S(1)} %all_gather.3), channel_id=1, source_target_pairs={{0,4},{4,8},{8,12},{12,0},{1,5},{5,9},{9,13},{13,1},{2,6},{6,10},{... | collective-permute-start | bytes 786440 | tf_op jit(solution)/shard_map/ppermute | solution.py:131
  165.1 4.3 %collective-permute-start.8 = (bf16[128,1024]{1,0:T(8,128)(2,1)S(1)}, bf16[128,1024]{1,0:T(8,128)(2,1)S(1)}, u32[]{:S(2)}, u32[]{:S(2)}) collective-permute-start(bf16[128,1024]{1,0:T(8,128)(2,1)S(1)} %all_gather.3), channel_id=1, source_target_pairs={{0,8},{4,12},{8,0},{12,4},{1,9},{5,13},{9,1},{13,5},{2,10},{6,14},... | collective-permute-start | bytes 786440 | tf_op jit(solution)/shard_map/ppermute | solution.py:131
  169.5 1.9 collective-permute-start.9
  173.6 38.8 %all-to-all-done.5 = bf16[32,2,6,576]{3,1,2,0:T(2,128)(2,1)S(1)} async-done(((bf16[32,2,6,576]{3,1,2,0:T(2,128)(2,1)}), bf16[32,2,6,576]{3,1,2,0:T(2,128)(2,1)S(1)}, u32[]{:S(2)}, u32[]{:S(2)}) %all-to-all-start.5) | async-done | bytes 442400 | tf_op jit(solution)/shard_map/all_to_all | solution.py:22
  213.8 4.8 %all-to-all-start.6 = ((bf16[128,4,144]{0,2,1:T(8,128)(2,1)}), bf16[128,4,144]{0,2,1:T(8,128)(2,1)S(1)}, u32[]{:S(2)}, u32[]{:S(2)}) async-start(bf16[128,4,144]{0,2,1:T(8,128)(2,1)} %bitcast.27), calls=%async_computation.6 | async-start | bytes 294912 | tf_op jit(solution)/shard_map/all_to_all | solution.py:144
  220.3 2.3 %all-to-all-done.6 = bf16[128,4,144]{0,2,1:T(8,128)(2,1)S(1)} async-done(((bf16[128,4,144]{0,2,1:T(8,128)(2,1)}), bf16[128,4,144]{0,2,1:T(8,128)(2,1)S(1)}, u32[]{:S(2)}, u32[]{:S(2)}) %all-to-all-start.6) | async-done | bytes 147488 | tf_op jit(solution)/shard_map/all_to_all | solution.py:144
  222.6 2.5 %fusion.9 = f32[128,144]{0,1:T(8,128)} fusion(f32[128,144]{0,1:T(8,128)S(1)} %convert_reduce_fusion.2, bf16[18,4,8,1024]{3,2,1,0:T(8,128)(2,1)} %bitcast.83, bf16[4,128,1024]{2,1,0:T(8,128)(2,1)S(1)} %gather_fusion.2, pred[4]{0:T(512)(128)(4,1)S(1)} %compare_and_fusion), kind=kOutput, calls=%fused_computation.22 | convolution fusion | flops 151537664 | bytes 2375684 | tf_op jit(solution)/shard_map/gtc,fgc->tf/dot_general | solution.py:136
  (88 shorter events, 22.7 us)
Async XLA Ops:
  0.6 3.8 %copy-start = (bf16[128,2304]{1,0:T(8,128)(2,1)S(1)}, bf16[128,2304]{1,0:T(8,128)(2,1)}, u32[]{:S(2)}) copy-start(bf16[128,2304]{1,0:T(8,128)(2,1)} %param.13) | copy-start | bytes 1769476
  2.1 0.8 copy-start.9
  3.8 0.6 copy-start.2
  9.6 30.1 %copy-start.1 = (bf16[1,2304,256]{2,1,0:T(8,128)(2,1)S(1)}, bf16[1,2304,256]{2,1,0:T(8,128)(2,1)}, u32[]{:S(2)}) copy-start(bf16[1,2304,256]{2,1,0:T(8,128)(2,1)} %param.16) | copy-start | bytes 3538948
  10.9 91.1 %all-to-all-start.1 = ((bf16[32,2,6,576]{3,1,2,0:T(2,128)(2,1)}), bf16[32,2,6,576]{3,1,2,0:T(2,128)(2,1)S(1)}, u32[]{:S(2)}, u32[]{:S(2)}) async-start(bf16[32,2,6,576]{3,1,2,0:T(2,128)(2,1)} %copy.72), calls=%async_computation.1 | async-start | bytes 983040 | tf_op jit(solution)/shard_map/all_to_all | solution.py:22
  40.6 19.5 %collective-permute-start.4 = (bf16[576,256]{1,0:T(8,128)(2,1)}, bf16[576,256]{1,0:T(8,128)(2,1)S(1)}, u32[]{:S(2)}, u32[]{:S(2)}) collective-permute-start(bf16[576,256]{1,0:T(8,128)(2,1)} %bitcast.18), channel_id=1, source_target_pairs={{0,1},{1,2},{2,3},{3,0},{4,5},{5,6},{6,7},{7,4},{8,9},{9,10},{10,1... | collective-permute-start | bytes 884744 | tf_op jit(solution)/shard_map/ppermute | solution.py:28
  44.1 19.9 %collective-permute-start.5 = (bf16[576,256]{1,0:T(8,128)(2,1)}, bf16[576,256]{1,0:T(8,128)(2,1)S(1)}, u32[]{:S(2)}, u32[]{:S(2)}) collective-permute-start(bf16[576,256]{1,0:T(8,128)(2,1)} %bitcast.20), channel_id=1, source_target_pairs={{0,2},{1,3},{2,0},{3,1},{4,6},{5,7},{6,4},{7,5},{8,10},{9,11},{10,... | collective-permute-start | bytes 884744 | tf_op jit(solution)/shard_map/ppermute | solution.py:28
  48.9 15.1 %collective-permute-start.6 = (bf16[576,256]{1,0:T(8,128)(2,1)}, bf16[576,256]{1,0:T(8,128)(2,1)}, u32[]{:S(2)}, u32[]{:S(2)}) collective-permute-start(bf16[576,256]{1,0:T(8,128)(2,1)} %bitcast.22), channel_id=1, source_target_pairs={{0,3},{1,0},{2,1},{3,2},{4,7},{5,4},{6,5},{7,6},{8,11},{9,8},{10,9... | collective-permute-start | bytes 884744 | tf_op jit(solution)/shard_map/ppermute | solution.py:28
  54.8 18.4 %collective-permute-start.1 = (bf16[256,576]{0,1:T(8,128)(2,1)}, bf16[256,576]{0,1:T(8,128)(2,1)S(1)}, u32[]{:S(2)}, u32[]{:S(2)}) collective-permute-start(bf16[256,576]{0,1:T(8,128)(2,1)} %get-tuple-element.37), channel_id=1, source_target_pairs={{0,1},{1,2},{2,3},{3,0},{4,5},{5,6},{6,7},{7,4},{8,9},{9,10},{10,1... | collective-permute-start | bytes 884744 | tf_op jit(solution)/shard_map/ppermute | solution.py:28
  57.4 15.8 %collective-permute-start.2 = (bf16[256,576]{0,1:T(8,128)(2,1)}, bf16[256,576]{0,1:T(8,128)(2,1)}, u32[]{:S(2)}, u32[]{:S(2)}) collective-permute-start(bf16[256,576]{0,1:T(8,128)(2,1)} %get-tuple-element.36), channel_id=1, source_target_pairs={{0,2},{1,3},{2,0},{3,1},{4,6},{5,7},{6,4},{7,5},{8,10},{9,11},{10,... | collective-permute-start | bytes 884744 | tf_op jit(solution)/shard_map/ppermute | solution.py:28
  60.1 14.9 %collective-permute-start.3 = (bf16[256,576]{0,1:T(8,128)(2,1)}, bf16[256,576]{0,1:T(8,128)(2,1)}, u32[]{:S(2)}, u32[]{:S(2)}) collective-permute-start(bf16[256,576]{0,1:T(8,128)(2,1)} %get-tuple-element.35), channel_id=1, source_target_pairs={{0,3},{1,0},{2,1},{3,2},{4,7},{5,4},{6,5},{7,6},{8,11},{9,8},{10,9... | collective-permute-start | bytes 884744 | tf_op jit(solution)/shard_map/ppermute | solution.py:28
  73.2 1.8 copy-start.6
  105.5 4.6 %copy-start.4 = (bf16[1,64,6,256]{3,1,2,0:T(8,128)(2,1)S(1)}, bf16[1,64,6,256]{3,1,2,0:T(8,128)(2,1)}, u32[]{:S(2)}) copy-start(bf16[1,64,6,256]{3,1,2,0:T(8,128)(2,1)} %param.14) | copy-start | bytes 589828
  105.5 16.1 %all-to-all-start.2 = ((bf16[4,384,256]{1,2,0:T(8,128)(2,1)}), bf16[4,384,256]{1,2,0:T(8,128)(2,1)S(1)}, u32[]{:S(2)}, u32[]{:S(2)}) async-start(bf16[4,384,256]{1,2,0:T(8,128)(2,1)} %fusion), calls=%async_computation.2 | async-start | bytes 1572864 | tf_op jit(solution)/shard_map/all_to_all | solution.py:117
  122.0 4.5 %copy-start.7 = (bf16[128,256]{1,0:T(8,128)(2,1)S(1)}, bf16[128,256]{1,0:T(8,128)(2,1)}, u32[]{:S(2)}) copy-start(bf16[128,256]{1,0:T(8,128)(2,1)} %param.19) | copy-start | bytes 196612
  122.0 4.5 %copy-start.8 = (bf16[128,256]{1,0:T(8,128)(2,1)S(1)}, bf16[128,256]{1,0:T(8,128)(2,1)}, u32[]{:S(2)}) copy-start(bf16[128,256]{1,0:T(8,128)(2,1)} %param.18) | copy-start | bytes 196612
  122.0 5.9 %copy-start.10 = (f32[4,256]{1,0:T(4,128)S(1)}, f32[4,256]{1,0:T(4,128)}, u32[]{:S(2)}) copy-start(f32[4,256]{1,0:T(4,128)} %param.20) | copy-start | bytes 12292
  123.0 13.8 %all-to-all-start.3 = ((bf16[4,384,256]{2,1,0:T(8,128)(2,1)}), bf16[4,384,256]{2,1,0:T(8,128)(2,1)S(1)}, u32[]{:S(2)}, u32[]{:S(2)}) async-start(bf16[4,384,256]{2,1,0:T(8,128)(2,1)} %broadcast_in_dim.60), calls=%async_computation.3 | async-start | bytes 1572864 | tf_op jit(solution)/shard_map/all_to_all | solution.py:122
  126.6 3.1 %collective-permute-start = (f32[3,256]{1,0:T(4,128)S(1)}, f32[3,256]{1,0:T(4,128)S(1)}, u32[]{:S(2)}, u32[]{:S(2)}) collective-permute-start(f32[3,256]{1,0:T(4,128)S(1)} %slice.48), channel_id=1, source_target_pairs={{16,0},{32,16},{48,32},{64,48},{80,64},{96,80},{112,96},{128,112},... | collective-permute-start | bytes 9224 | tf_op jit(solution)/shard_map/ppermute | solution.py:15
  145.3 67.1 %all-to-all-start.5 = ((bf16[32,2,6,576]{3,1,2,0:T(2,128)(2,1)}), bf16[32,2,6,576]{3,1,2,0:T(2,128)(2,1)S(1)}, u32[]{:S(2)}, u32[]{:S(2)}) async-start(bf16[32,2,6,576]{3,1,2,0:T(2,128)(2,1)} %copy.81), calls=%async_computation.5 | async-start | bytes 983040 | tf_op jit(solution)/shard_map/all_to_all | solution.py:22
  150.0 21.6 %copy-start.5 = (bf16[1,64,6,256]{3,1,2,0:T(8,128)(2,1)S(1)}, bf16[1,64,6,256]{3,1,2,0:T(8,128)(2,1)}, u32[]{:S(2)}) copy-start(bf16[1,64,6,256]{3,1,2,0:T(8,128)(2,1)} %param.14) | copy-start | bytes 589828
  162.7 50.0 %collective-permute-start.7 = (bf16[128,1024]{1,0:T(8,128)(2,1)S(1)}, bf16[128,1024]{1,0:T(8,128)(2,1)S(1)}, u32[]{:S(2)}, u32[]{:S(2)}) collective-permute-start(bf16[128,1024]{1,0:T(8,128)(2,1)S(1)} %all_gather.3), channel_id=1, source_target_pairs={{0,4},{4,8},{8,12},{12,0},{1,5},{5,9},{9,13},{13,1},{2,6},{6,10},{... | collective-permute-start | bytes 786440 | tf_op jit(solution)/shard_map/ppermute | solution.py:131
  165.1 47.7 %collective-permute-start.8 = (bf16[128,1024]{1,0:T(8,128)(2,1)S(1)}, bf16[128,1024]{1,0:T(8,128)(2,1)S(1)}, u32[]{:S(2)}, u32[]{:S(2)}) collective-permute-start(bf16[128,1024]{1,0:T(8,128)(2,1)S(1)} %all_gather.3), channel_id=1, source_target_pairs={{0,8},{4,12},{8,0},{12,4},{1,9},{5,13},{9,1},{13,5},{2,10},{6,14},... | collective-permute-start | bytes 786440 | tf_op jit(solution)/shard_map/ppermute | solution.py:131
  169.5 43.3 %collective-permute-start.9 = (bf16[128,1024]{1,0:T(8,128)(2,1)S(1)}, bf16[128,1024]{1,0:T(8,128)(2,1)}, u32[]{:S(2)}, u32[]{:S(2)}) collective-permute-start(bf16[128,1024]{1,0:T(8,128)(2,1)S(1)} %all_gather.3), channel_id=1, source_target_pairs={{0,12},{4,0},{8,4},{12,8},{1,13},{5,1},{9,5},{13,9},{2,14},{6,2},{... | collective-permute-start | bytes 786440 | tf_op jit(solution)/shard_map/ppermute | solution.py:131
  173.6 39.2 %copy-start.3 = (bf16[128,384]{1,0:T(8,128)(2,1)S(1)}, bf16[128,384]{1,0:T(8,128)(2,1)}, u32[]{:S(2)}) copy-start(bf16[128,384]{1,0:T(8,128)(2,1)} %copy-done.2) | copy-start | bytes 294916
  213.8 8.8 %all-to-all-start.6 = ((bf16[128,4,144]{0,2,1:T(8,128)(2,1)}), bf16[128,4,144]{0,2,1:T(8,128)(2,1)S(1)}, u32[]{:S(2)}, u32[]{:S(2)}) async-start(bf16[128,4,144]{0,2,1:T(8,128)(2,1)} %bitcast.27), calls=%async_computation.6 | async-start | bytes 294912 | tf_op jit(solution)/shard_map/all_to_all | solution.py:144

commit v12 on v11

--- a/solution.py
+++ b/solution.py
@@ -123,7 +123,12 @@
     summed_rows = jnp.einsum(
         "qsh,qfh->sf", up_all, up_got, preferred_element_type=jnp.float32
     ).astype(jnp.bfloat16)
-    key_grad, summed_rows = lax.optimization_barrier((key_grad, summed_rows))
+    key_weights = jnp.take(
+        w_key.reshape(w_key.shape[0], groups, -1), (my_group - jnp.arange(groups)) % groups, axis=1
+    )
+    key_grad, key_weights, summed_rows = lax.optimization_barrier(
+        (key_grad, key_weights, summed_rows)
+    )
     key_group = lax.all_gather(key_grad, "q", axis=1, tiled=True)
     key_got = [key_group]
     for shift in range(1, groups):
@@ -132,11 +137,10 @@
         )
     came_back = across_ctx(summed_rows)
     key_got, came_back = lax.optimization_barrier((key_got, came_back))
-    key_got = jnp.take(jnp.stack(key_got), (my_group - jnp.arange(groups)) % groups, axis=0)
     key_input = jnp.einsum(
         "gtc,fgc->tf",
-        key_got,
-        w_key.reshape(w_key.shape[0], groups, -1),
+        jnp.stack(key_got),
+        key_weights,
         preferred_element_type=jnp.float32,
     )
     token_rows = jnp.dot(placement, came_back, preferred_element_type=jnp.float32)

time: 227 us -> 226 us (level)
    all_to_all x1, waiting for transfers between devices: 11.1 us -> 7.78 us  [local(): hidden_parts = lax.all_to_all(hidden_parts, 'q', 0, 0, tiled=True)]
  transfers between devices with their start and end apart: 15 -> 15, of which waited for: 8 -> 7; matrix products, arithmetic and copies ran while one was open for 7% -> 8% of each run, Pallas kernels for 0% -> 0%
where the time goes in v12:
time: 226 us; the launch traced here: 225 us
  waiting for transfers between devices  91.1 us (40%)
  starting transfers between devices  77.7 us (34%)
  blocking collectives  20.8 us (9%)
  local copies, waits for them, and re-layouts  16.3 us (7%)
  other arithmetic  9.84 us (4%)
  matrix products  7.49 us (3%)
    all_to_all x2, waiting for transfers between devices, across_ctx(): lax.all_to_all(blocks, 'z', split_axis=0, concat_axis=0, tiled=True)  63.2 us
    all_to_all x2, starting transfers between devices, across_ctx(): lax.all_to_all(blocks, 'z', split_axis=0, concat_axis=0, tiled=True)  33.4 us
    ppermute x6, starting transfers between devices, around(): lax.ppermute(value, 'q', [(source, (source + steps) % count) for source i...  20.6 us
    all_gather x1, blocking collectives, local(): key_group = lax.all_gather(key_grad, 'q', axis=1, tiled=True)  12.6 us
    all_to_all x1, waiting for transfers between devices, local(): up_all = lax.all_to_all(up_all, 'q', 0, 0, tiled=True)  8.99 us
    ppermute x3, starting transfers between devices, local(): lax.ppermute(key_group, 'g', [(i, (i + shift) % groups) for i in range(gr...  8.64 us
    ppermute x6, waiting for transfers between devices, around(): lax.ppermute(value, 'q', [(source, (source + steps) % count) for source i...  8.28 us
    all_to_all x2, blocking collectives, across_ctx(): lax.all_to_all(blocks, 'k', split_axis=1, concat_axis=1, tiled=True)  8.22 us
  transfers between devices with their start and end apart: 15, of which 7 were waited for; matrix products, arithmetic and copies ran while one was open for 8% of the time, Pallas kernels for 0%

profile of v12, /device:TPU:6, one launch (start us, length us, event | category | flops | bytes accessed | tf_op | source)
XLA Modules:
  0.0 224.5 jit_solution(4092737588688443431)
XLA Ops:
  4.8 4.1 %all_to_all.35 = bf16[32,2,6,576]{3,0,2,1:T(8,128)(2,1)S(1)} all-to-all(bf16[32,2,6,576]{3,0,2,1:T(8,128)(2,1)S(1)} %copy.87), channel_id=1, replica_groups=mesh['z'=32,'k'=2,'g'=4,'q'=4] {'k'}, dimensions={1} | all-to-all | bytes 884736 | tf_op jit(solution)/shard_map/all_to_all | solution.py:21
  10.2 28.7 %all-to-all-start.1 = ((bf16[32,2,6,576]{3,1,2,0:T(2,128)(2,1)}), bf16[32,2,6,576]{3,1,2,0:T(2,128)(2,1)S(1)}, u32[]{:S(2)}, u32[]{:S(2)}) async-start(bf16[32,2,6,576]{3,1,2,0:T(2,128)(2,1)} %copy.88), calls=%async_computation.1 | async-start | bytes 983040 | tf_op jit(solution)/shard_map/all_to_all | solution.py:22
  40.0 3.5 %collective-permute-start.4 = (bf16[576,256]{1,0:T(8,128)(2,1)}, bf16[576,256]{1,0:T(8,128)(2,1)S(1)}, u32[]{:S(2)}, u32[]{:S(2)}) collective-permute-start(bf16[576,256]{1,0:T(8,128)(2,1)} %bitcast.20), channel_id=1, source_target_pairs={{0,1},{1,2},{2,3},{3,0},{4,5},{5,6},{6,7},{7,4},{8,9},{9,10},{10,1... | collective-permute-start | bytes 884744 | tf_op jit(solution)/shard_map/ppermute | solution.py:28
  43.5 4.8 %collective-permute-start.5 = (bf16[576,256]{1,0:T(8,128)(2,1)}, bf16[576,256]{1,0:T(8,128)(2,1)S(1)}, u32[]{:S(2)}, u32[]{:S(2)}) collective-permute-start(bf16[576,256]{1,0:T(8,128)(2,1)} %bitcast.22), channel_id=1, source_target_pairs={{0,2},{1,3},{2,0},{3,1},{4,6},{5,7},{6,4},{7,5},{8,10},{9,11},{10,... | collective-permute-start | bytes 884744 | tf_op jit(solution)/shard_map/ppermute | solution.py:28
  48.3 3.3 %collective-permute-start.6 = (bf16[576,256]{1,0:T(8,128)(2,1)}, bf16[576,256]{1,0:T(8,128)(2,1)}, u32[]{:S(2)}, u32[]{:S(2)}) collective-permute-start(bf16[576,256]{1,0:T(8,128)(2,1)} %bitcast.24), channel_id=1, source_target_pairs={{0,3},{1,0},{2,1},{3,2},{4,7},{5,4},{6,5},{7,6},{8,11},{9,8},{10,9... | collective-permute-start | bytes 884744 | tf_op jit(solution)/shard_map/ppermute | solution.py:28
  51.6 1.6 copy.84
  54.2 2.6 %collective-permute-start.1 = (bf16[256,576]{0,1:T(8,128)(2,1)}, bf16[256,576]{0,1:T(8,128)(2,1)S(1)}, u32[]{:S(2)}, u32[]{:S(2)}) collective-permute-start(bf16[256,576]{0,1:T(8,128)(2,1)} %get-tuple-element.41), channel_id=1, source_target_pairs={{0,1},{1,2},{2,3},{3,0},{4,5},{5,6},{6,7},{7,4},{8,9},{9,10},{10,1... | collective-permute-start | bytes 884744 | tf_op jit(solution)/shard_map/ppermute | solution.py:28
  56.8 2.7 %collective-permute-start.2 = (bf16[256,576]{0,1:T(8,128)(2,1)}, bf16[256,576]{0,1:T(8,128)(2,1)}, u32[]{:S(2)}, u32[]{:S(2)}) collective-permute-start(bf16[256,576]{0,1:T(8,128)(2,1)} %get-tuple-element.40), channel_id=1, source_target_pairs={{0,2},{1,3},{2,0},{3,1},{4,6},{5,7},{6,4},{7,5},{8,10},{9,11},{10,... | collective-permute-start | bytes 884744 | tf_op jit(solution)/shard_map/ppermute | solution.py:28
  59.5 3.8 %collective-permute-start.3 = (bf16[256,576]{0,1:T(8,128)(2,1)}, bf16[256,576]{0,1:T(8,128)(2,1)}, u32[]{:S(2)}, u32[]{:S(2)}) collective-permute-start(bf16[256,576]{0,1:T(8,128)(2,1)} %get-tuple-element.39), channel_id=1, source_target_pairs={{0,3},{1,0},{2,1},{3,2},{4,7},{5,4},{6,5},{7,6},{8,11},{9,8},{10,9... | collective-permute-start | bytes 884744 | tf_op jit(solution)/shard_map/ppermute | solution.py:28
  64.5 1.6 gather_fusion.2
  66.1 6.4 %collective-permute-done.1 = bf16[256,576]{0,1:T(8,128)(2,1)S(1)} collective-permute-done((bf16[256,576]{0,1:T(8,128)(2,1)}, bf16[256,576]{0,1:T(8,128)(2,1)S(1)}, u32[]{:S(2)}, u32[]{:S(2)}) %collective-permute-start.1) | collective-permute-done | bytes 294944 | tf_op jit(solution)/shard_map/ppermute | solution.py:28
  72.6 1.8 collective-permute-done.3
  74.4 1.4 pad_maximum_fusion
  76.4 2.4 %broadcast_select_fusion = bf16[4,576,256]{2,1,0:T(8,128)(2,1)} fusion(bf16[4,576,256]{2,1,0:T(8,128)(2,1)} %gather_fusion.2, pred[4]{0:T(512)(128)(4,1)S(1)} %compare_and_fusion), kind=kLoop, calls=%fused_computation.17 | loop fusion | flops 589824 | bytes 2359300 | tf_op jit(solution)/shard_map/jit(_take)/select_n | solution.py:109
  79.1 22.3 %all-to-all-done.1 = bf16[32,2,6,576]{3,1,2,0:T(2,128)(2,1)S(1)} async-done(((bf16[32,2,6,576]{3,1,2,0:T(2,128)(2,1)}), bf16[32,2,6,576]{3,1,2,0:T(2,128)(2,1)S(1)}, u32[]{:S(2)}, u32[]{:S(2)}) %all-to-all-start.1) | async-done | bytes 442400 | tf_op jit(solution)/shard_map/all_to_all | solution.py:22
  101.7 1.9 fusion
  103.6 4.6 %all-to-all-start.2 = ((bf16[4,384,256]{1,2,0:T(8,128)(2,1)}), bf16[4,384,256]{1,2,0:T(8,128)(2,1)}, u32[]{:S(2)}, u32[]{:S(2)}) async-start(bf16[4,384,256]{1,2,0:T(8,128)(2,1)} %fusion), calls=%async_computation.2 | async-start | bytes 1572864 | tf_op jit(solution)/shard_map/all_to_all | solution.py:117
  110.0 1.4 copy.110
  112.0 7.8 %all-to-all-done.2 = bf16[4,384,256]{1,2,0:T(8,128)(2,1)} async-done(((bf16[4,384,256]{1,2,0:T(8,128)(2,1)}), bf16[4,384,256]{1,2,0:T(8,128)(2,1)}, u32[]{:S(2)}, u32[]{:S(2)}) %all-to-all-start.2) | async-done | bytes 786464 | tf_op jit(solution)/shard_map/all_to_all | solution.py:117
  122.3 4.2 %all-to-all-start.3 = ((bf16[4,384,256]{2,1,0:T(8,128)(2,1)}), bf16[4,384,256]{2,1,0:T(8,128)(2,1)}, u32[]{:S(2)}, u32[]{:S(2)}) async-start(bf16[4,384,256]{2,1,0:T(8,128)(2,1)} %broadcast_in_dim.62), calls=%async_computation.3 | async-start | bytes 1572864 | tf_op jit(solution)/shard_map/all_to_all | solution.py:122
  127.9 9.0 %all-to-all-done.3 = bf16[4,384,256]{2,1,0:T(8,128)(2,1)} async-done(((bf16[4,384,256]{2,1,0:T(8,128)(2,1)}), bf16[4,384,256]{2,1,0:T(8,128)(2,1)}, u32[]{:S(2)}, u32[]{:S(2)}) %all-to-all-start.3) | async-done | bytes 786464 | tf_op jit(solution)/shard_map/all_to_all | solution.py:122
  136.9 1.9 fusion.2
  139.4 4.1 %all_to_all.36 = bf16[32,2,6,576]{3,0,2,1:T(8,128)(2,1)S(1)} all-to-all(bf16[32,2,6,576]{3,0,2,1:T(8,128)(2,1)S(1)} %copy.96), channel_id=1, replica_groups=mesh['z'=32,'k'=2,'g'=4,'q'=4] {'k'}, dimensions={1} | all-to-all | bytes 884736 | tf_op jit(solution)/shard_map/all_to_all | solution.py:21
  144.8 4.7 %all-to-all-start.5 = ((bf16[32,2,6,576]{3,1,2,0:T(2,128)(2,1)}), bf16[32,2,6,576]{3,1,2,0:T(2,128)(2,1)S(1)}, u32[]{:S(2)}, u32[]{:S(2)}) async-start(bf16[32,2,6,576]{3,1,2,0:T(2,128)(2,1)} %copy.97), calls=%async_computation.5 | async-start | bytes 983040 | tf_op jit(solution)/shard_map/all_to_all | solution.py:22
  149.5 12.6 %all_gather.3 = bf16[128,1024]{1,0:T(8,128)(2,1)S(1)} all-gather(bf16[128,256]{1,0:T(8,128)(2,1)S(1)} %fusion.22), channel_id=1, replica_groups=mesh['z'=32,'k'=2,'g'=4,'q'=4] {'q'}, dimensions={1}, use_global_device_ids=true | all-gather | bytes 327680 | tf_op jit(solution)/shard_map/all_gather | solution.py:132
  162.0 2.4 %collective-permute-start.7 = (bf16[128,1024]{1,0:T(8,128)(2,1)S(1)}, bf16[128,1024]{1,0:T(8,128)(2,1)}, u32[]{:S(2)}, u32[]{:S(2)}) collective-permute-start(bf16[128,1024]{1,0:T(8,128)(2,1)S(1)} %all_gather.3), channel_id=1, source_target_pairs={{0,4},{4,8},{8,12},{12,0},{1,5},{5,9},{9,13},{13,1},{2,6},{6,10},{... | collective-permute-start | bytes 786440 | tf_op jit(solution)/shard_map/ppermute | solution.py:136
  164.4 4.3 %collective-permute-start.8 = (bf16[128,1024]{1,0:T(8,128)(2,1)S(1)}, bf16[128,1024]{1,0:T(8,128)(2,1)}, u32[]{:S(2)}, u32[]{:S(2)}) collective-permute-start(bf16[128,1024]{1,0:T(8,128)(2,1)S(1)} %all_gather.3), channel_id=1, source_target_pairs={{0,8},{4,12},{8,0},{12,4},{1,9},{5,13},{9,1},{13,5},{2,10},{6,14},... | collective-permute-start | bytes 786440 | tf_op jit(solution)/shard_map/ppermute | solution.py:136
  168.8 1.9 collective-permute-start.9
  170.9 40.9 %all-to-all-done.5 = bf16[32,2,6,576]{3,1,2,0:T(2,128)(2,1)S(1)} async-done(((bf16[32,2,6,576]{3,1,2,0:T(2,128)(2,1)}), bf16[32,2,6,576]{3,1,2,0:T(2,128)(2,1)S(1)}, u32[]{:S(2)}, u32[]{:S(2)}) %all-to-all-start.5) | async-done | bytes 442400 | tf_op jit(solution)/shard_map/all_to_all | solution.py:22
  213.3 4.9 %all-to-all-start.6 = ((bf16[128,4,144]{0,2,1:T(8,128)(2,1)}), bf16[128,4,144]{0,2,1:T(8,128)(2,1)S(1)}, u32[]{:S(2)}, u32[]{:S(2)}) async-start(bf16[128,4,144]{0,2,1:T(8,128)(2,1)} %bitcast.29), calls=%async_computation.6 | async-start | bytes 294912 | tf_op jit(solution)/shard_map/all_to_all | solution.py:148
  219.3 2.9 %all-to-all-done.6 = bf16[128,4,144]{0,2,1:T(8,128)(2,1)S(1)} async-done(((bf16[128,4,144]{0,2,1:T(8,128)(2,1)}), bf16[128,4,144]{0,2,1:T(8,128)(2,1)S(1)}, u32[]{:S(2)}, u32[]{:S(2)}) %all-to-all-start.6) | async-done | bytes 147488 | tf_op jit(solution)/shard_map/all_to_all | solution.py:148
  222.3 2.2 fusion.3
  (99 shorter events, 20.5 us)
Async XLA Ops:
  0.6 3.2 %copy-start = (bf16[128,2304]{1,0:T(8,128)(2,1)S(1)}, bf16[128,2304]{1,0:T(8,128)(2,1)}, u32[]{:S(2)}) copy-start(bf16[128,2304]{1,0:T(8,128)(2,1)} %param.13) | copy-start | bytes 1769476
  2.1 0.8 copy-start.14
  8.9 30.1 %copy-start.3 = (bf16[1,2304,256]{2,1,0:T(8,128)(2,1)S(1)}, bf16[1,2304,256]{2,1,0:T(8,128)(2,1)}, u32[]{:S(2)}) copy-start(bf16[1,2304,256]{2,1,0:T(8,128)(2,1)} %param.16) | copy-start | bytes 3538948
  10.2 91.1 %all-to-all-start.1 = ((bf16[32,2,6,576]{3,1,2,0:T(2,128)(2,1)}), bf16[32,2,6,576]{3,1,2,0:T(2,128)(2,1)S(1)}, u32[]{:S(2)}, u32[]{:S(2)}) async-start(bf16[32,2,6,576]{3,1,2,0:T(2,128)(2,1)} %copy.88), calls=%async_computation.1 | async-start | bytes 983040 | tf_op jit(solution)/shard_map/all_to_all | solution.py:22
  40.0 19.5 %collective-permute-start.4 = (bf16[576,256]{1,0:T(8,128)(2,1)}, bf16[576,256]{1,0:T(8,128)(2,1)S(1)}, u32[]{:S(2)}, u32[]{:S(2)}) collective-permute-start(bf16[576,256]{1,0:T(8,128)(2,1)} %bitcast.20), channel_id=1, source_target_pairs={{0,1},{1,2},{2,3},{3,0},{4,5},{5,6},{6,7},{7,4},{8,9},{9,10},{10,1... | collective-permute-start | bytes 884744 | tf_op jit(solution)/shard_map/ppermute | solution.py:28
  43.5 19.9 %collective-permute-start.5 = (bf16[576,256]{1,0:T(8,128)(2,1)}, bf16[576,256]{1,0:T(8,128)(2,1)S(1)}, u32[]{:S(2)}, u32[]{:S(2)}) collective-permute-start(bf16[576,256]{1,0:T(8,128)(2,1)} %bitcast.22), channel_id=1, source_target_pairs={{0,2},{1,3},{2,0},{3,1},{4,6},{5,7},{6,4},{7,5},{8,10},{9,11},{10,... | collective-permute-start | bytes 884744 | tf_op jit(solution)/shard_map/ppermute | solution.py:28
  48.3 15.1 %collective-permute-start.6 = (bf16[576,256]{1,0:T(8,128)(2,1)}, bf16[576,256]{1,0:T(8,128)(2,1)}, u32[]{:S(2)}, u32[]{:S(2)}) collective-permute-start(bf16[576,256]{1,0:T(8,128)(2,1)} %bitcast.24), channel_id=1, source_target_pairs={{0,3},{1,0},{2,1},{3,2},{4,7},{5,4},{6,5},{7,6},{8,11},{9,8},{10,9... | collective-permute-start | bytes 884744 | tf_op jit(solution)/shard_map/ppermute | solution.py:28
  54.2 18.4 %collective-permute-start.1 = (bf16[256,576]{0,1:T(8,128)(2,1)}, bf16[256,576]{0,1:T(8,128)(2,1)S(1)}, u32[]{:S(2)}, u32[]{:S(2)}) collective-permute-start(bf16[256,576]{0,1:T(8,128)(2,1)} %get-tuple-element.41), channel_id=1, source_target_pairs={{0,1},{1,2},{2,3},{3,0},{4,5},{5,6},{6,7},{7,4},{8,9},{9,10},{10,1... | collective-permute-start | bytes 884744 | tf_op jit(solution)/shard_map/ppermute | solution.py:28
  56.8 15.8 %collective-permute-start.2 = (bf16[256,576]{0,1:T(8,128)(2,1)}, bf16[256,576]{0,1:T(8,128)(2,1)}, u32[]{:S(2)}, u32[]{:S(2)}) collective-permute-start(bf16[256,576]{0,1:T(8,128)(2,1)} %get-tuple-element.40), channel_id=1, source_target_pairs={{0,2},{1,3},{2,0},{3,1},{4,6},{5,7},{6,4},{7,5},{8,10},{9,11},{10,... | collective-permute-start | bytes 884744 | tf_op jit(solution)/shard_map/ppermute | solution.py:28
  59.5 14.9 %collective-permute-start.3 = (bf16[256,576]{0,1:T(8,128)(2,1)}, bf16[256,576]{0,1:T(8,128)(2,1)}, u32[]{:S(2)}, u32[]{:S(2)}) collective-permute-start(bf16[256,576]{0,1:T(8,128)(2,1)} %get-tuple-element.39), channel_id=1, source_target_pairs={{0,3},{1,0},{2,1},{3,2},{4,7},{5,4},{6,5},{7,6},{8,11},{9,8},{10,9... | collective-permute-start | bytes 884744 | tf_op jit(solution)/shard_map/ppermute | solution.py:28
  72.6 1.8 copy-start.8
  103.6 4.6 %copy-start.12 = (bf16[128,256]{1,0:T(8,128)(2,1)S(1)}, bf16[128,256]{1,0:T(8,128)(2,1)}, u32[]{:S(2)}) copy-start(bf16[128,256]{1,0:T(8,128)(2,1)} %param.19) | copy-start | bytes 196612
  103.6 4.6 %copy-start.13 = (bf16[128,256]{1,0:T(8,128)(2,1)S(1)}, bf16[128,256]{1,0:T(8,128)(2,1)}, u32[]{:S(2)}) copy-start(bf16[128,256]{1,0:T(8,128)(2,1)} %param.18) | copy-start | bytes 196612
  103.6 6.0 %copy-start.4 = (bf16[1,64,6,256]{3,1,2,0:T(8,128)(2,1)S(1)}, bf16[1,64,6,256]{3,1,2,0:T(8,128)(2,1)}, u32[]{:S(2)}) copy-start(bf16[1,64,6,256]{3,1,2,0:T(8,128)(2,1)} %param.14) | copy-start | bytes 589828
  103.6 16.2 %all-to-all-start.2 = ((bf16[4,384,256]{1,2,0:T(8,128)(2,1)}), bf16[4,384,256]{1,2,0:T(8,128)(2,1)}, u32[]{:S(2)}, u32[]{:S(2)}) async-start(bf16[4,384,256]{1,2,0:T(8,128)(2,1)} %fusion), calls=%async_computation.2 | async-start | bytes 1572864 | tf_op jit(solution)/shard_map/all_to_all | solution.py:117
  108.3 1.3 copy-start.6
  108.3 19.5 %collective-permute-start = (f32[3,256]{1,0:T(4,128)S(1)}, f32[3,256]{1,0:T(4,128)S(1)}, u32[]{:S(2)}, u32[]{:S(2)}) collective-permute-start(f32[3,256]{1,0:T(4,128)S(1)} %slice.48), channel_id=1, source_target_pairs={{16,0},{32,16},{48,32},{64,48},{80,64},{96,80},{112,96},{128,112},... | collective-permute-start | bytes 9224 | tf_op jit(solution)/shard_map/ppermute | solution.py:15
  122.3 14.6 %all-to-all-start.3 = ((bf16[4,384,256]{2,1,0:T(8,128)(2,1)}), bf16[4,384,256]{2,1,0:T(8,128)(2,1)}, u32[]{:S(2)}, u32[]{:S(2)}) async-start(bf16[4,384,256]{2,1,0:T(8,128)(2,1)} %broadcast_in_dim.62), calls=%async_computation.3 | async-start | bytes 1572864 | tf_op jit(solution)/shard_map/all_to_all | solution.py:122
  126.5 1.3 copy-start.15
  126.5 1.3 copy-start.7
  126.5 10.3 %copy-start.2 = (bf16[4,576,256]{2,1,0:T(8,128)(2,1)S(1)}, bf16[4,576,256]{2,1,0:T(8,128)(2,1)}, u32[]{:S(2)}) copy-start(bf16[4,576,256]{2,1,0:T(8,128)(2,1)} %broadcast_select_fusion) | copy-start | bytes 3538948
  144.8 67.1 %all-to-all-start.5 = ((bf16[32,2,6,576]{3,1,2,0:T(2,128)(2,1)}), bf16[32,2,6,576]{3,1,2,0:T(2,128)(2,1)S(1)}, u32[]{:S(2)}, u32[]{:S(2)}) async-start(bf16[32,2,6,576]{3,1,2,0:T(2,128)(2,1)} %copy.97), calls=%async_computation.5 | async-start | bytes 983040 | tf_op jit(solution)/shard_map/all_to_all | solution.py:22
  162.0 49.9 %copy-start.9 = (bf16[128,1024]{1,0:T(8,128)(2,1)}, bf16[128,1024]{1,0:T(8,128)(2,1)S(1)}, u32[]{:S(2)}) copy-start(bf16[128,1024]{1,0:T(8,128)(2,1)S(1)} %all_gather.3) | copy-start | bytes 786436
  162.0 50.2 %collective-permute-start.7 = (bf16[128,1024]{1,0:T(8,128)(2,1)S(1)}, bf16[128,1024]{1,0:T(8,128)(2,1)}, u32[]{:S(2)}, u32[]{:S(2)}) collective-permute-start(bf16[128,1024]{1,0:T(8,128)(2,1)S(1)} %all_gather.3), channel_id=1, source_target_pairs={{0,4},{4,8},{8,12},{12,0},{1,5},{5,9},{9,13},{13,1},{2,6},{6,10},{... | collective-permute-start | bytes 786440 | tf_op jit(solution)/shard_map/ppermute | solution.py:136
  164.4 47.9 %collective-permute-start.8 = (bf16[128,1024]{1,0:T(8,128)(2,1)S(1)}, bf16[128,1024]{1,0:T(8,128)(2,1)}, u32[]{:S(2)}, u32[]{:S(2)}) collective-permute-start(bf16[128,1024]{1,0:T(8,128)(2,1)S(1)} %all_gather.3), channel_id=1, source_target_pairs={{0,8},{4,12},{8,0},{12,4},{1,9},{5,13},{9,1},{13,5},{2,10},{6,14},... | collective-permute-start | bytes 786440 | tf_op jit(solution)/shard_map/ppermute | solution.py:136
  168.8 43.5 %collective-permute-start.9 = (bf16[128,1024]{1,0:T(8,128)(2,1)S(1)}, bf16[128,1024]{1,0:T(8,128)(2,1)}, u32[]{:S(2)}, u32[]{:S(2)}) collective-permute-start(bf16[128,1024]{1,0:T(8,128)(2,1)S(1)} %all_gather.3), channel_id=1, source_target_pairs={{0,12},{4,0},{8,4},{12,8},{1,13},{5,1},{9,5},{13,9},{2,14},{6,2},{... | collective-permute-start | bytes 786440 | tf_op jit(solution)/shard_map/ppermute | solution.py:136
  211.9 6.3 %copy-start.5 = (bf16[1,64,6,256]{3,1,2,0:T(8,128)(2,1)S(1)}, bf16[1,64,6,256]{3,1,2,0:T(8,128)(2,1)}, u32[]{:S(2)}) copy-start(bf16[1,64,6,256]{3,1,2,0:T(8,128)(2,1)} %param.14) | copy-start | bytes 589828
  212.0 6.3 %copy-start.11 = (bf16[1,64,6,256]{3,1,2,0:T(8,128)(2,1)S(1)}, bf16[1,64,6,256]{3,1,2,0:T(8,128)(2,1)}, u32[]{:S(2)}) copy-start(bf16[1,64,6,256]{3,1,2,0:T(8,128)(2,1)} %param.15) | copy-start | bytes 589828
  213.3 9.0 %copy-start.1 = (bf16[144,4,1024]{2,0,1:T(8,128)(2,1)S(1)}, bf16[144,4,1024]{2,0,1:T(8,128)(2,1)}, u32[]{:S(2)}) copy-start(bf16[144,4,1024]{2,0,1:T(8,128)(2,1)} %select_bitcast_fusion) | copy-start | bytes 3538948
  213.3 9.0 %copy-start.10 = (bf16[128,1024]{1,0:T(8,128)(2,1)S(1)}, bf16[128,1024]{1,0:T(8,128)(2,1)}, u32[]{:S(2)}) copy-start(bf16[128,1024]{1,0:T(8,128)(2,1)} %copy-done.9) | copy-start | bytes 786436
  213.3 8.9 %all-to-all-start.6 = ((bf16[128,4,144]{0,2,1:T(8,128)(2,1)}), bf16[128,4,144]{0,2,1:T(8,128)(2,1)S(1)}, u32[]{:S(2)}, u32[]{:S(2)}) async-start(bf16[128,4,144]{0,2,1:T(8,128)(2,1)} %bitcast.29), calls=%async_computation.6 | async-start | bytes 294912 | tf_op jit(solution)/shard_map/all_to_all | solution.py:148
